TPU v7x, 512 devices: a whole 4x8x8 slice. The times are simulated.
512 devices in a mesh: prompt: 32 (over x, y), sample: 16 (over z, core).
Axes of the slice: x: 4, y: 8, z: 8, core: 2. Of those that a mesh axis runs over, the one named last changes fastest.
Arguments:
- queries: bfloat16 [32, 16, 4, 8192], P('prompt', 'sample'), may hold values from -24 to 24
- new_kv: bfloat16 [32, 16, 4, 2, 1024], P('prompt', 'sample'), may hold values from -24 to 24
- suffix_kv: bfloat16 [32, 16, 256, 2, 1024], P('prompt', 'sample'), may hold values from -24 to 24
- suffix_len: int32 [32, 16], P('prompt', 'sample'), may hold values from 1 to 256, as said below
- prefix_head: bfloat16 [32, 2048, 2, 1024], P('prompt', 'sample'), may hold values from -24 to 24
- prefix_tail: bfloat16 [32, 2048, 2, 1024], P('prompt', 'sample'), may hold values from -24 to 24
- prefix_len: int32 [32], replicated, may hold values from 1024 to 4096, as said below
Outputs:
- attended: bfloat16 [32, 16, 4, 8192], P('prompt', 'sample')
Inputs may be any that keep to these rules, and one draw needn't show every extreme that they name: `suffix_len`: some sample has all 256 slots live and some only one. `prefix_len`: some prompt has all 4096 positions live and some only 1024.
All inputs are finite; a program needn't handle non-finite values.
Results may differ from a plain program's by a relative error of at most 0.001.
Values may be sent and summed in bfloat16 or wider, within the bound.
No kernel may reach another device: no remote copies, remote signals or barrier semaphores. Data moves between devices by JAX's collectives and lax.ppermute only.
A program may use at most 64 MiB of HBM per device.

v0:
```python
import jax
import jax.numpy as jnp
from jax import lax
from jax.sharding import PartitionSpec as P

QH = 64
KVH = 8
HEAD_SIZE = 128


NEG = -1e30


def from_behind(value, axis, steps):
    count = lax.axis_size(axis)
    pairs = [(source, (source + steps) % count) for source in range(count)]
    return lax.ppermute(value, axis, pairs)


def apply_weights(logit_scores, valid_mask, value_matrix, form):
    masked = jnp.where(valid_mask, logit_scores, NEG)
    maxima = jnp.max(masked, axis=-1)
    weights = jnp.where(valid_mask, jnp.exp(masked - maxima[..., None]), 0.0)
    totals = jnp.sum(weights, axis=-1)
    numerator = jnp.einsum(form, weights, value_matrix, precision=lax.Precision.HIGHEST)
    leading = numerator.shape[:2]
    return (
        numerator.reshape(leading + (QH, HEAD_SIZE)),
        maxima.reshape(leading + (QH,)),
        totals.reshape(leading + (QH,)),
    )


def prefix_terms(query_rows, pairs, start, length):
    sample_count, step_count = (query_rows.shape[0], query_rows.shape[1])
    block_len = pairs.shape[0]
    grouped_queries = query_rows.reshape(sample_count, step_count, KVH, QH // KVH, HEAD_SIZE)
    key_matrix = pairs[:, 0].reshape(block_len, KVH, HEAD_SIZE)
    value_matrix = pairs[:, 1].reshape(block_len, KVH, HEAD_SIZE).astype(jnp.float32)
    logit_scores = jnp.einsum(
        "rhlxf,vlf->rhlxv", grouped_queries, key_matrix, preferred_element_type=jnp.float32
    ) * HEAD_SIZE ** (-0.5)
    valid_mask = start + jnp.arange(block_len, dtype=jnp.int32) < length
    return apply_weights(logit_scores, valid_mask, value_matrix, "urpyj,jpi->urpyi")


def suffix_terms(query_rows, cache, fresh, length):
    sample_count, step_count = (query_rows.shape[0], query_rows.shape[1])
    slots = cache.shape[1]
    joined = jnp.concatenate([cache, fresh], axis=1)
    total_len = joined.shape[1]
    grouped_queries = query_rows.reshape(sample_count, step_count, KVH, QH // KVH, HEAD_SIZE)
    key_matrix = joined[:, :, 0].reshape(sample_count, total_len, KVH, HEAD_SIZE)
    value_matrix = (
        joined[:, :, 1].reshape(sample_count, total_len, KVH, HEAD_SIZE).astype(jnp.float32)
    )
    logit_scores = jnp.einsum(
        "stkgd,slkd->stkgl", grouped_queries, key_matrix, preferred_element_type=jnp.float32
    ) * HEAD_SIZE ** (-0.5)
    cache_live = jnp.arange(slots, dtype=jnp.int32)[None, :] < length[:, None]
    steps_live = (
        jnp.arange(step_count, dtype=jnp.int32)[None, :]
        <= jnp.arange(step_count, dtype=jnp.int32)[:, None]
    )
    valid_mask = jnp.concatenate(
        [
            jnp.broadcast_to(cache_live[:, None, :], (sample_count, step_count, slots)),
            steps_live[None],
        ],
        axis=2,
    )
    return apply_weights(
        logit_scores, valid_mask[:, :, None, None, :], value_matrix, "stkgl,slkd->stkgd"
    )


def join(former, latter):
    maxima = jnp.maximum(former[1], latter[1])
    scale_a = jnp.exp(former[1] - maxima)
    scale_b = jnp.exp(latter[1] - maxima)
    return (
        former[0] * scale_a[..., None] + latter[0] * scale_b[..., None],
        maxima,
        former[2] * scale_a + latter[2] * scale_b,
    )


def settle(stacked):
    maxima = jnp.max(stacked[1], axis=0)
    factors = jnp.exp(stacked[1] - maxima[None])
    return (
        jnp.sum(stacked[0] * factors[..., None], axis=0),
        maxima,
        jnp.sum(stacked[2] * factors, axis=0),
    )


def spread(partial_sums):
    return (
        lax.all_to_all(partial_sums[0][None], "sample", split_axis=1, concat_axis=0, tiled=True),
        lax.all_to_all(partial_sums[1][None], "sample", split_axis=1, concat_axis=0, tiled=True),
        lax.all_to_all(partial_sums[2][None], "sample", split_axis=1, concat_axis=0, tiled=True),
    )


def per_device(queries, new_kv, suffix_kv, suffix_len, prefix_head, prefix_tail, prefix_len):
    sample_count = lax.axis_size("sample")
    prompt_row = lax.axis_index("prompt")
    sample_slot = lax.axis_index("sample")
    block_len = prefix_head.shape[1]
    half_len = block_len * sample_count
    own_length = prefix_len[prompt_row]
    local_rows = queries[0]
    every_rows = lax.all_gather(queries, "sample", axis=1, tiled=True)[0]
    near_part = suffix_terms(local_rows, suffix_kv[0], new_kv[0], suffix_len[0])
    moved = from_behind(prefix_tail, "prompt", -1)
    own_part = prefix_terms(every_rows, prefix_head[0], sample_slot * block_len, own_length)
    tail_part = prefix_terms(every_rows, moved[0], half_len + sample_slot * block_len, own_length)
    result = join(settle(spread(join(own_part, tail_part))), near_part)
    attended = (result[0] / result[2][..., None]).astype(jnp.bfloat16)
    return attended.reshape(queries.shape)


def solution(mesh):
    in_specs = (
        P("prompt", "sample", None, None),
        P("prompt", "sample", None, None, None),
        P("prompt", "sample", None, None, None),
        P("prompt", "sample"),
        P("prompt", "sample", None, None),
        P("prompt", "sample", None, None),
        P(),
    )
    out_specs = P("prompt", "sample", None, None)
    return jax.shard_map(
        per_device, mesh=mesh, in_specs=in_specs, out_specs=out_specs, check_vma=False
    )
```

profile of v0, /device:TPU:1, one launch (start us, length us, event | category | flops | bytes accessed | tf_op | source)
XLA Modules:
  0.0 154.0 jit_solution(10899200841303403284)
XLA Ops:
  6.5 0.7 all-gather.2.cloned.1.call-update
  7.3 1.4 copy.107
  8.6 8.1 %collective-permute-start = (bf16[1,128,2,1024]{1,3,2,0:T(8,128)(2,1)S(1)}, bf16[1,128,2,1024]{1,3,2,0:T(8,128)(2,1)S(1)}, u32[]{:S(2)}, u32[]{:S(2)}) collective-permute-start(bf16[1,128,2,1024]{1,3,2,0:T(8,128)(2,1)S(1)} %copy.107), channel_id=1, source_target_pairs={{0,496},{16,0},{32,16},{48,32},{64,48},{80,64},{96,80},{112,96},{1... | collective-permute-start | bytes 1572872 | tf_op jit(solution)/shard_map/ppermute | solution.py:17
  16.8 1.4 copy.98
  18.2 0.6 dynamic_slice.3
  18.8 0.7 add_compare_fusion.1
  19.4 0.7 add_compare_fusion
  20.1 7.2 %collective-permute-done = bf16[1,128,2,1024]{1,3,2,0:T(8,128)(2,1)S(1)} collective-permute-done((bf16[1,128,2,1024]{1,3,2,0:T(8,128)(2,1)S(1)}, bf16[1,128,2,1024]{1,3,2,0:T(8,128)(2,1)S(1)}, u32[]{:S(2)}, u32[]{:S(2)}) %collective-permute-start) | collective-permute-done | bytes 524320 | tf_op jit(solution)/shard_map/ppermute | solution.py:17
  27.4 30.0 %all-gather.2.cloned.1.call-done = bf16[1,16,4,8192]{3,2,0,1:T(4,128)(2,1)} async-done(((bf16[1,1,4,8192]{3,2,0,1:T(4,128)(2,1)}), bf16[1,16,4,8192]{3,2,0,1:T(4,128)(2,1)}) %all-gather.2.cloned.1.call-update) | async-done | bytes 1048592 | tf_op jit(solution)/shard_map/all_gather | solution.py:114
  57.4 2.1 %reshape.433 = bf16[16,4,8,8,128]{4,3,2,1,0:T(8,128)(2,1)S(1)} reshape(bf16[1,16,4,8192]{3,2,0,1:T(4,128)(2,1)} %all-gather.2.cloned.1.call-done) | data formatting | bytes 2097152 | tf_op jit(solution)/shard_map/reshape;squeeze | solution.py:37
  59.5 1.0 bitcast_reduce_fusion
  60.6 1.0 bitcast_reduce_fusion.1
  61.6 3.3 %fusion.47 = (f32[16,4,8,8]{0,3,1,2:T(8,128)S(1)}, f32[16,4,8,8,128]{4,0,3,1,2:T(8,128)}, f32[16,4,8,8]{0,3,1,2:T(8,128)S(1)}, f32[16,4,8,8,128]{4,0,3,1,2:T(8,128)}) fusion(f32[16,4,8,8]{0,3,1,2:T(8,128)S(1)} %get-tuple-element.26, f32[8,128,16,4,8]{1,2,4,3,0:T(8,128)S(1)} %get-tuple-element.27, pred[128]{0:T(512)(128)(4,1)S(1)} %add_compare_fusion.1, ...), kind=kLoop, calls=%fused_computation.79 | loop fusion | flops 5234688 | bytes 8454400 | tf_op jit(solution)/shard_map/reduce_sum | solution.py:24
  65.0 0.7 reshape.437
  65.7 4.5 %all-to-all-start.1 = ((f32[16,1,256]{2,1,0:T(1,128)}), f32[16,1,256]{2,1,0:T(1,128)S(1)}, u32[]{:S(2)}, u32[]{:S(2)}) async-start(f32[16,1,256]{2,1,0:T(1,128)} %reshape.437), calls=%async_computation.1 | async-start | bytes 32768 | tf_op jit(solution)/shard_map/all_to_all | solution.py:101
  70.4 3.4 %fusion.11 = f32[16,4,8,8,128]{4,3,1,0,2:T(8,128)S(1)} fusion(bf16[128,8,128,1,1]{0,2,4,3,1:T(8,128)(2,1)S(1)} %bitcast.166, f32[16,4,8,8,128]{4,0,3,1,2:T(8,128)} %get-tuple-element.11), kind=kOutput, calls=%fused_computation.20 | convolution fusion | flops 805306368 | bytes 4456448 | tf_op jit(solution)/shard_map/urpyj,jpi->urpyi/dot_general | solution.py:25
  73.8 3.1 %fusion.14 = f32[16,4,8,8,128]{4,3,1,0,2:T(8,128)} fusion(bf16[128,8,128,1,1]{0,2,4,3,1:T(8,128)(2,1)S(1)} %bitcast.167, f32[16,4,8,8,128]{4,0,3,1,2:T(8,128)S(1)} %copy-done), kind=kOutput, calls=%fused_computation.21 | convolution fusion | flops 805306368 | bytes 4456448 | tf_op jit(solution)/shard_map/urpyj,jpi->urpyi/dot_general | solution.py:25
  77.0 0.7 reshape.439
  77.7 7.2 %all-to-all-start.2 = ((f32[16,1,256]{2,1,0:T(1,128)}), f32[16,1,256]{2,1,0:T(1,128)S(1)}, u32[]{:S(2)}, u32[]{:S(2)}) async-start(f32[16,1,256]{2,1,0:T(1,128)} %reshape.439), calls=%async_computation.2 | async-start | bytes 32768 | tf_op jit(solution)/shard_map/all_to_all | solution.py:102
  84.9 3.4 %fusion.2 = f32[1,16,4,64,128]{4,3,2,0,1:T(8,128)} fusion(f32[16,4,8,8,128]{4,3,1,0,2:T(8,128)} %fusion.14, f32[16,4,8,8,128]{4,3,1,0,2:T(8,128)S(1)} %fusion.11, f32[16,4,64]{2,1,0:T(4,128)S(1)} %copy.119, f32[16,4,64]{2,1,0:T(4,128)S(1)} %copy.114), kind=kLoop, calls=%fused_computation.4 | loop fusion | flops 1572864 | bytes 6324224 | tf_op jit(solution)/shard_map/add | solution.py:82
  88.4 3.9 %all-to-all-done.2 = f32[16,1,256]{2,1,0:T(1,128)S(1)} async-done(((f32[16,1,256]{2,1,0:T(1,128)}), f32[16,1,256]{2,1,0:T(1,128)S(1)}, u32[]{:S(2)}, u32[]{:S(2)}) %all-to-all-start.2) | async-done | bytes 16416 | tf_op jit(solution)/shard_map/all_to_all | solution.py:102
  92.3 3.9 %all-to-all-start = ((f32[1,16,4,64,128]{4,3,2,0,1:T(8,128)}), f32[1,16,4,64,128]{4,3,2,0,1:T(8,128)S(1)}, u32[]{:S(2)}, u32[]{:S(2)}) async-start(f32[1,16,4,64,128]{4,3,2,0,1:T(8,128)} %fusion.2), calls=%async_computation | async-start | bytes 4194304 | tf_op jit(solution)/shard_map/all_to_all | solution.py:100
  96.8 12.8 %fusion.19 = (bf16[260,1024]{1,0:T(8,128)(2,1)S(1)}, bf16[260,1024]{1,0:T(8,128)(2,1)S(1)}) fusion(bf16[1,4,2,1024]{3,2,1,0:T(2,128)(2,1)S(1)} %bitcast.181, bf16[1,256,2,1024]{3,2,1,0:T(2,128)(2,1)} %bitcast.165), kind=kLoop, calls=%fused_computation.28 | loop fusion | flops 2129920 | bytes 2129920 | tf_op jit(solution)/shard_map/slice | solution.py:55
  109.8 0.4 fusion.53
  110.8 0.5 convolution_bitcast_fusion
  111.4 0.5 broadcast.97
  111.9 0.7 reduce.10
  112.6 0.7 reduce.11
  113.5 31.7 %all-to-all-done = f32[1,16,4,64,128]{4,3,2,0,1:T(8,128)S(1)} async-done(((f32[1,16,4,64,128]{4,3,2,0,1:T(8,128)}), f32[1,16,4,64,128]{4,3,2,0,1:T(8,128)S(1)}, u32[]{:S(2)}, u32[]{:S(2)}) %all-to-all-start) | async-done | bytes 2097184 | tf_op jit(solution)/shard_map/all_to_all | solution.py:100
  145.2 0.7 fusion
  146.2 0.2 fusion.34
  146.4 0.7 copy.133
  (45 shorter events, 1.8 us)
Async XLA Ops:
  6.5 11.6 %copy-start.3 = (s32[32]{0:T(128)S(1)}, s32[32]{0:T(128)}, u32[]{:S(2)}) copy-start(s32[32]{0:T(128)} %param.13) | copy-start | bytes 388
  6.5 50.8 %all-gather.2.cloned.1.call-start = ((), (), s32[]{:S(2)}) async-start(), calls=%async_computation.3 | async-start | bytes 1114112 | tf_op jit(solution)/shard_map/all_gather | solution.py:114
  8.6 18.7 %collective-permute-start = (bf16[1,128,2,1024]{1,3,2,0:T(8,128)(2,1)S(1)}, bf16[1,128,2,1024]{1,3,2,0:T(8,128)(2,1)S(1)}, u32[]{:S(2)}, u32[]{:S(2)}) collective-permute-start(bf16[1,128,2,1024]{1,3,2,0:T(8,128)(2,1)S(1)} %copy.107), channel_id=1, source_target_pairs={{0,496},{16,0},{32,16},{48,32},{64,48},{80,64},{96,80},{112,96},{1... | collective-permute-start | bytes 1572872 | tf_op jit(solution)/shard_map/ppermute | solution.py:17
  65.7 12.0 %all-to-all-start.1 = ((f32[16,1,256]{2,1,0:T(1,128)}), f32[16,1,256]{2,1,0:T(1,128)S(1)}, u32[]{:S(2)}, u32[]{:S(2)}) async-start(f32[16,1,256]{2,1,0:T(1,128)} %reshape.437), calls=%async_computation.1 | async-start | bytes 32768 | tf_op jit(solution)/shard_map/all_to_all | solution.py:101
  70.4 3.4 %copy-start = (f32[16,4,8,8,128]{4,0,3,1,2:T(8,128)S(1)}, f32[16,4,8,8,128]{4,0,3,1,2:T(8,128)}, u32[]{:S(2)}) copy-start(f32[16,4,8,8,128]{4,0,3,1,2:T(8,128)} %get-tuple-element.29) | copy-start | bytes 6291460
  77.7 14.6 %all-to-all-start.2 = ((f32[16,1,256]{2,1,0:T(1,128)}), f32[16,1,256]{2,1,0:T(1,128)S(1)}, u32[]{:S(2)}, u32[]{:S(2)}) async-start(f32[16,1,256]{2,1,0:T(1,128)} %reshape.439), calls=%async_computation.2 | async-start | bytes 32768 | tf_op jit(solution)/shard_map/all_to_all | solution.py:102
  88.4 8.4 %copy-start.2 = (bf16[1,1,4,2,1024]{4,3,2,1,0:T(2,128)(2,1)S(1)}, bf16[1,1,4,2,1024]{4,3,2,1,0:T(2,128)(2,1)}, u32[]{:S(2)}) copy-start(bf16[1,1,4,2,1024]{4,3,2,1,0:T(2,128)(2,1)} %param.8) | copy-start | bytes 49156
  92.3 52.9 %all-to-all-start = ((f32[1,16,4,64,128]{4,3,2,0,1:T(8,128)}), f32[1,16,4,64,128]{4,3,2,0,1:T(8,128)S(1)}, u32[]{:S(2)}, u32[]{:S(2)}) async-start(f32[1,16,4,64,128]{4,3,2,0,1:T(8,128)} %fusion.2), calls=%async_computation | async-start | bytes 4194304 | tf_op jit(solution)/shard_map/all_to_all | solution.py:100
  96.8 13.0 %copy-start.1 = (bf16[1,1,4,8192]{3,2,1,0:T(4,128)(2,1)S(1)}, bf16[1,1,4,8192]{3,2,1,0:T(4,128)(2,1)}, u32[]{:S(2)}) copy-start(bf16[1,1,4,8192]{3,2,1,0:T(4,128)(2,1)} %param.7) | copy-start | bytes 196612
Sparse Core Ops, SparseCore 0:
  9.5 47.8 all-gather.1
where the time goes:
time: 154 us
  waiting for transfers between devices  73.5 us (48%)
  starting transfers between devices  23.7 us (15%)
  other arithmetic  23.6 us (15%)
  between operations  14.4 us (9%)
  matrix products  9.42 us (6%)
  local copies, waits for them, and re-layouts  9.41 us (6%)
    all_to_all x1, waiting for transfers between devices, spread(): lax.all_to_all(partial_sums[0][None], 'sample', split_axis=1, concat_axis...  31.7 us
    all_gather x1, waiting for transfers between devices, per_device(): every_rows = lax.all_gather(queries, 'sample', axis=1, tiled=True)[0]  30 us
    slice x1, other arithmetic, suffix_terms(): joined[:, :, 1].reshape(sample_count, total_len, KVH, HEAD_SIZE)  12.8 us
    ppermute x1, starting transfers between devices, from_behind(): return lax.ppermute(value, axis, pairs)  8.12 us
    all_to_all x1, starting transfers between devices, spread(): lax.all_to_all(partial_sums[2][None], 'sample', split_axis=1, concat_axis...  7.22 us
    ppermute x1, waiting for transfers between devices, from_behind(): return lax.ppermute(value, axis, pairs)  7.22 us
    dot_general x3, matrix products, apply_weights(): jnp.einsum(form, weights, value_matrix, precision=lax.Precision.HIGHEST)  7.01 us
    unnamed x16, local copies, waits for them, and re-layouts  4.55 us
  transfers between devices with their start and end apart: 5, of which 4 were waited for; matrix products, arithmetic and copies ran while one was open for 21% of the time, Pallas kernels for 0%

commit v1 on v0

v1 whole, which is shorter than its diff:
```python
import jax
import jax.numpy as jnp
from jax import lax
from jax.sharding import PartitionSpec as P

QH = 64
KVH = 8
HEAD_SIZE = 128
GROUP = QH // KVH


NEG = -1e30


def shifted(value, axis, steps):
    count = lax.axis_size(axis)
    pairs = [(source, (source + steps) % count) for source in range(count)]
    return lax.ppermute(value, axis, pairs)


def split_dot(weights, value_matrix, form):
    rounded = lax.reduce_precision(weights, exponent_bits=8, mantissa_bits=7)
    high = rounded.astype(jnp.bfloat16)
    low = (weights - rounded).astype(jnp.bfloat16)
    return jnp.einsum(form, high, value_matrix, preferred_element_type=jnp.float32) + jnp.einsum(
        form, low, value_matrix, preferred_element_type=jnp.float32
    )


def softmax_terms(logit_scores, valid_mask, value_matrix, form):
    masked = jnp.where(valid_mask, logit_scores, NEG)
    maxima = jnp.max(masked, axis=-1)
    weights = jnp.where(valid_mask, jnp.exp(masked - maxima[..., None]), 0.0)
    totals = jnp.sum(weights, axis=-1)
    return split_dot(weights, value_matrix, form), maxima, totals


def suffix_terms(query_rows, cache, fresh, length):
    step_count = query_rows.shape[0]
    slots = cache.shape[0]
    grouped = query_rows.reshape(step_count, KVH, GROUP, HEAD_SIZE)
    cache_keys = cache[:, 0].reshape(slots, KVH, HEAD_SIZE)
    cache_values = cache[:, 1].reshape(slots, KVH, HEAD_SIZE)
    fresh_keys = fresh[:, 0].reshape(step_count, KVH, HEAD_SIZE)
    fresh_values = fresh[:, 1].reshape(step_count, KVH, HEAD_SIZE)
    scale = HEAD_SIZE ** (-0.5)
    cache_scores = jnp.einsum("tkgd,lkd->tkgl", grouped, cache_keys, preferred_element_type=jnp.float32) * scale
    fresh_scores = jnp.einsum("tkgd,ukd->tkgu", grouped, fresh_keys, preferred_element_type=jnp.float32) * scale
    cache_live = (jnp.arange(slots, dtype=jnp.int32) < length)[None, None, None, :]
    steps_live = (
        jnp.arange(step_count, dtype=jnp.int32)[None, :] <= jnp.arange(step_count, dtype=jnp.int32)[:, None]
    )[:, None, None, :]
    cache_masked = jnp.where(cache_live, cache_scores, NEG)
    fresh_masked = jnp.where(steps_live, fresh_scores, NEG)
    maxima = jnp.maximum(jnp.max(cache_masked, axis=-1), jnp.max(fresh_masked, axis=-1))
    cache_weights = jnp.where(cache_live, jnp.exp(cache_masked - maxima[..., None]), 0.0)
    fresh_weights = jnp.where(steps_live, jnp.exp(fresh_masked - maxima[..., None]), 0.0)
    totals = jnp.sum(cache_weights, axis=-1) + jnp.sum(fresh_weights, axis=-1)
    numerator = split_dot(cache_weights, cache_values, "tkgl,lkd->tkgd") + split_dot(
        fresh_weights, fresh_values, "tkgu,ukd->tkgd"
    )
    return (
        numerator.reshape(step_count, QH, HEAD_SIZE),
        maxima.reshape(step_count, QH),
        totals.reshape(step_count, QH),
    )


def per_device(queries, new_kv, suffix_kv, suffix_len, prefix_head, prefix_tail, prefix_len):
    sample_count = lax.axis_size("sample")
    prompt_count = lax.axis_size("prompt")
    prompt_row = lax.axis_index("prompt")
    sample_slot = lax.axis_index("sample")
    side = sample_slot % 2
    block_len = prefix_head.shape[1]
    half_len = block_len * sample_count
    step_count = queries.shape[2]

    def by_head(block):
        return block[0].reshape(block_len, 2, KVH, HEAD_SIZE).transpose(2, 1, 0, 3)

    outgoing_kv = jnp.stack([by_head(prefix_head), by_head(prefix_tail)], axis=1)
    outgoing_kv = outgoing_kv.reshape(2 * KVH, 2, block_len, HEAD_SIZE)
    gathered_kv = lax.all_to_all(outgoing_kv, "sample", 0, 0, tiled=True)
    keys = gathered_kv[:, 0].reshape(half_len, HEAD_SIZE)
    values = gathered_kv[:, 1].reshape(half_len, HEAD_SIZE)

    own_rows = queries[0, 0]
    previous_rows = shifted(own_rows, "prompt", 1)

    def query_groups(rows):
        return rows.reshape(step_count, KVH, GROUP, HEAD_SIZE).transpose(1, 0, 2, 3)

    outgoing_q = jnp.stack([query_groups(own_rows), query_groups(previous_rows)], axis=1)
    outgoing_q = outgoing_q.reshape(2 * KVH, step_count, GROUP, HEAD_SIZE)
    gathered_q = lax.all_to_all(outgoing_q, "sample", 0, 0, tiled=True)
    query_matrix = gathered_q.reshape(sample_count * step_count * GROUP, HEAD_SIZE)

    target_prompt = (prompt_row - side + prompt_count) % prompt_count
    length = prefix_len[target_prompt]
    positions = side * half_len + jnp.arange(half_len, dtype=jnp.int32)
    valid = (positions < length)[None, :]
    scores = jnp.einsum("rd,kd->rk", query_matrix, keys, preferred_element_type=jnp.float32) * HEAD_SIZE ** (-0.5)
    numerator, maxima, totals = softmax_terms(scores, valid, values, "rk,kd->rd")
    rows_per_sample = step_count * GROUP
    numerator = numerator.reshape(sample_count, rows_per_sample, HEAD_SIZE)
    stats = jnp.concatenate(
        [
            maxima.reshape(sample_count, rows_per_sample),
            totals.reshape(sample_count, rows_per_sample),
            jnp.zeros((sample_count, HEAD_SIZE - 2 * rows_per_sample), jnp.float32),
        ],
        axis=1,
    )
    outgoing_parts = jnp.concatenate([numerator, stats[:, None, :]], axis=1)
    returned = lax.all_to_all(outgoing_parts, "sample", 0, 0, tiled=True)
    returned = returned.reshape(KVH, 2, rows_per_sample + 1, HEAD_SIZE)
    head_parts = returned[:, 0]
    tail_parts = shifted(returned[:, 1], "prompt", -1)

    def unpack(parts):
        numer = parts[:, :rows_per_sample].reshape(KVH, step_count, GROUP, HEAD_SIZE)
        numer = numer.transpose(1, 0, 2, 3).reshape(step_count, QH, HEAD_SIZE)
        maxi = parts[:, rows_per_sample, :rows_per_sample].reshape(KVH, step_count, GROUP)
        maxi = maxi.transpose(1, 0, 2).reshape(step_count, QH)
        tot = parts[:, rows_per_sample, rows_per_sample : 2 * rows_per_sample].reshape(KVH, step_count, GROUP)
        tot = tot.transpose(1, 0, 2).reshape(step_count, QH)
        return numer, maxi, tot

    head_numer, head_max, head_tot = unpack(head_parts)
    tail_numer, tail_max, tail_tot = unpack(tail_parts)
    near_numer, near_max, near_tot = suffix_terms(own_rows, suffix_kv[0, 0], new_kv[0, 0], suffix_len[0, 0])

    top = jnp.maximum(jnp.maximum(head_max, tail_max), near_max)
    head_scale = jnp.exp(head_max - top)
    tail_scale = jnp.exp(tail_max - top)
    near_scale = jnp.exp(near_max - top)
    numer = (
        head_numer * head_scale[..., None] + tail_numer * tail_scale[..., None] + near_numer * near_scale[..., None]
    )
    total = head_tot * head_scale + tail_tot * tail_scale + near_tot * near_scale
    attended = (numer / total[..., None]).astype(jnp.bfloat16)
    return attended.reshape(queries.shape)


def solution(mesh):
    in_specs = (
        P("prompt", "sample", None, None),
        P("prompt", "sample", None, None, None),
        P("prompt", "sample", None, None, None),
        P("prompt", "sample"),
        P("prompt", "sample", None, None),
        P("prompt", "sample", None, None),
        P(),
    )
    out_specs = P("prompt", "sample", None, None)
    return jax.shard_map(
        per_device, mesh=mesh, in_specs=in_specs, out_specs=out_specs, check_vma=False
    )
```

time: 154 us -> 95.7 us (0.62)
  waiting for transfers between devices: 73.5 us -> 41.2 us
  other arithmetic: 23.6 us -> 6.19 us
  between operations: 14.4 us -> 1.05 us
  starting transfers between devices: 23.7 us -> 29.3 us
  matrix products: 9.42 us -> 7.02 us
    all_gather x1 -> x0, waiting for transfers between devices: 30 us -> none  [per_device(): every_rows = lax.all_gather(queries, 'sample', axis=1, tiled=True)[0]]
    slice x1 -> x0, other arithmetic: 12.8 us -> none  [suffix_terms(): joined[:, :, 1].reshape(sample_count, total_len, KVH, HEAD_SIZE)]
    ppermute x1 -> x2, waiting for transfers between devices: 7.22 us -> 2.93 us  [shifted(): return lax.ppermute(value, axis, pairs)]
    add x3 -> x2, other arithmetic: 3.51 us -> 0.02 us  [the longest x1 0.02 us: per_device(): head_tot * head_scale + tail_tot * tail_scale + near_tot * near_scale]
    all_to_all x3, starting transfers between devices: 15.6 us -> 18.8 us  [the longest x1 11.8 us: per_device(): gathered_kv = lax.all_to_all(outgoing_kv, 'sample', 0, 0, tiled=True)]
    all_to_all x3, waiting for transfers between devices: 35.6 us -> 38.3 us  [the longest x1 17.6 us: per_device(): gathered_kv = lax.all_to_all(outgoing_kv, 'sample', 0, 0, tiled=True)]
    dot_general x6 -> x9, matrix products: 9.42 us -> 7.02 us  [the longest x1 2.67 us: per_device(): jnp.einsum('rd,kd->rk', query_matrix, keys, preferred_element_type=jnp.fl...]
    ppermute x1 -> x2, starting transfers between devices: 8.12 us -> 10.5 us  [shifted(): return lax.ppermute(value, axis, pairs)]
  transfers between devices with their start and end apart: 5 -> 5, of which waited for: 4 -> 5; matrix products, arithmetic and copies ran while one was open for 21% -> 8% of each run, Pallas kernels for 0% -> 0%
where the time goes in v1:
time: 95.7 us; the launch traced here: 95.2 us
  waiting for transfers between devices  41.2 us (43%)
  starting transfers between devices  29.3 us (31%)
  local copies, waits for them, and re-layouts  10.4 us (11%)
  matrix products  7.02 us (7%)
  other arithmetic  6.19 us (6%)
  between operations  1.05 us (1%)
    all_to_all x1, waiting for transfers between devices, per_device(): gathered_kv = lax.all_to_all(outgoing_kv, 'sample', 0, 0, tiled=True)  17.6 us
    all_to_all x1, starting transfers between devices, per_device(): gathered_kv = lax.all_to_all(outgoing_kv, 'sample', 0, 0, tiled=True)  11.8 us
    all_to_all x1, waiting for transfers between devices, per_device(): returned = lax.all_to_all(outgoing_parts, 'sample', 0, 0, tiled=True)  11.6 us
    ppermute x2, starting transfers between devices, shifted(): return lax.ppermute(value, axis, pairs)  10.5 us
    all_to_all x1, waiting for transfers between devices, per_device(): gathered_q = lax.all_to_all(outgoing_q, 'sample', 0, 0, tiled=True)  9.08 us
    unnamed x15, local copies, waits for them, and re-layouts  5.27 us
    all_to_all x1, starting transfers between devices, per_device(): gathered_q = lax.all_to_all(outgoing_q, 'sample', 0, 0, tiled=True)  3.53 us
    all_to_all x1, starting transfers between devices, per_device(): returned = lax.all_to_all(outgoing_parts, 'sample', 0, 0, tiled=True)  3.44 us
  transfers between devices with their start and end apart: 5, of which 5 were waited for; matrix products, arithmetic and copies ran while one was open for 8% of the time, Pallas kernels for 0%

profile of v1, /device:TPU:1, one launch (start us, length us, event | category | flops | bytes accessed | tf_op | source)
XLA Modules:
  0.0 95.2 jit_solution(16688624162504879785)
XLA Ops:
  0.0 1.4 %copy.78 = bf16[1,128,2,1024]{1,3,2,0:T(8,128)(2,1)S(1)} copy(bf16[1,128,2,1024]{3,2,1,0:T(2,128)(2,1)} %param.11) | data formatting | bytes 1048576 | tf_op args[4]
  1.4 1.4 %copy.79 = bf16[1,128,2,1024]{1,3,2,0:T(8,128)(2,1)S(1)} copy(bf16[1,128,2,1024]{3,2,1,0:T(2,128)(2,1)} %param.12) | data formatting | bytes 1048576 | tf_op args[5]
  2.9 1.3 %copy.80 = bf16[8,2,2,128,128]{4,3,2,1,0:T(8,128)(2,1)} copy(bf16[8,2,2,128,128]{3,4,0,2,1:T(8,128)(2,1)S(1)} %pad_maximum_fusion) | data formatting | bytes 2097152 | tf_op jit(solution)/shard_map/stack | solution.py:82
  4.3 11.8 %all-to-all-start.1 = ((bf16[16,2,128,128]{3,2,1,0:T(8,128)(2,1)}), bf16[16,2,128,128]{3,2,1,0:T(8,128)(2,1)S(1)}, u32[]{:S(2)}, u32[]{:S(2)}) async-start(bf16[16,2,128,128]{3,2,1,0:T(8,128)(2,1)} %bitcast.14), calls=%async_computation.1 | async-start | bytes 2097152 | tf_op jit(solution)/shard_map/all_to_all | solution.py:84
  16.1 3.2 %collective-permute-start = (bf16[4,8192]{1,0:T(4,128)(2,1)S(1)}, bf16[4,8192]{1,0:T(4,128)(2,1)S(1)}, u32[]{:S(2)}, u32[]{:S(2)}) collective-permute-start(bf16[4,8192]{1,0:T(4,128)(2,1)S(1)} %bitcast.142), channel_id=1, source_target_pairs={{0,16},{16,32},{32,48},{48,64},{64,80},{80,96},{96,112},{112,128},... | collective-permute-start | bytes 196616 | tf_op jit(solution)/shard_map/ppermute | solution.py:18
  20.0 2.4 %copy.86 = bf16[1,1,256,2,1024]{2,4,3,1,0:T(8,128)(2,1)S(1)} copy(bf16[1,1,256,2,1024]{4,3,2,1,0:T(2,128)(2,1)} %param.9) | data formatting | bytes 2097152 | tf_op args[2]
  22.6 0.7 dynamic_slice.3
  23.3 0.4 fusion.44
  23.8 0.3 fusion.43
  24.1 0.2 fusion.13
  24.4 0.3 fusion.27
  24.6 0.3 convolution_add_fusion.1
  24.9 0.7 add_compare_fusion
  25.7 0.1 collective-permute-done
  25.8 0.7 copy.77
  26.5 17.6 %all-to-all-done.1 = bf16[16,2,128,128]{3,2,1,0:T(8,128)(2,1)S(1)} async-done(((bf16[16,2,128,128]{3,2,1,0:T(8,128)(2,1)}), bf16[16,2,128,128]{3,2,1,0:T(8,128)(2,1)S(1)}, u32[]{:S(2)}, u32[]{:S(2)}) %all-to-all-start.1) | async-done | bytes 1048608 | tf_op jit(solution)/shard_map/all_to_all | solution.py:84
  44.0 3.5 %all-to-all-start = ((bf16[16,4,8,128]{3,2,1,0:T(8,128)(2,1)}), bf16[16,4,8,128]{3,2,1,0:T(8,128)(2,1)S(1)}, u32[]{:S(2)}, u32[]{:S(2)}) async-start(bf16[16,4,8,128]{3,2,1,0:T(8,128)(2,1)} %bitcast.6), calls=%async_computation | async-start | bytes 262144 | tf_op jit(solution)/shard_map/all_to_all | solution.py:96
  47.6 9.1 %all-to-all-done = bf16[16,4,8,128]{3,2,1,0:T(8,128)(2,1)S(1)} async-done(((bf16[16,4,8,128]{3,2,1,0:T(8,128)(2,1)}), bf16[16,4,8,128]{3,2,1,0:T(8,128)(2,1)S(1)}, u32[]{:S(2)}, u32[]{:S(2)}) %all-to-all-start) | async-done | bytes 131104 | tf_op jit(solution)/shard_map/all_to_all | solution.py:96
  56.7 2.7 %fusion.1 = (f32[512]{0:T(512)S(1)}, f32[512,2048]{1,0:T(8,128)}) fusion(pred[2048]{0:T(1024)(128)(4,1)S(1)} %add_compare_fusion, bf16[512,128]{1,0:T(8,128)(2,1)S(1)} %bitcast.123, bf16[2048,128]{1,0:T(8,128)(2,1)S(1)} %bitcast.119), kind=kOutput, calls=%fused_computation.5 | convolution fusion | flops 271580672 | bytes 4853760 | tf_op jit(solution)/shard_map/rd,kd->rk/dot_general | solution.py:103
  59.5 3.4 %fusion.37 = f32[512]{0:T(512)S(1)} fusion(f32[512]{0:T(512)S(1)} %get-tuple-element.23, f32[512,2048]{1,0:T(8,128)} %get-tuple-element.24, pred[2048]{0:T(1024)(128)(4,1)S(1)} %add_compare_fusion), kind=kLoop, calls=%fused_computation.67 | loop fusion | flops 5242368 | bytes 4200448 | tf_op jit(solution)/shard_map/reduce_sum | solution.py:34
  62.9 1.4 %fusion.2 = f32[512,128]{1,0:T(8,128)S(1)} fusion(bf16[2048,128]{1,0:T(8,128)(2,1)S(1)} %bitcast.126, f32[512,2048]{1,0:T(8,128)S(1)} %copy-done, f32[512]{0:T(512)S(1)} %get-tuple-element.23, pred[2048]{0:T(1024)(128)(4,1)S(1)} %add_compare_fusion), kind=kOutput, calls=%fused_computation.6 | convolution fusion | flops 275775488 | bytes 4984832 | tf_op jit(solution)/shard_map/rk,kd->rd/dot_general | solution.py:25
  64.3 1.1 %fusion.5 = f32[512,128]{1,0:T(8,128)S(1)} fusion(f32[512,128]{1,0:T(8,128)S(1)} %fusion.2, bf16[2048,128]{1,0:T(8,128)(2,1)S(1)} %bitcast.127, f32[512,2048]{1,0:T(8,128)S(1)} %copy-done, f32[512]{0:T(512)S(1)} %get-tuple-element.23, pred[2048]{0:T(1024)(128)(4,1)S(1)} %add_compare_fusion), kind=kOutput, calls=%fused_computation.8 | convolution fusion | flops 274792448 | bytes 5246976 | tf_op jit(solution)/shard_map/rk,kd->rd/dot_general | solution.py:25
  65.5 0.7 pad_maximum_fusion.1
  66.3 3.4 %all-to-all-start.2 = ((f32[16,33,128]{2,1,0:T(8,128)}), f32[16,33,128]{2,1,0:T(8,128)S(1)}, u32[]{:S(2)}, u32[]{:S(2)}) async-start(f32[16,33,128]{2,1,0:T(8,128)} %pad_maximum_fusion.1), calls=%async_computation.2 | async-start | bytes 655360 | tf_op jit(solution)/shard_map/all_to_all | solution.py:116
  69.7 0.1 fusion.31
  70.0 0.3 fusion.15
  70.3 0.3 fusion.9
  70.8 11.6 %all-to-all-done.2 = f32[16,33,128]{2,1,0:T(8,128)S(1)} async-done(((f32[16,33,128]{2,1,0:T(8,128)}), f32[16,33,128]{2,1,0:T(8,128)S(1)}, u32[]{:S(2)}, u32[]{:S(2)}) %all-to-all-start.2) | async-done | bytes 270368 | tf_op jit(solution)/shard_map/all_to_all | solution.py:116
  82.4 0.2 fusion.40
  82.7 7.3 %collective-permute-start.1 = (f32[8,33,128]{2,0,1:T(8,128)S(1)}, f32[8,33,128]{2,0,1:T(8,128)S(1)}, u32[]{:S(2)}, u32[]{:S(2)}) collective-permute-start(f32[8,33,128]{2,0,1:T(8,128)S(1)} %bitcast.134), channel_id=1, source_target_pairs={{0,496},{16,0},{32,16},{48,32},{64,48},{80,64},{96,80},{112,96},{1... | collective-permute-start | bytes 405512 | tf_op jit(solution)/shard_map/ppermute | solution.py:18
  90.5 2.8 %collective-permute-done.1 = f32[8,33,128]{2,0,1:T(8,128)S(1)} collective-permute-done((f32[8,33,128]{2,0,1:T(8,128)S(1)}, f32[8,33,128]{2,0,1:T(8,128)S(1)}, u32[]{:S(2)}, u32[]{:S(2)}) %collective-permute-start.1) | collective-permute-done | bytes 135200 | tf_op jit(solution)/shard_map/ppermute | solution.py:18
  94.5 0.7 fusion.22
  (62 shorter events, 2.6 us)
Async XLA Ops:
  0.0 16.1 %copy-start.2 = (bf16[1,1,4,8192]{3,2,1,0:T(4,128)(2,1)S(1)}, bf16[1,1,4,8192]{3,2,1,0:T(4,128)(2,1)}, u32[]{:S(2)}) copy-start(bf16[1,1,4,8192]{3,2,1,0:T(4,128)(2,1)} %param.7) | copy-start | bytes 196612
  2.8 19.7 %copy-start.1 = (bf16[1,1,4,2,1024]{4,3,2,1,0:T(2,128)(2,1)S(1)}, bf16[1,1,4,2,1024]{4,3,2,1,0:T(2,128)(2,1)}, u32[]{:S(2)}) copy-start(bf16[1,1,4,2,1024]{4,3,2,1,0:T(2,128)(2,1)} %param.8) | copy-start | bytes 49156
  2.8 19.8 %copy-start.3 = (s32[32]{0:T(128)S(1)}, s32[32]{0:T(128)}, u32[]{:S(2)}) copy-start(s32[32]{0:T(128)} %param.13) | copy-start | bytes 388
  4.3 39.8 %all-to-all-start.1 = ((bf16[16,2,128,128]{3,2,1,0:T(8,128)(2,1)}), bf16[16,2,128,128]{3,2,1,0:T(8,128)(2,1)S(1)}, u32[]{:S(2)}, u32[]{:S(2)}) async-start(bf16[16,2,128,128]{3,2,1,0:T(8,128)(2,1)} %bitcast.14), calls=%async_computation.1 | async-start | bytes 2097152 | tf_op jit(solution)/shard_map/all_to_all | solution.py:84
  16.1 9.7 %collective-permute-start = (bf16[4,8192]{1,0:T(4,128)(2,1)S(1)}, bf16[4,8192]{1,0:T(4,128)(2,1)S(1)}, u32[]{:S(2)}, u32[]{:S(2)}) collective-permute-start(bf16[4,8192]{1,0:T(4,128)(2,1)S(1)} %bitcast.142), channel_id=1, source_target_pairs={{0,16},{16,32},{32,48},{48,64},{64,80},{80,96},{96,112},{112,128},... | collective-permute-start | bytes 196616 | tf_op jit(solution)/shard_map/ppermute | solution.py:18
  44.0 12.7 %all-to-all-start = ((bf16[16,4,8,128]{3,2,1,0:T(8,128)(2,1)}), bf16[16,4,8,128]{3,2,1,0:T(8,128)(2,1)S(1)}, u32[]{:S(2)}, u32[]{:S(2)}) async-start(bf16[16,4,8,128]{3,2,1,0:T(8,128)(2,1)} %bitcast.6), calls=%async_computation | async-start | bytes 262144 | tf_op jit(solution)/shard_map/all_to_all | solution.py:96
  59.5 3.5 %copy-start = (f32[512,2048]{1,0:T(8,128)S(1)}, f32[512,2048]{1,0:T(8,128)}, u32[]{:S(2)}) copy-start(f32[512,2048]{1,0:T(8,128)} %get-tuple-element.24) | copy-start | bytes 12582916
  66.3 16.1 %all-to-all-start.2 = ((f32[16,33,128]{2,1,0:T(8,128)}), f32[16,33,128]{2,1,0:T(8,128)S(1)}, u32[]{:S(2)}, u32[]{:S(2)}) async-start(f32[16,33,128]{2,1,0:T(8,128)} %pad_maximum_fusion.1), calls=%async_computation.2 | async-start | bytes 655360 | tf_op jit(solution)/shard_map/all_to_all | solution.py:116
  82.7 10.6 %collective-permute-start.1 = (f32[8,33,128]{2,0,1:T(8,128)S(1)}, f32[8,33,128]{2,0,1:T(8,128)S(1)}, u32[]{:S(2)}, u32[]{:S(2)}) collective-permute-start(f32[8,33,128]{2,0,1:T(8,128)S(1)} %bitcast.134), channel_id=1, source_target_pairs={{0,496},{16,0},{32,16},{48,32},{64,48},{80,64},{96,80},{112,96},{1... | collective-permute-start | bytes 405512 | tf_op jit(solution)/shard_map/ppermute | solution.py:18

commit v2 on v1

--- a/solution.py
+++ b/solution.py
@@ -68,7 +68,6 @@
 
 def per_device(queries, new_kv, suffix_kv, suffix_len, prefix_head, prefix_tail, prefix_len):
     sample_count = lax.axis_size("sample")
-    prompt_count = lax.axis_size("prompt")
     prompt_row = lax.axis_index("prompt")
     sample_slot = lax.axis_index("sample")
     side = sample_slot % 2
@@ -76,28 +75,27 @@
     half_len = block_len * sample_count
     step_count = queries.shape[2]
 
+    moved_tail = shifted(prefix_tail, "prompt", -1)
+    own_rows = queries[0, 0]
+
     def by_head(block):
-        return block[0].reshape(block_len, 2, KVH, HEAD_SIZE).transpose(2, 1, 0, 3)
+        return block[0].reshape(block_len, 2, KVH, HEAD_SIZE).transpose(2, 1, 0, 3).reshape(KVH, 2 * block_len, HEAD_SIZE)
 
-    outgoing_kv = jnp.stack([by_head(prefix_head), by_head(prefix_tail)], axis=1)
-    outgoing_kv = outgoing_kv.reshape(2 * KVH, 2, block_len, HEAD_SIZE)
-    gathered_kv = lax.all_to_all(outgoing_kv, "sample", 0, 0, tiled=True)
-    keys = gathered_kv[:, 0].reshape(half_len, HEAD_SIZE)
-    values = gathered_kv[:, 1].reshape(half_len, HEAD_SIZE)
+    query_groups = own_rows.reshape(step_count, KVH, GROUP, HEAD_SIZE).transpose(1, 0, 2, 3)
+    query_groups = query_groups.reshape(KVH, step_count * GROUP, HEAD_SIZE)
+    outgoing = jnp.stack(
+        [
+            jnp.concatenate([by_head(prefix_head), query_groups], axis=1),
+            jnp.concatenate([by_head(moved_tail), query_groups], axis=1),
+        ],
+        axis=1,
+    ).reshape(2 * KVH, 2 * block_len + step_count * GROUP, HEAD_SIZE)
+    gathered = lax.all_to_all(outgoing, "sample", 0, 0, tiled=True)
+    keys = gathered[:, :block_len].reshape(half_len, HEAD_SIZE)
+    values = gathered[:, block_len : 2 * block_len].reshape(half_len, HEAD_SIZE)
+    query_matrix = gathered[:, 2 * block_len :].reshape(sample_count * step_count * GROUP, HEAD_SIZE)
 
-    own_rows = queries[0, 0]
-    previous_rows = shifted(own_rows, "prompt", 1)
-
-    def query_groups(rows):
-        return rows.reshape(step_count, KVH, GROUP, HEAD_SIZE).transpose(1, 0, 2, 3)
-
-    outgoing_q = jnp.stack([query_groups(own_rows), query_groups(previous_rows)], axis=1)
-    outgoing_q = outgoing_q.reshape(2 * KVH, step_count, GROUP, HEAD_SIZE)
-    gathered_q = lax.all_to_all(outgoing_q, "sample", 0, 0, tiled=True)
-    query_matrix = gathered_q.reshape(sample_count * step_count * GROUP, HEAD_SIZE)
-
-    target_prompt = (prompt_row - side + prompt_count) % prompt_count
-    length = prefix_len[target_prompt]
+    length = prefix_len[prompt_row]
     positions = side * half_len + jnp.arange(half_len, dtype=jnp.int32)
     valid = (positions < length)[None, :]
     scores = jnp.einsum("rd,kd->rk", query_matrix, keys, preferred_element_type=jnp.float32) * HEAD_SIZE ** (-0.5)
@@ -116,7 +114,7 @@
     returned = lax.all_to_all(outgoing_parts, "sample", 0, 0, tiled=True)
     returned = returned.reshape(KVH, 2, rows_per_sample + 1, HEAD_SIZE)
     head_parts = returned[:, 0]
-    tail_parts = shifted(returned[:, 1], "prompt", -1)
+    tail_parts = returned[:, 1]
 
     def unpack(parts):
         numer = parts[:, :rows_per_sample].reshape(KVH, step_count, GROUP, HEAD_SIZE)

time: 95.7 us -> 93.7 us (0.979)
  starting transfers between devices: 29.3 us -> 23.7 us
  waiting for transfers between devices: 41.2 us -> 44.4 us
    ppermute x2 -> x1, waiting for transfers between devices: 2.93 us -> 8.02 us  [shifted(): return lax.ppermute(value, axis, pairs)]
    all_to_all x2 -> x1, starting transfers between devices: 15.4 us -> 11.9 us  [per_device(): gathered = lax.all_to_all(outgoing, 'sample', 0, 0, tiled=True)]
    ppermute x2 -> x1, starting transfers between devices: 10.5 us -> 8.12 us  [shifted(): return lax.ppermute(value, axis, pairs)]
    all_to_all x2 -> x1, waiting for transfers between devices: 26.6 us -> 24.4 us  [per_device(): gathered = lax.all_to_all(outgoing, 'sample', 0, 0, tiled=True)]
    another operation x2 -> x1, local copies, waits for them, and re-layouts: 2 us -> 1.09 us  [per_device(): jnp.stack([jnp.concatenate([by_head(prefix_head), query_groups], axis=1),...]
    unnamed x15 -> x12, local copies, waits for them, and re-layouts: 5.27 us -> 6.06 us
  transfers between devices with their start and end apart: 5 -> 3, of which waited for: 5 -> 3; matrix products, arithmetic and copies ran while one was open for 8% -> 10% of each run, Pallas kernels for 0% -> 0%
where the time goes in v2:
time: 93.7 us; the launch traced here: 93.3 us
  waiting for transfers between devices  44.4 us (47%)
  starting transfers between devices  23.7 us (25%)
  local copies, waits for them, and re-layouts  10.9 us (12%)
  matrix products  7.03 us (8%)
  other arithmetic  6.2 us (7%)
  between operations  1.01 us (1%)
    all_to_all x1, waiting for transfers between devices, per_device(): gathered = lax.all_to_all(outgoing, 'sample', 0, 0, tiled=True)  24.4 us
    all_to_all x1, waiting for transfers between devices, per_device(): returned = lax.all_to_all(outgoing_parts, 'sample', 0, 0, tiled=True)  12 us
    all_to_all x1, starting transfers between devices, per_device(): gathered = lax.all_to_all(outgoing, 'sample', 0, 0, tiled=True)  11.9 us
    ppermute x1, starting transfers between devices, shifted(): return lax.ppermute(value, axis, pairs)  8.12 us
    ppermute x1, waiting for transfers between devices, shifted(): return lax.ppermute(value, axis, pairs)  8.02 us
    unnamed x12, local copies, waits for them, and re-layouts  6.06 us
    all_to_all x1, starting transfers between devices, per_device(): returned = lax.all_to_all(outgoing_parts, 'sample', 0, 0, tiled=True)  3.7 us
    reduce_sum x1, other arithmetic, softmax_terms(): totals = jnp.sum(weights, axis=-1)  3.43 us
  transfers between devices with their start and end apart: 3, of which 3 were waited for; matrix products, arithmetic and copies ran while one was open for 10% of the time, Pallas kernels for 0%

profile of v2, /device:TPU:1, one launch (start us, length us, event | category | flops | bytes accessed | tf_op | source)
XLA Modules:
  0.0 93.3 jit_solution(1780186591003489954)
XLA Ops:
  0.0 1.4 %copy.85 = bf16[1,128,2,1024]{1,3,2,0:T(8,128)(2,1)S(1)} copy(bf16[1,128,2,1024]{3,2,1,0:T(2,128)(2,1)} %param.12) | data formatting | bytes 1048576 | tf_op args[5]
  1.4 8.1 %collective-permute-start = (bf16[1,128,2,1024]{1,3,2,0:T(8,128)(2,1)S(1)}, bf16[1,128,2,1024]{1,3,2,0:T(8,128)(2,1)S(1)}, u32[]{:S(2)}, u32[]{:S(2)}) collective-permute-start(bf16[1,128,2,1024]{1,3,2,0:T(8,128)(2,1)S(1)} %copy.85), channel_id=1, source_target_pairs={{0,496},{16,0},{32,16},{48,32},{64,48},{80,64},{96,80},{112,96},{1... | collective-permute-start | bytes 1572872 | tf_op jit(solution)/shard_map/ppermute | solution.py:18
  9.5 0.9 copy.157
  10.4 1.4 %copy.82 = bf16[1,128,2,1024]{1,3,2,0:T(8,128)(2,1)S(1)} copy(bf16[1,128,2,1024]{3,2,1,0:T(2,128)(2,1)} %param.11) | data formatting | bytes 1048576 | tf_op args[4]
  11.8 0.3 copy.83
  12.1 8.0 %collective-permute-done = bf16[1,128,2,1024]{1,3,2,0:T(8,128)(2,1)S(1)} collective-permute-done((bf16[1,128,2,1024]{1,3,2,0:T(8,128)(2,1)S(1)}, bf16[1,128,2,1024]{1,3,2,0:T(8,128)(2,1)S(1)}, u32[]{:S(2)}, u32[]{:S(2)}) %collective-permute-start) | collective-permute-done | bytes 524320 | tf_op jit(solution)/shard_map/ppermute | solution.py:18
  20.1 0.3 copy.86
  20.5 0.1 pad_maximum_fusion
  20.6 1.1 %copy.87 = bf16[8,2,288,128]{3,2,1,0:T(8,128)(2,1)} copy(bf16[8,2,288,128]{3,2,0,1:T(8,128)(2,1)S(1)} %pad_maximum_fusion) | data formatting | bytes 2359296 | tf_op jit(solution)/shard_map/stack | solution.py:86
  21.7 11.9 %all-to-all-start = ((bf16[16,288,128]{2,1,0:T(8,128)(2,1)}), bf16[16,288,128]{2,1,0:T(8,128)(2,1)S(1)}, u32[]{:S(2)}, u32[]{:S(2)}) async-start(bf16[16,288,128]{2,1,0:T(8,128)(2,1)} %bitcast.11), calls=%async_computation | async-start | bytes 2359296 | tf_op jit(solution)/shard_map/all_to_all | solution.py:93
  34.2 2.4 %copy.93 = bf16[1,1,256,2,1024]{2,4,3,1,0:T(8,128)(2,1)S(1)} copy(bf16[1,1,256,2,1024]{4,3,2,1,0:T(2,128)(2,1)} %param.9) | data formatting | bytes 2097152 | tf_op args[2]
  36.8 0.7 dynamic_slice.3
  37.5 0.4 fusion.46
  38.0 0.3 fusion.45
  38.3 0.6 add_compare_fusion
  39.0 0.2 fusion.15
  39.2 0.3 fusion.29
  39.5 0.3 convolution_add_fusion.1
  39.8 24.4 %all-to-all-done = bf16[16,288,128]{2,1,0:T(8,128)(2,1)S(1)} async-done(((bf16[16,288,128]{2,1,0:T(8,128)(2,1)}), bf16[16,288,128]{2,1,0:T(8,128)(2,1)S(1)}, u32[]{:S(2)}, u32[]{:S(2)}) %all-to-all-start) | async-done | bytes 1179680 | tf_op jit(solution)/shard_map/all_to_all | solution.py:93
  64.1 0.1 fusion.40
  64.3 2.7 %fusion.1 = (f32[512]{0:T(512)S(1)}, f32[512,2048]{1,0:T(8,128)}) fusion(pred[2048]{0:T(1024)(128)(4,1)S(1)} %add_compare_fusion, bf16[512,128]{1,0:T(8,128)(2,1)S(1)} %bitcast.117, bf16[2048,128]{1,0:T(8,128)(2,1)S(1)} %bitcast.111), kind=kOutput, calls=%fused_computation.5 | convolution fusion | flops 271580672 | bytes 4853760 | tf_op jit(solution)/shard_map/rd,kd->rk/dot_general | solution.py:101
  67.0 3.4 %fusion.39 = f32[512]{0:T(512)S(1)} fusion(f32[512]{0:T(512)S(1)} %get-tuple-element.25, f32[512,2048]{1,0:T(8,128)} %get-tuple-element.26, pred[2048]{0:T(1024)(128)(4,1)S(1)} %add_compare_fusion), kind=kLoop, calls=%fused_computation.70 | loop fusion | flops 5242368 | bytes 4200448 | tf_op jit(solution)/shard_map/reduce_sum | solution.py:34
  70.5 1.4 %fusion.2 = f32[512,128]{1,0:T(8,128)S(1)} fusion(bf16[2048,128]{1,0:T(8,128)(2,1)S(1)} %bitcast.121, f32[512,2048]{1,0:T(8,128)S(1)} %copy-done, f32[512]{0:T(512)S(1)} %get-tuple-element.25, pred[2048]{0:T(1024)(128)(4,1)S(1)} %add_compare_fusion), kind=kOutput, calls=%fused_computation.6 | convolution fusion | flops 275775488 | bytes 4984832 | tf_op jit(solution)/shard_map/rk,kd->rd/dot_general | solution.py:25
  71.9 1.1 %fusion.5 = f32[512,128]{1,0:T(8,128)S(1)} fusion(f32[512,128]{1,0:T(8,128)S(1)} %fusion.2, bf16[2048,128]{1,0:T(8,128)(2,1)S(1)} %bitcast.122, f32[512,2048]{1,0:T(8,128)S(1)} %copy-done, f32[512]{0:T(512)S(1)} %get-tuple-element.25, pred[2048]{0:T(1024)(128)(4,1)S(1)} %add_compare_fusion), kind=kOutput, calls=%fused_computation.9 | convolution fusion | flops 274792448 | bytes 5246976 | tf_op jit(solution)/shard_map/rk,kd->rd/dot_general | solution.py:25
  73.1 0.7 pad_maximum_fusion.3
  73.8 3.7 %all-to-all-start.1 = ((f32[16,33,128]{2,1,0:T(8,128)}), f32[16,33,128]{2,1,0:T(8,128)S(1)}, u32[]{:S(2)}, u32[]{:S(2)}) async-start(f32[16,33,128]{2,1,0:T(8,128)} %pad_maximum_fusion.3), calls=%async_computation.1 | async-start | bytes 655360 | tf_op jit(solution)/shard_map/all_to_all | solution.py:114
  77.5 0.1 fusion.33
  77.9 0.3 fusion.17
  78.2 0.3 fusion.9
  78.6 12.0 %all-to-all-done.1 = f32[16,33,128]{2,1,0:T(8,128)S(1)} async-done(((f32[16,33,128]{2,1,0:T(8,128)}), f32[16,33,128]{2,1,0:T(8,128)S(1)}, u32[]{:S(2)}, u32[]{:S(2)}) %all-to-all-start.1) | async-done | bytes 270368 | tf_op jit(solution)/shard_map/all_to_all | solution.py:114
  90.7 0.2 fusion.42
  92.6 0.7 fusion.24
  (58 shorter events, 2.5 us)
Async XLA Ops:
  1.4 18.7 %collective-permute-start = (bf16[1,128,2,1024]{1,3,2,0:T(8,128)(2,1)S(1)}, bf16[1,128,2,1024]{1,3,2,0:T(8,128)(2,1)S(1)}, u32[]{:S(2)}, u32[]{:S(2)}) collective-permute-start(bf16[1,128,2,1024]{1,3,2,0:T(8,128)(2,1)S(1)} %copy.85), channel_id=1, source_target_pairs={{0,496},{16,0},{32,16},{48,32},{64,48},{80,64},{96,80},{112,96},{1... | collective-permute-start | bytes 1572872 | tf_op jit(solution)/shard_map/ppermute | solution.py:18
  20.5 16.2 %copy-start.1 = (bf16[1,1,4,2,1024]{4,3,2,1,0:T(2,128)(2,1)S(1)}, bf16[1,1,4,2,1024]{4,3,2,1,0:T(2,128)(2,1)}, u32[]{:S(2)}) copy-start(bf16[1,1,4,2,1024]{4,3,2,1,0:T(2,128)(2,1)} %param.8) | copy-start | bytes 49156
  20.5 16.3 %copy-start.2 = (s32[32]{0:T(128)S(1)}, s32[32]{0:T(128)}, u32[]{:S(2)}) copy-start(s32[32]{0:T(128)} %param.13) | copy-start | bytes 388
  21.7 42.4 %all-to-all-start = ((bf16[16,288,128]{2,1,0:T(8,128)(2,1)}), bf16[16,288,128]{2,1,0:T(8,128)(2,1)S(1)}, u32[]{:S(2)}, u32[]{:S(2)}) async-start(bf16[16,288,128]{2,1,0:T(8,128)(2,1)} %bitcast.11), calls=%async_computation | async-start | bytes 2359296 | tf_op jit(solution)/shard_map/all_to_all | solution.py:93
  67.0 3.5 %copy-start = (f32[512,2048]{1,0:T(8,128)S(1)}, f32[512,2048]{1,0:T(8,128)}, u32[]{:S(2)}) copy-start(f32[512,2048]{1,0:T(8,128)} %get-tuple-element.26) | copy-start | bytes 12582916
  73.8 16.8 %all-to-all-start.1 = ((f32[16,33,128]{2,1,0:T(8,128)}), f32[16,33,128]{2,1,0:T(8,128)S(1)}, u32[]{:S(2)}, u32[]{:S(2)}) async-start(f32[16,33,128]{2,1,0:T(8,128)} %pad_maximum_fusion.3), calls=%async_computation.1 | async-start | bytes 655360 | tf_op jit(solution)/shard_map/all_to_all | solution.py:114

commit v3 on v2

--- a/solution.py
+++ b/solution.py
@@ -67,40 +67,43 @@
 
 
 def per_device(queries, new_kv, suffix_kv, suffix_len, prefix_head, prefix_tail, prefix_len):
-    sample_count = lax.axis_size("sample")
+    team_count = lax.axis_size(("zl", "core"))
     prompt_row = lax.axis_index("prompt")
-    sample_slot = lax.axis_index("sample")
-    side = sample_slot % 2
+    team = lax.axis_index("zg")
     block_len = prefix_head.shape[1]
-    half_len = block_len * sample_count
     step_count = queries.shape[2]
+    rows_per_sample = step_count * GROUP
 
     moved_tail = shifted(prefix_tail, "prompt", -1)
     own_rows = queries[0, 0]
+    partner_rows = shifted(own_rows, "zg", 1)
 
-    def by_head(block):
-        return block[0].reshape(block_len, 2, KVH, HEAD_SIZE).transpose(2, 1, 0, 3).reshape(KVH, 2 * block_len, HEAD_SIZE)
+    halves = jnp.stack(
+        [prefix_head[0].reshape(block_len, 2, KVH, HEAD_SIZE), moved_tail[0].reshape(block_len, 2, KVH, HEAD_SIZE)]
+    )
+    kv_part = halves.transpose(3, 2, 0, 1, 4).reshape(KVH, 2 * 2 * block_len, HEAD_SIZE)
 
-    query_groups = own_rows.reshape(step_count, KVH, GROUP, HEAD_SIZE).transpose(1, 0, 2, 3)
-    query_groups = query_groups.reshape(KVH, step_count * GROUP, HEAD_SIZE)
-    outgoing = jnp.stack(
-        [
-            jnp.concatenate([by_head(prefix_head), query_groups], axis=1),
-            jnp.concatenate([by_head(moved_tail), query_groups], axis=1),
-        ],
-        axis=1,
-    ).reshape(2 * KVH, 2 * block_len + step_count * GROUP, HEAD_SIZE)
-    gathered = lax.all_to_all(outgoing, "sample", 0, 0, tiled=True)
-    keys = gathered[:, :block_len].reshape(half_len, HEAD_SIZE)
-    values = gathered[:, block_len : 2 * block_len].reshape(half_len, HEAD_SIZE)
-    query_matrix = gathered[:, 2 * block_len :].reshape(sample_count * step_count * GROUP, HEAD_SIZE)
+    def query_groups(rows):
+        return rows.reshape(step_count, KVH, GROUP, HEAD_SIZE).transpose(1, 0, 2, 3).reshape(KVH, rows_per_sample, HEAD_SIZE)
 
-    length = prefix_len[prompt_row]
-    positions = side * half_len + jnp.arange(half_len, dtype=jnp.int32)
-    valid = (positions < length)[None, :]
+    outgoing = jnp.concatenate([kv_part, query_groups(own_rows), query_groups(partner_rows)], axis=1)
+    gathered = lax.all_to_all(outgoing, ("zl", "core"), 0, 0, tiled=True)
+    span = 2 * block_len
+    keys = gathered[:, :span].reshape(team_count * span, HEAD_SIZE)
+    values = gathered[:, span : 2 * span].reshape(team_count * span, HEAD_SIZE)
+    query_parts = gathered[:, 2 * span :].reshape(team_count, 2, rows_per_sample, HEAD_SIZE).transpose(1, 0, 2, 3)
+    query_parts = jnp.where(team == 0, query_parts, query_parts[::-1])
+    query_matrix = query_parts.reshape(2 * team_count * rows_per_sample, HEAD_SIZE)
+
+    member = jnp.arange(team_count, dtype=jnp.int32)[:, None, None]
+    half = jnp.arange(2, dtype=jnp.int32)[None, :, None]
+    offset = jnp.arange(block_len, dtype=jnp.int32)[None, None, :]
+    prefix_half_len = block_len * team_count * 2
+    positions = half * prefix_half_len + (team * team_count + member) * block_len + offset
+    valid = (positions.reshape(-1) < prefix_len[prompt_row])[None, :]
     scores = jnp.einsum("rd,kd->rk", query_matrix, keys, preferred_element_type=jnp.float32) * HEAD_SIZE ** (-0.5)
     numerator, maxima, totals = softmax_terms(scores, valid, values, "rk,kd->rd")
-    rows_per_sample = step_count * GROUP
+    sample_count = 2 * team_count
     numerator = numerator.reshape(sample_count, rows_per_sample, HEAD_SIZE)
     stats = jnp.concatenate(
         [
@@ -111,10 +114,8 @@
         axis=1,
     )
     outgoing_parts = jnp.concatenate([numerator, stats[:, None, :]], axis=1)
-    returned = lax.all_to_all(outgoing_parts, "sample", 0, 0, tiled=True)
-    returned = returned.reshape(KVH, 2, rows_per_sample + 1, HEAD_SIZE)
-    head_parts = returned[:, 0]
-    tail_parts = returned[:, 1]
+    returned = lax.all_to_all(outgoing_parts, ("zg", "zl", "core"), 0, 0, tiled=True)
+    returned = returned.reshape(2, KVH, rows_per_sample + 1, HEAD_SIZE)
 
     def unpack(parts):
         numer = parts[:, :rows_per_sample].reshape(KVH, step_count, GROUP, HEAD_SIZE)
@@ -125,33 +126,41 @@
         tot = tot.transpose(1, 0, 2).reshape(step_count, QH)
         return numer, maxi, tot
 
-    head_numer, head_max, head_tot = unpack(head_parts)
-    tail_numer, tail_max, tail_tot = unpack(tail_parts)
+    first_numer, first_max, first_tot = unpack(returned[0])
+    second_numer, second_max, second_tot = unpack(returned[1])
     near_numer, near_max, near_tot = suffix_terms(own_rows, suffix_kv[0, 0], new_kv[0, 0], suffix_len[0, 0])
 
-    top = jnp.maximum(jnp.maximum(head_max, tail_max), near_max)
-    head_scale = jnp.exp(head_max - top)
-    tail_scale = jnp.exp(tail_max - top)
+    top = jnp.maximum(jnp.maximum(first_max, second_max), near_max)
+    first_scale = jnp.exp(first_max - top)
+    second_scale = jnp.exp(second_max - top)
     near_scale = jnp.exp(near_max - top)
     numer = (
-        head_numer * head_scale[..., None] + tail_numer * tail_scale[..., None] + near_numer * near_scale[..., None]
+        first_numer * first_scale[..., None]
+        + second_numer * second_scale[..., None]
+        + near_numer * near_scale[..., None]
     )
-    total = head_tot * head_scale + tail_tot * tail_scale + near_tot * near_scale
+    total = first_tot * first_scale + second_tot * second_scale + near_tot * near_scale
     attended = (numer / total[..., None]).astype(jnp.bfloat16)
     return attended.reshape(queries.shape)
 
 
 def solution(mesh):
+    prompts, samples = mesh.devices.shape
+    teams = 2
+    team_mesh = jax.sharding.Mesh(
+        mesh.devices.reshape(prompts, teams, samples // (2 * teams), 2), ("prompt", "zg", "zl", "core")
+    )
+    spread = ("zg", "zl", "core")
     in_specs = (
-        P("prompt", "sample", None, None),
-        P("prompt", "sample", None, None, None),
-        P("prompt", "sample", None, None, None),
-        P("prompt", "sample"),
-        P("prompt", "sample", None, None),
-        P("prompt", "sample", None, None),
+        P("prompt", spread, None, None),
+        P("prompt", spread, None, None, None),
+        P("prompt", spread, None, None, None),
+        P("prompt", spread),
+        P("prompt", spread, None, None),
+        P("prompt", spread, None, None),
         P(),
     )
-    out_specs = P("prompt", "sample", None, None)
+    out_specs = P("prompt", spread, None, None)
     return jax.shard_map(
-        per_device, mesh=mesh, in_specs=in_specs, out_specs=out_specs, check_vma=False
+        per_device, mesh=team_mesh, in_specs=in_specs, out_specs=out_specs, check_vma=False
     )

time: 93.7 us -> 93.3 us (level)
  waiting for transfers between devices: 44.4 us -> 34.9 us
  starting transfers between devices: 23.7 us -> 32.4 us
  other arithmetic: 6.2 us -> 7.39 us
    ppermute x1 -> x2, starting transfers between devices: 8.12 us -> 18.8 us  [shifted(): return lax.ppermute(value, axis, pairs)]
    ppermute x1 -> x2, waiting for transfers between devices: 8.02 us -> 0.01 us  [shifted(): return lax.ppermute(value, axis, pairs)]
    all_to_all x2, starting transfers between devices: 15.6 us -> 13.6 us  [the longest x1 7.84 us: per_device(): lax.all_to_all(outgoing_parts, ('zg', 'zl', 'core'), 0, 0, tiled=True)]
    all_to_all x2, waiting for transfers between devices: 36.4 us -> 34.8 us  [the longest x1 22.8 us: per_device(): gathered = lax.all_to_all(outgoing, ('zl', 'core'), 0, 0, tiled=True)]
    another operation x1 -> x0, local copies, waits for them, and re-layouts: 1.09 us -> none  [per_device(): jnp.stack([jnp.concatenate([by_head(prefix_head), query_groups], axis=1),...]
    concatenate x0 -> x1, other arithmetic: none -> 1.09 us  [per_device(): jnp.concatenate([kv_part, query_groups(own_rows), query_groups(partner_ro...]
    unnamed x12 -> x10, local copies, waits for them, and re-layouts: 6.06 us -> 6.06 us
  transfers between devices with their start and end apart: 3 -> 4, of which waited for: 3 -> 2; matrix products, arithmetic and copies ran while one was open for 10% -> 10% of each run, Pallas kernels for 0% -> 0%
where the time goes in v3:
time: 93.3 us; the launch traced here: 92.9 us
  waiting for transfers between devices  34.9 us (37%)
  starting transfers between devices  32.4 us (35%)
  local copies, waits for them, and re-layouts  10.2 us (11%)
  other arithmetic  7.39 us (8%)
  matrix products  7.02 us (8%)
  between operations  1.02 us (1%)
    all_to_all x1, waiting for transfers between devices, per_device(): gathered = lax.all_to_all(outgoing, ('zl', 'core'), 0, 0, tiled=True)  22.8 us
    ppermute x2, starting transfers between devices, shifted(): return lax.ppermute(value, axis, pairs)  18.8 us
    all_to_all x1, waiting for transfers between devices, per_device(): lax.all_to_all(outgoing_parts, ('zg', 'zl', 'core'), 0, 0, tiled=True)  12 us
    all_to_all x1, starting transfers between devices, per_device(): lax.all_to_all(outgoing_parts, ('zg', 'zl', 'core'), 0, 0, tiled=True)  7.84 us
    unnamed x10, local copies, waits for them, and re-layouts  6.06 us
    all_to_all x1, starting transfers between devices, per_device(): gathered = lax.all_to_all(outgoing, ('zl', 'core'), 0, 0, tiled=True)  5.8 us
    reduce_sum x1, other arithmetic, softmax_terms(): totals = jnp.sum(weights, axis=-1)  3.43 us
    dot_general x1, matrix products, per_device(): jnp.einsum('rd,kd->rk', query_matrix, keys, preferred_element_type=jnp.fl...  2.68 us
  transfers between devices with their start and end apart: 4, of which 2 were waited for; matrix products, arithmetic and copies ran while one was open for 10% of the time, Pallas kernels for 0%

profile of v3, /device:TPU:1, one launch (start us, length us, event | category | flops | bytes accessed | tf_op | source)
XLA Modules:
  0.0 92.9 jit_solution(6722284502227572738)
XLA Ops:
  0.0 1.4 %copy.73 = bf16[1,128,2,1024]{1,3,2,0:T(8,128)(2,1)S(1)} copy(bf16[1,128,2,1024]{3,2,1,0:T(2,128)(2,1)} %param.12) | data formatting | bytes 1048576 | tf_op args[5]
  1.4 8.1 %collective-permute-start = (bf16[1,128,2,1024]{1,3,2,0:T(8,128)(2,1)S(1)}, bf16[1,128,2,1024]{1,3,2,0:T(8,128)(2,1)S(1)}, u32[]{:S(2)}, u32[]{:S(2)}) collective-permute-start(bf16[1,128,2,1024]{1,3,2,0:T(8,128)(2,1)S(1)} %copy.73), channel_id=1, source_target_pairs={{0,496},{16,0},{32,16},{48,32},{64,48},{80,64},{96,80},{112,96},{1... | collective-permute-start | bytes 1572872 | tf_op jit(solution)/shard_map/ppermute | solution.py:18
  9.5 10.6 %collective-permute-start.1 = (bf16[4,8192]{1,0:T(4,128)(2,1)}, bf16[4,8192]{1,0:T(4,128)(2,1)S(1)}, u32[]{:S(2)}, u32[]{:S(2)}) collective-permute-start(bf16[4,8192]{1,0:T(4,128)(2,1)} %bitcast.128), channel_id=1, source_target_pairs={{0,8},{8,0},{1,9},{9,1},{2,10},{10,2},{3,11},{11,3},{4,12},{12,4},... | collective-permute-start | bytes 196616 | tf_op jit(solution)/shard_map/ppermute | solution.py:18
  20.2 0.9 copy.149
  21.0 1.4 %copy.72 = bf16[1,128,2,1024]{1,3,2,0:T(8,128)(2,1)S(1)} copy(bf16[1,128,2,1024]{3,2,1,0:T(2,128)(2,1)} %param.11) | data formatting | bytes 1048576 | tf_op args[4]
  22.4 1.2 %dynamic_slice.3 = s32[1]{0:T(128)} dynamic-slice(s32[32]{0:T(128)} %param.13, s32[]{:T(128)S(6)} %select_n.35), dynamic_slice_sizes={1} | dynamic-slice | bytes 12 | tf_op jit(solution)/shard_map/dynamic_slice | solution.py:103
  23.7 0.1 maximum_bitcast_fusion
  23.8 0.7 copy.74
  24.5 1.1 %pad_maximum_fusion = bf16[8,576,128]{2,1,0:T(8,128)(2,1)} fusion(bf16[8,32,128]{2,1,0:T(8,128)(2,1)S(1)} %get-tuple-element.29, bf16[8,32,128]{2,1,0:T(8,128)(2,1)S(1)} %get-tuple-element.30, bf16[8,512,128]{2,1,0:T(8,128)(2,1)S(1)} %bitcast.106), kind=kLoop, calls=%fused_computation.8 | loop fusion | flops 3538944 | bytes 2359296 | tf_op jit(solution)/shard_map/concatenate | solution.py:89
  25.6 5.8 %all-to-all-start = ((bf16[8,576,128]{2,1,0:T(8,128)(2,1)}), bf16[8,576,128]{2,1,0:T(8,128)(2,1)S(1)}, u32[]{:S(2)}, u32[]{:S(2)}) async-start(bf16[8,576,128]{2,1,0:T(8,128)(2,1)} %pad_maximum_fusion), calls=%async_computation | async-start | bytes 2359296 | tf_op jit(solution)/shard_map/all_to_all | solution.py:90
  31.5 0.7 add_compare_fusion
  32.9 2.4 %copy.81 = bf16[1,1,256,2,1024]{2,4,3,1,0:T(8,128)(2,1)S(1)} copy(bf16[1,1,256,2,1024]{4,3,2,1,0:T(2,128)(2,1)} %param.9) | data formatting | bytes 2097152 | tf_op args[2]
  35.5 0.4 fusion.41
  36.0 0.3 fusion.40
  36.3 0.2 fusion.13
  36.5 0.3 fusion.27
  36.8 0.3 convolution_add_fusion.1
  37.1 22.8 %all-to-all-done = bf16[8,576,128]{2,1,0:T(8,128)(2,1)S(1)} async-done(((bf16[8,576,128]{2,1,0:T(8,128)(2,1)}), bf16[8,576,128]{2,1,0:T(8,128)(2,1)S(1)}, u32[]{:S(2)}, u32[]{:S(2)}) %all-to-all-start) | async-done | bytes 1179680 | tf_op jit(solution)/shard_map/all_to_all | solution.py:90
  60.1 2.7 %fusion.1 = (f32[512]{0:T(512)S(1)}, f32[512,2048]{1,0:T(8,128)}) fusion(pred[2048]{0:T(1024)(128)(4,1)S(1)} %lt.29, bf16[512,128]{1,0:T(8,128)(2,1)S(1)} %bitcast.109, bf16[2048,128]{1,0:T(8,128)(2,1)S(1)} %bitcast.108), kind=kOutput, calls=%fused_computation.5 | convolution fusion | flops 271580672 | bytes 4853760 | tf_op jit(solution)/shard_map/rd,kd->rk/dot_general | solution.py:104
  62.8 3.4 %fusion.37 = f32[512]{0:T(512)S(1)} fusion(f32[512]{0:T(512)S(1)} %get-tuple-element.27, f32[512,2048]{1,0:T(8,128)} %get-tuple-element.28, pred[2048]{0:T(1024)(128)(4,1)S(1)} %lt.29), kind=kLoop, calls=%fused_computation.81 | loop fusion | flops 5242368 | bytes 4200448 | tf_op jit(solution)/shard_map/reduce_sum | solution.py:34
  66.3 1.4 %fusion.2 = f32[512,128]{1,0:T(8,128)S(1)} fusion(bf16[2048,128]{1,0:T(8,128)(2,1)S(1)} %bitcast.114, f32[512,2048]{1,0:T(8,128)S(1)} %copy-done, f32[512]{0:T(512)S(1)} %get-tuple-element.27, pred[2048]{0:T(1024)(128)(4,1)S(1)} %lt.29), kind=kOutput, calls=%fused_computation.6 | convolution fusion | flops 275775488 | bytes 4984832 | tf_op jit(solution)/shard_map/rk,kd->rd/dot_general | solution.py:25
  67.6 1.1 %fusion.5 = f32[512,128]{1,0:T(8,128)S(1)} fusion(f32[512,128]{1,0:T(8,128)S(1)} %fusion.2, bf16[2048,128]{1,0:T(8,128)(2,1)S(1)} %bitcast.115, f32[512,2048]{1,0:T(8,128)S(1)} %copy-done, f32[512]{0:T(512)S(1)} %get-tuple-element.27, pred[2048]{0:T(1024)(128)(4,1)S(1)} %lt.29), kind=kOutput, calls=%fused_computation.9 | convolution fusion | flops 274792448 | bytes 5246976 | tf_op jit(solution)/shard_map/rk,kd->rd/dot_general | solution.py:25
  68.9 0.7 pad_maximum_fusion.1
  69.6 7.8 %all-to-all-start.1 = ((f32[16,33,128]{2,1,0:T(8,128)}), f32[16,33,128]{2,1,0:T(8,128)S(1)}, u32[]{:S(2)}, u32[]{:S(2)}) async-start(f32[16,33,128]{2,1,0:T(8,128)} %pad_maximum_fusion.1), calls=%async_computation.1 | async-start | bytes 655360 | tf_op jit(solution)/shard_map/all_to_all | solution.py:117
  77.5 0.1 fusion.31
  77.8 0.3 fusion.15
  78.1 0.3 fusion.9
  78.5 12.0 %all-to-all-done.1 = f32[16,33,128]{2,1,0:T(8,128)S(1)} async-done(((f32[16,33,128]{2,1,0:T(8,128)}), f32[16,33,128]{2,1,0:T(8,128)S(1)}, u32[]{:S(2)}, u32[]{:S(2)}) %all-to-all-start.1) | async-done | bytes 270368 | tf_op jit(solution)/shard_map/all_to_all | solution.py:117
  90.7 0.1 slice_reduce_fusion.3
  91.5 0.1 div.17
  91.7 0.1 mul.123
  92.1 0.7 fusion.22
  (58 shorter events, 2.2 us)
Async XLA Ops:
  1.4 22.3 %collective-permute-start = (bf16[1,128,2,1024]{1,3,2,0:T(8,128)(2,1)S(1)}, bf16[1,128,2,1024]{1,3,2,0:T(8,128)(2,1)S(1)}, u32[]{:S(2)}, u32[]{:S(2)}) collective-permute-start(bf16[1,128,2,1024]{1,3,2,0:T(8,128)(2,1)S(1)} %copy.73), channel_id=1, source_target_pairs={{0,496},{16,0},{32,16},{48,32},{64,48},{80,64},{96,80},{112,96},{1... | collective-permute-start | bytes 1572872 | tf_op jit(solution)/shard_map/ppermute | solution.py:18
  9.5 14.2 %collective-permute-start.1 = (bf16[4,8192]{1,0:T(4,128)(2,1)}, bf16[4,8192]{1,0:T(4,128)(2,1)S(1)}, u32[]{:S(2)}, u32[]{:S(2)}) collective-permute-start(bf16[4,8192]{1,0:T(4,128)(2,1)} %bitcast.128), channel_id=1, source_target_pairs={{0,8},{8,0},{1,9},{9,1},{2,10},{10,2},{3,11},{11,3},{4,12},{12,4},... | collective-permute-start | bytes 196616 | tf_op jit(solution)/shard_map/ppermute | solution.py:18
  23.8 11.5 %copy-start.1 = (bf16[1,1,4,2,1024]{4,3,2,1,0:T(2,128)(2,1)S(1)}, bf16[1,1,4,2,1024]{4,3,2,1,0:T(2,128)(2,1)}, u32[]{:S(2)}) copy-start(bf16[1,1,4,2,1024]{4,3,2,1,0:T(2,128)(2,1)} %param.8) | copy-start | bytes 49156
  25.6 34.3 %all-to-all-start = ((bf16[8,576,128]{2,1,0:T(8,128)(2,1)}), bf16[8,576,128]{2,1,0:T(8,128)(2,1)S(1)}, u32[]{:S(2)}, u32[]{:S(2)}) async-start(bf16[8,576,128]{2,1,0:T(8,128)(2,1)} %pad_maximum_fusion), calls=%async_computation | async-start | bytes 2359296 | tf_op jit(solution)/shard_map/all_to_all | solution.py:90
  62.8 3.5 %copy-start = (f32[512,2048]{1,0:T(8,128)S(1)}, f32[512,2048]{1,0:T(8,128)}, u32[]{:S(2)}) copy-start(f32[512,2048]{1,0:T(8,128)} %get-tuple-element.28) | copy-start | bytes 12582916
  69.6 20.9 %all-to-all-start.1 = ((f32[16,33,128]{2,1,0:T(8,128)}), f32[16,33,128]{2,1,0:T(8,128)S(1)}, u32[]{:S(2)}, u32[]{:S(2)}) async-start(f32[16,33,128]{2,1,0:T(8,128)} %pad_maximum_fusion.1), calls=%async_computation.1 | async-start | bytes 655360 | tf_op jit(solution)/shard_map/all_to_all | solution.py:117

commit v4 on v3

--- a/solution.py
+++ b/solution.py
@@ -1,6 +1,7 @@
 import jax
 import jax.numpy as jnp
 from jax import lax
+from jax.experimental import pallas as pl
 from jax.sharding import PartitionSpec as P
 
 QH = 64
@@ -10,6 +11,53 @@
 
 
 NEG = -1e30
+ROW_BLOCK = 128
+
+
+def prefix_kernel(live_ref, query_ref, key_ref, value_ref, numer_ref, max_ref, total_ref):
+    scores = lax.dot_general(
+        query_ref[...], key_ref[...], (((1,), (1,)), ((), ())), preferred_element_type=jnp.float32
+    ) * HEAD_SIZE ** (-0.5)
+    live = live_ref[...] > 0
+    masked = jnp.where(live, scores, NEG)
+    maxima = jnp.max(masked, axis=1, keepdims=True)
+    weights = jnp.where(live, jnp.exp(masked - maxima), 0.0)
+    max_ref[...] = maxima
+    total_ref[...] = jnp.sum(weights, axis=1, keepdims=True)
+    high = weights.astype(jnp.bfloat16)
+    low = (weights - high.astype(jnp.float32)).astype(jnp.bfloat16)
+    values = value_ref[...]
+    numer_ref[...] = jnp.dot(high, values, preferred_element_type=jnp.float32) + jnp.dot(
+        low, values, preferred_element_type=jnp.float32
+    )
+
+
+def prefix_attention(live, query_matrix, keys, values):
+    rows, width = query_matrix.shape
+    span = keys.shape[0]
+    return pl.pallas_call(
+        prefix_kernel,
+        grid=(rows // ROW_BLOCK,),
+        in_specs=[
+            pl.BlockSpec((1, span), lambda i: (0, 0)),
+            pl.BlockSpec((ROW_BLOCK, width), lambda i: (i, 0)),
+            pl.BlockSpec((span, width), lambda i: (0, 0)),
+            pl.BlockSpec((span, width), lambda i: (0, 0)),
+        ],
+        out_specs=[
+            pl.BlockSpec((ROW_BLOCK, width), lambda i: (i, 0)),
+            pl.BlockSpec((ROW_BLOCK, 1), lambda i: (i, 0)),
+            pl.BlockSpec((ROW_BLOCK, 1), lambda i: (i, 0)),
+        ],
+        out_shape=[
+            jax.ShapeDtypeStruct((rows, width), jnp.float32),
+            jax.ShapeDtypeStruct((rows, 1), jnp.float32),
+            jax.ShapeDtypeStruct((rows, 1), jnp.float32),
+        ],
+        cost_estimate=pl.CostEstimate(
+            flops=6 * rows * span * width, transcendentals=rows * span, bytes_accessed=2 * (rows + 2 * span) * width + 8 * rows * width
+        ),
+    )(live, query_matrix, keys, values)
 
 
 def shifted(value, axis, steps):
@@ -25,14 +73,6 @@
     return jnp.einsum(form, high, value_matrix, preferred_element_type=jnp.float32) + jnp.einsum(
         form, low, value_matrix, preferred_element_type=jnp.float32
     )
-
-
-def softmax_terms(logit_scores, valid_mask, value_matrix, form):
-    masked = jnp.where(valid_mask, logit_scores, NEG)
-    maxima = jnp.max(masked, axis=-1)
-    weights = jnp.where(valid_mask, jnp.exp(masked - maxima[..., None]), 0.0)
-    totals = jnp.sum(weights, axis=-1)
-    return split_dot(weights, value_matrix, form), maxima, totals
 
 
 def suffix_terms(query_rows, cache, fresh, length):
@@ -100,9 +140,8 @@
     offset = jnp.arange(block_len, dtype=jnp.int32)[None, None, :]
     prefix_half_len = block_len * team_count * 2
     positions = half * prefix_half_len + (team * team_count + member) * block_len + offset
-    valid = (positions.reshape(-1) < prefix_len[prompt_row])[None, :]
-    scores = jnp.einsum("rd,kd->rk", query_matrix, keys, preferred_element_type=jnp.float32) * HEAD_SIZE ** (-0.5)
-    numerator, maxima, totals = softmax_terms(scores, valid, values, "rk,kd->rd")
+    live = (positions.reshape(1, -1) < prefix_len[prompt_row]).astype(jnp.int32)
+    numerator, maxima, totals = prefix_attention(live, query_matrix, keys, values)
     sample_count = 2 * team_count
     numerator = numerator.reshape(sample_count, rows_per_sample, HEAD_SIZE)
     stats = jnp.concatenate(

time: 93.3 us -> 94.4 us (1.012)
  Pallas kernels: 0 us -> 5.72 us
  matrix products: 7.02 us -> 1.92 us
  waiting for transfers between devices: 34.9 us -> 37.6 us
  local copies, waits for them, and re-layouts: 10.2 us -> 7.75 us
    pallas_call x0 -> x1, Pallas kernels: none -> 5.72 us  [prefix_attention(): pl.pallas_call(prefix_kernel, grid=(rows // ROW_BLOCK,), in_specs=[pl.Blo...]
    unnamed x10, local copies, waits for them, and re-layouts: 6.06 us -> 1.93 us
    reduce_sum x1 -> x0, other arithmetic: 3.43 us -> none  [softmax_terms(): totals = jnp.sum(weights, axis=-1)]
    all_to_all x1, waiting for transfers between devices: 22.8 us -> 25.5 us  [per_device(): gathered = lax.all_to_all(outgoing, ('zl', 'core'), 0, 0, tiled=True)]
    dot_general x1 -> x0, matrix products: 2.68 us -> none  [per_device(): jnp.einsum('rd,kd->rk', query_matrix, keys, preferred_element_type=jnp.fl...]
    pallas_call x0 -> x2, other arithmetic: none -> 2.19 us  [prefix_attention(): pl.pallas_call(prefix_kernel, grid=(rows // ROW_BLOCK,), in_specs=[pl.Blo...]
    another operation x0 -> x2, local copies, waits for them, and re-layouts: none -> 1.71 us  [per_device(): jnp.stack([prefix_head[0].reshape(block_len, 2, KVH, HEAD_SIZE), moved_ta...]
    dot_general x3 -> x2, matrix products: 1.99 us -> 0.64 us  [split_dot(): jnp.einsum(form, low, value_matrix, preferred_element_type=jnp.float32)]
  transfers between devices with their start and end apart: 4 -> 4, of which waited for: 2 -> 2; matrix products, arithmetic and copies ran while one was open for 10% -> 9% of each run, Pallas kernels for 0% -> 0%
where the time goes in v4:
time: 94.4 us; the launch traced here: 93.8 us
  waiting for transfers between devices  37.6 us (40%)
  starting transfers between devices  31.5 us (33%)
  other arithmetic  8.33 us (9%)
  local copies, waits for them, and re-layouts  7.75 us (8%)
  Pallas kernels  5.72 us (6%)
  matrix products  1.92 us (2%)
  between operations  1.02 us (1%)
    all_to_all x1, waiting for transfers between devices, per_device(): gathered = lax.all_to_all(outgoing, ('zl', 'core'), 0, 0, tiled=True)  25.5 us
    ppermute x2, starting transfers between devices, shifted(): return lax.ppermute(value, axis, pairs)  18.9 us
    all_to_all x1, waiting for transfers between devices, per_device(): lax.all_to_all(outgoing_parts, ('zg', 'zl', 'core'), 0, 0, tiled=True)  12 us
    all_to_all x1, starting transfers between devices, per_device(): lax.all_to_all(outgoing_parts, ('zg', 'zl', 'core'), 0, 0, tiled=True)  6.81 us
    all_to_all x1, starting transfers between devices, per_device(): gathered = lax.all_to_all(outgoing, ('zl', 'core'), 0, 0, tiled=True)  5.8 us
    pallas_call x1, Pallas kernels, prefix_attention(): pl.pallas_call(prefix_kernel, grid=(rows // ROW_BLOCK,), in_specs=[pl.Blo...  5.72 us
    pallas_call x2, other arithmetic, prefix_attention(): pl.pallas_call(prefix_kernel, grid=(rows // ROW_BLOCK,), in_specs=[pl.Blo...  2.19 us
    unnamed x10, local copies, waits for them, and re-layouts  1.93 us
  transfers between devices with their start and end apart: 4, of which 2 were waited for; matrix products, arithmetic and copies ran while one was open for 9% of the time, Pallas kernels for 0%

profile of v4, /device:TPU:1, one launch (start us, length us, event | category | flops | bytes accessed | tf_op | source)
XLA Modules:
  0.0 93.8 jit_solution(725172895544296730)
XLA Ops:
  0.0 8.2 %collective-permute-start = (bf16[1,128,2,1024]{3,2,1,0:T(2,128)(2,1)}, bf16[1,128,2,1024]{3,2,1,0:T(2,128)(2,1)S(1)}, u32[]{:S(2)}, u32[]{:S(2)}) collective-permute-start(bf16[1,128,2,1024]{3,2,1,0:T(2,128)(2,1)} %param.12), channel_id=1, source_target_pairs={{0,496},{16,0},{32,16},{48,32},{64,48},{80,64},{96,80},{112,96},{1... | collective-permute-start | bytes 1572872 | tf_op jit(solution)/shard_map/ppermute | solution.py:66
  8.3 10.6 %collective-permute-start.1 = (bf16[4,8192]{1,0:T(4,128)(2,1)}, bf16[4,8192]{1,0:T(4,128)(2,1)S(1)}, u32[]{:S(2)}, u32[]{:S(2)}) collective-permute-start(bf16[4,8192]{1,0:T(4,128)(2,1)} %bitcast.122), channel_id=1, source_target_pairs={{0,8},{8,0},{1,9},{9,1},{2,10},{10,2},{3,11},{11,3},{4,12},{12,4},... | collective-permute-start | bytes 196616 | tf_op jit(solution)/shard_map/ppermute | solution.py:66
  18.9 0.9 copy.155
  19.8 1.4 %stack_reshape_squeeze.6 = bf16[1,128,2,8,128]{4,3,2,1,0:T(8,128)(2,1)S(1)} reshape(bf16[1,128,2,1024]{3,2,1,0:T(2,128)(2,1)} %param.11) | data formatting | bytes 1048576 | tf_op jit(solution)/shard_map/stack;reshape;squeeze | solution.py:121
  21.8 1.1 %copy.85 = bf16[1,1,256,2,1024]{2,4,3,1,0:T(8,128)(2,1)S(1)} copy(bf16[1,1,256,2,1024]{4,3,2,1,0:T(2,128)(2,1)S(1)} %copy-done) | data formatting | bytes 2097152 | tf_op args[2]
  23.0 0.7 dynamic_slice.3
  23.8 0.3 stack_reshape_squeeze.7
  24.1 0.1 maximum_bitcast_fusion
  24.2 0.3 copy.78
  24.5 1.1 %pad_maximum_fusion = bf16[8,576,128]{2,1,0:T(8,128)(2,1)} fusion(bf16[8,32,128]{2,1,0:T(8,128)(2,1)S(1)} %get-tuple-element.33, bf16[8,32,128]{2,1,0:T(8,128)(2,1)S(1)} %get-tuple-element.34, bf16[8,512,128]{2,1,0:T(8,128)(2,1)S(1)} %bitcast.102), kind=kLoop, calls=%fused_computation | loop fusion | flops 3538944 | bytes 2359296 | tf_op jit(solution)/shard_map/concatenate | solution.py:129
  25.6 5.8 %all-to-all-start = ((bf16[8,576,128]{2,1,0:T(8,128)(2,1)}), bf16[8,576,128]{2,1,0:T(8,128)(2,1)S(1)}, u32[]{:S(2)}, u32[]{:S(2)}) async-start(bf16[8,576,128]{2,1,0:T(8,128)(2,1)} %pad_maximum_fusion), calls=%async_computation | async-start | bytes 2359296 | tf_op jit(solution)/shard_map/all_to_all | solution.py:130
  31.4 0.4 fusion.34
  31.9 0.3 fusion.33
  32.2 0.2 fusion.7
  32.5 1.3 %compare_convert_fusion = s32[8,2,128]{2,1,0:T(2,128)} fusion(s32[]{:T(128)} %bitcast, s32[8,2]{1,0:T(8,128)S(1)} %broadcast_add_fusion), kind=kLoop, calls=%fused_computation.46 | loop fusion | flops 6144 | bytes 8260 | tf_op jit(solution)/shard_map/convert_element_type | solution.py:143
  33.8 0.3 fusion.21
  34.1 0.3 convolution_add_fusion.1
  34.4 25.5 %all-to-all-done = bf16[8,576,128]{2,1,0:T(8,128)(2,1)S(1)} async-done(((bf16[8,576,128]{2,1,0:T(8,128)(2,1)}), bf16[8,576,128]{2,1,0:T(8,128)(2,1)S(1)}, u32[]{:S(2)}, u32[]{:S(2)}) %all-to-all-start) | async-done | bytes 1179680 | tf_op jit(solution)/shard_map/all_to_all | solution.py:130
  60.0 0.7 reverse_select_fusion
  60.7 1.1 %fusion.31 = (bf16[8,256,128]{2,1,0:T(8,128)(2,1)}, bf16[8,256,128]{2,1,0:T(8,128)(2,1)}) fusion(bf16[8,576,128]{2,1,0:T(8,128)(2,1)S(1)} %all-to-all-done), kind=kLoop, calls=%fused_computation.73 | loop fusion | bytes 2097152 | tf_op jit(solution)/shard_map/slice | solution.py:133
  61.7 5.7 %shard_map.73 = (f32[512,128]{1,0:T(8,128)}, f32[512,1]{1,0:T(8,128)}, f32[512,1]{1,0:T(8,128)}) custom-call(s32[1,2048]{1,0:T(1,128)} %bitcast.129, bf16[512,128]{1,0:T(8,128)(2,1)} %bitcast.114, bf16[2048,128]{1,0:T(8,128)(2,1)} %bitcast.108, bf16[2048,128]{1,0:T(8,128)(2,1)} %bitcast.107), custom_call_target="tpu_custom_call" | custom-call | flops 805306368 | bytes 1703936 | tf_op jit(solution)/shard_map/pallas_call | solution.py:38
  67.4 1.1 %reduce = f32[512]{0:T(512)S(1)} reduce(f32[512,1]{1,0:T(8,128)} %get-tuple-element.9, f32[]{:T(128)} %constant.38), dimensions={1}, to_apply=%get-tuple-element.9.reduce_sub_computation | reduce | bytes 4100 | tf_op jit(solution)/shard_map/pallas_call | solution.py:38
  68.6 1.1 %reduce.1 = f32[512]{0:T(512)S(1)} reduce(f32[512,1]{1,0:T(8,128)} %get-tuple-element.10, f32[]{:T(128)} %constant.38), dimensions={1}, to_apply=%get-tuple-element.10.reduce_sub_computation | reduce | bytes 4100 | tf_op jit(solution)/shard_map/pallas_call | solution.py:38
  69.9 1.7 %pad_maximum_fusion.1 = f32[16,33,128]{2,1,0:T(8,128)} fusion(f32[16,1,128]{2,1,0:T(1,128)S(1)} %bitcast.125, f32[16,32,128]{2,1,0:T(8,128)} %bitcast.110), kind=kLoop, calls=%fused_computation.14 | loop fusion | flops 67584 | bytes 540672 | tf_op jit(solution)/shard_map/concatenate | solution.py:155
  71.6 6.8 %all-to-all-start.1 = ((f32[16,33,128]{2,1,0:T(8,128)}), f32[16,33,128]{2,1,0:T(8,128)S(1)}, u32[]{:S(2)}, u32[]{:S(2)}) async-start(f32[16,33,128]{2,1,0:T(8,128)} %pad_maximum_fusion.1), calls=%async_computation.1 | async-start | bytes 655360 | tf_op jit(solution)/shard_map/all_to_all | solution.py:156
  78.4 0.1 fusion.25
  78.7 0.3 fusion.9
  79.0 0.3 fusion.3
  79.4 12.0 %all-to-all-done.1 = f32[16,33,128]{2,1,0:T(8,128)S(1)} async-done(((f32[16,33,128]{2,1,0:T(8,128)}), f32[16,33,128]{2,1,0:T(8,128)S(1)}, u32[]{:S(2)}, u32[]{:S(2)}) %all-to-all-start.1) | async-done | bytes 270368 | tf_op jit(solution)/shard_map/all_to_all | solution.py:156
  91.4 0.1 slice_reduce_fusion.3
  92.2 0.1 div.17
  93.1 0.7 fusion.16
  (58 shorter events, 2.2 us)
Async XLA Ops:
  0.0 21.8 %copy-start = (bf16[1,1,256,2,1024]{4,3,2,1,0:T(2,128)(2,1)S(1)}, bf16[1,1,256,2,1024]{4,3,2,1,0:T(2,128)(2,1)}, u32[]{:S(2)}) copy-start(bf16[1,1,256,2,1024]{4,3,2,1,0:T(2,128)(2,1)} %param.9) | copy-start | bytes 3145732
  0.0 23.8 %collective-permute-start = (bf16[1,128,2,1024]{3,2,1,0:T(2,128)(2,1)}, bf16[1,128,2,1024]{3,2,1,0:T(2,128)(2,1)S(1)}, u32[]{:S(2)}, u32[]{:S(2)}) collective-permute-start(bf16[1,128,2,1024]{3,2,1,0:T(2,128)(2,1)} %param.12), channel_id=1, source_target_pairs={{0,496},{16,0},{32,16},{48,32},{64,48},{80,64},{96,80},{112,96},{1... | collective-permute-start | bytes 1572872 | tf_op jit(solution)/shard_map/ppermute | solution.py:66
  8.3 15.5 %collective-permute-start.1 = (bf16[4,8192]{1,0:T(4,128)(2,1)}, bf16[4,8192]{1,0:T(4,128)(2,1)S(1)}, u32[]{:S(2)}, u32[]{:S(2)}) collective-permute-start(bf16[4,8192]{1,0:T(4,128)(2,1)} %bitcast.122), channel_id=1, source_target_pairs={{0,8},{8,0},{1,9},{9,1},{2,10},{10,2},{3,11},{11,3},{4,12},{12,4},... | collective-permute-start | bytes 196616 | tf_op jit(solution)/shard_map/ppermute | solution.py:66
  21.1 1.8 %copy-start.1 = (bf16[1,1,4,2,1024]{4,3,2,1,0:T(2,128)(2,1)S(1)}, bf16[1,1,4,2,1024]{4,3,2,1,0:T(2,128)(2,1)}, u32[]{:S(2)}) copy-start(bf16[1,1,4,2,1024]{4,3,2,1,0:T(2,128)(2,1)} %param.8) | copy-start | bytes 49156
  21.2 1.9 %copy-start.2 = (s32[32]{0:T(128)S(1)}, s32[32]{0:T(128)}, u32[]{:S(2)}) copy-start(s32[32]{0:T(128)} %param.13) | copy-start | bytes 388
  25.6 34.3 %all-to-all-start = ((bf16[8,576,128]{2,1,0:T(8,128)(2,1)}), bf16[8,576,128]{2,1,0:T(8,128)(2,1)S(1)}, u32[]{:S(2)}, u32[]{:S(2)}) async-start(bf16[8,576,128]{2,1,0:T(8,128)(2,1)} %pad_maximum_fusion), calls=%async_computation | async-start | bytes 2359296 | tf_op jit(solution)/shard_map/all_to_all | solution.py:130
  71.6 19.9 %all-to-all-start.1 = ((f32[16,33,128]{2,1,0:T(8,128)}), f32[16,33,128]{2,1,0:T(8,128)S(1)}, u32[]{:S(2)}, u32[]{:S(2)}) async-start(f32[16,33,128]{2,1,0:T(8,128)} %pad_maximum_fusion.1), calls=%async_computation.1 | async-start | bytes 655360 | tf_op jit(solution)/shard_map/all_to_all | solution.py:156

commit v5 on v4

--- a/solution.py
+++ b/solution.py
@@ -14,27 +14,32 @@
 ROW_BLOCK = 128
 
 
-def prefix_kernel(live_ref, query_ref, key_ref, value_ref, numer_ref, max_ref, total_ref):
+def prefix_kernel(bias_ref, query_ref, key_ref, value_ref, out_ref):
     scores = lax.dot_general(
         query_ref[...], key_ref[...], (((1,), (1,)), ((), ())), preferred_element_type=jnp.float32
-    ) * HEAD_SIZE ** (-0.5)
-    live = live_ref[...] > 0
-    masked = jnp.where(live, scores, NEG)
-    maxima = jnp.max(masked, axis=1, keepdims=True)
-    weights = jnp.where(live, jnp.exp(masked - maxima), 0.0)
-    max_ref[...] = maxima
-    total_ref[...] = jnp.sum(weights, axis=1, keepdims=True)
+    ) * HEAD_SIZE ** (-0.5) + bias_ref[...]
+    maxima = jnp.max(scores, axis=1, keepdims=True)
+    weights = jnp.exp(scores - maxima)
+    totals = jnp.sum(weights, axis=1, keepdims=True)
     high = weights.astype(jnp.bfloat16)
     low = (weights - high.astype(jnp.float32)).astype(jnp.bfloat16)
     values = value_ref[...]
-    numer_ref[...] = jnp.dot(high, values, preferred_element_type=jnp.float32) + jnp.dot(
+    numer = jnp.dot(high, values, preferred_element_type=jnp.float32) + jnp.dot(
         low, values, preferred_element_type=jnp.float32
     )
+    samples, rows, width = out_ref.shape
+    rows = rows - 2
+    out_ref[:, :rows, :] = numer.reshape(samples, rows, width)
+    max_row = jnp.transpose(jnp.broadcast_to(maxima, (ROW_BLOCK, ROW_BLOCK)))[0:1, :]
+    total_row = jnp.transpose(jnp.broadcast_to(totals, (ROW_BLOCK, ROW_BLOCK)))[0:1, :]
+    out_ref[:, rows : rows + 1, :] = jnp.broadcast_to(max_row[None], (samples, 1, width))
+    out_ref[:, rows + 1 : rows + 2, :] = jnp.broadcast_to(total_row[None], (samples, 1, width))
 
 
-def prefix_attention(live, query_matrix, keys, values):
+def prefix_attention(bias, query_matrix, keys, values, rows_per_sample):
     rows, width = query_matrix.shape
     span = keys.shape[0]
+    per_block = ROW_BLOCK // rows_per_sample
     return pl.pallas_call(
         prefix_kernel,
         grid=(rows // ROW_BLOCK,),
@@ -44,20 +49,12 @@
             pl.BlockSpec((span, width), lambda i: (0, 0)),
             pl.BlockSpec((span, width), lambda i: (0, 0)),
         ],
-        out_specs=[
-            pl.BlockSpec((ROW_BLOCK, width), lambda i: (i, 0)),
-            pl.BlockSpec((ROW_BLOCK, 1), lambda i: (i, 0)),
-            pl.BlockSpec((ROW_BLOCK, 1), lambda i: (i, 0)),
-        ],
-        out_shape=[
-            jax.ShapeDtypeStruct((rows, width), jnp.float32),
-            jax.ShapeDtypeStruct((rows, 1), jnp.float32),
-            jax.ShapeDtypeStruct((rows, 1), jnp.float32),
-        ],
+        out_specs=pl.BlockSpec((per_block, rows_per_sample + 2, width), lambda i: (i, 0, 0)),
+        out_shape=jax.ShapeDtypeStruct((rows // rows_per_sample, rows_per_sample + 2, width), jnp.float32),
         cost_estimate=pl.CostEstimate(
-            flops=6 * rows * span * width, transcendentals=rows * span, bytes_accessed=2 * (rows + 2 * span) * width + 8 * rows * width
+            flops=6 * rows * span * width, transcendentals=rows * span, bytes_accessed=2 * (rows + 2 * span) * width + 4 * rows * width
         ),
-    )(live, query_matrix, keys, values)
+    )(bias, query_matrix, keys, values)
 
 
 def shifted(value, axis, steps):
@@ -140,28 +137,21 @@
     offset = jnp.arange(block_len, dtype=jnp.int32)[None, None, :]
     prefix_half_len = block_len * team_count * 2
     positions = half * prefix_half_len + (team * team_count + member) * block_len + offset
-    live = (positions.reshape(1, -1) < prefix_len[prompt_row]).astype(jnp.int32)
-    numerator, maxima, totals = prefix_attention(live, query_matrix, keys, values)
+    bias = jnp.where(positions.reshape(1, -1) < prefix_len[prompt_row], 0.0, NEG).astype(jnp.float32)
     sample_count = 2 * team_count
-    numerator = numerator.reshape(sample_count, rows_per_sample, HEAD_SIZE)
-    stats = jnp.concatenate(
-        [
-            maxima.reshape(sample_count, rows_per_sample),
-            totals.reshape(sample_count, rows_per_sample),
-            jnp.zeros((sample_count, HEAD_SIZE - 2 * rows_per_sample), jnp.float32),
-        ],
-        axis=1,
-    )
-    outgoing_parts = jnp.concatenate([numerator, stats[:, None, :]], axis=1)
+    outgoing_parts = prefix_attention(bias, query_matrix, keys, values, rows_per_sample)
     returned = lax.all_to_all(outgoing_parts, ("zg", "zl", "core"), 0, 0, tiled=True)
-    returned = returned.reshape(2, KVH, rows_per_sample + 1, HEAD_SIZE)
+    returned = returned.reshape(2, KVH, rows_per_sample + 2, HEAD_SIZE)
+    lane_offset = (lax.axis_index(("zg", "zl", "core")) % (ROW_BLOCK // rows_per_sample)) * rows_per_sample
 
     def unpack(parts):
         numer = parts[:, :rows_per_sample].reshape(KVH, step_count, GROUP, HEAD_SIZE)
         numer = numer.transpose(1, 0, 2, 3).reshape(step_count, QH, HEAD_SIZE)
-        maxi = parts[:, rows_per_sample, :rows_per_sample].reshape(KVH, step_count, GROUP)
+        maxi = lax.dynamic_slice_in_dim(parts[:, rows_per_sample], lane_offset, rows_per_sample, axis=1)
+        maxi = maxi.reshape(KVH, step_count, GROUP)
         maxi = maxi.transpose(1, 0, 2).reshape(step_count, QH)
-        tot = parts[:, rows_per_sample, rows_per_sample : 2 * rows_per_sample].reshape(KVH, step_count, GROUP)
+        tot = lax.dynamic_slice_in_dim(parts[:, rows_per_sample + 1], lane_offset, rows_per_sample, axis=1)
+        tot = tot.reshape(KVH, step_count, GROUP)
         tot = tot.transpose(1, 0, 2).reshape(step_count, QH)
         return numer, maxi, tot
 

time: 94.4 us -> 90.5 us (0.959)
  other arithmetic: 8.33 us -> 4.92 us
    pallas_call x2 -> x0, other arithmetic: 2.19 us -> none  [prefix_attention(): pl.pallas_call(prefix_kernel, grid=(rows // ROW_BLOCK,), in_specs=[pl.Blo...]
    concatenate x2 -> x0, other arithmetic: 1.77 us -> none  [the longest x1 1.7 us: per_device(): outgoing_parts = jnp.concatenate([numerator, stats[:, None, :]], axis=1)]
    convert_element_type x1 -> x0, other arithmetic: 1.3 us -> none  [per_device(): live = (positions.reshape(1, -1) < prefix_len[prompt_row]).astype(jnp.int32)]
    select_n x0 -> x1, other arithmetic: none -> 1.28 us  [per_device(): jnp.where(positions.reshape(1, -1) < prefix_len[prompt_row], 0.0, NEG)]
    all_to_all x1, starting transfers between devices: 6.81 us -> 5.78 us  [per_device(): lax.all_to_all(outgoing_parts, ('zg', 'zl', 'core'), 0, 0, tiled=True)]
    unnamed x10 -> x22, local copies, waits for them, and re-layouts: 1.93 us -> 2.55 us
  transfers between devices with their start and end apart: 4 -> 4, of which waited for: 2 -> 2; matrix products, arithmetic and copies ran while one was open for 9% -> 11% of each run, Pallas kernels for 0% -> 0%
where the time goes in v5:
time: 90.5 us; the launch traced here: 90 us
  waiting for transfers between devices  36.8 us (41%)
  starting transfers between devices  30.6 us (34%)
  local copies, waits for them, and re-layouts  8.38 us (9%)
  Pallas kernels  5.58 us (6%)
  other arithmetic  4.92 us (5%)
  matrix products  2.62 us (3%)
  between operations  1.09 us (1%)
    all_to_all x1, waiting for transfers between devices, per_device(): gathered = lax.all_to_all(outgoing, ('zl', 'core'), 0, 0, tiled=True)  24.8 us
    ppermute x2, starting transfers between devices, shifted(): return lax.ppermute(value, axis, pairs)  18.9 us
    all_to_all x1, waiting for transfers between devices, per_device(): lax.all_to_all(outgoing_parts, ('zg', 'zl', 'core'), 0, 0, tiled=True)  12 us
    all_to_all x1, starting transfers between devices, per_device(): gathered = lax.all_to_all(outgoing, ('zl', 'core'), 0, 0, tiled=True)  5.93 us
    all_to_all x1, starting transfers between devices, per_device(): lax.all_to_all(outgoing_parts, ('zg', 'zl', 'core'), 0, 0, tiled=True)  5.78 us
    pallas_call x1, Pallas kernels, prefix_attention(): pl.pallas_call(prefix_kernel, grid=(rows // ROW_BLOCK,), in_specs=[pl.Blo...  5.58 us
    unnamed x22, local copies, waits for them, and re-layouts  2.55 us
  transfers between devices with their start and end apart: 4, of which 2 were waited for; matrix products, arithmetic and copies ran while one was open for 11% of the time, Pallas kernels for 0%

profile of v5, /device:TPU:1, one launch (start us, length us, event | category | flops | bytes accessed | tf_op | source)
XLA Modules:
  0.0 90.0 jit_solution(3593278796511125284)
XLA Ops:
  0.0 8.2 %collective-permute-start = (bf16[1,128,2,1024]{3,2,1,0:T(2,128)(2,1)}, bf16[1,128,2,1024]{3,2,1,0:T(2,128)(2,1)S(1)}, u32[]{:S(2)}, u32[]{:S(2)}) collective-permute-start(bf16[1,128,2,1024]{3,2,1,0:T(2,128)(2,1)} %param.12), channel_id=1, source_target_pairs={{0,496},{16,0},{32,16},{48,32},{64,48},{80,64},{96,80},{112,96},{1... | collective-permute-start | bytes 1572872 | tf_op jit(solution)/shard_map/ppermute | solution.py:63
  8.3 10.6 %collective-permute-start.1 = (bf16[4,8192]{1,0:T(4,128)(2,1)}, bf16[4,8192]{1,0:T(4,128)(2,1)S(1)}, u32[]{:S(2)}, u32[]{:S(2)}) collective-permute-start(bf16[4,8192]{1,0:T(4,128)(2,1)} %bitcast.115), channel_id=1, source_target_pairs={{0,8},{8,0},{1,9},{9,1},{2,10},{10,2},{3,11},{11,3},{4,12},{12,4},... | collective-permute-start | bytes 196616 | tf_op jit(solution)/shard_map/ppermute | solution.py:63
  18.9 0.9 copy.150
  19.8 1.4 %stack_reshape_squeeze.6 = bf16[1,128,2,8,128]{4,3,2,1,0:T(8,128)(2,1)S(1)} reshape(bf16[1,128,2,1024]{3,2,1,0:T(2,128)(2,1)} %param.11) | data formatting | bytes 1048576 | tf_op jit(solution)/shard_map/stack;reshape;squeeze | solution.py:118
  21.8 1.1 %copy.84 = bf16[1,1,256,2,1024]{2,4,3,1,0:T(8,128)(2,1)S(1)} copy(bf16[1,1,256,2,1024]{4,3,2,1,0:T(2,128)(2,1)S(1)} %copy-done) | data formatting | bytes 2097152 | tf_op args[2]
  23.0 0.6 copy.149
  23.6 0.6 dynamic_slice.15
  24.2 0.6 iota_compare_fusion
  24.8 0.3 stack_reshape_squeeze.7
  25.2 0.1 maximum_bitcast_fusion
  25.3 0.3 copy.77
  25.6 1.1 %pad_maximum_fusion = bf16[8,576,128]{2,1,0:T(8,128)(2,1)} fusion(bf16[8,32,128]{2,1,0:T(8,128)(2,1)S(1)} %get-tuple-element.27, bf16[8,32,128]{2,1,0:T(8,128)(2,1)S(1)} %get-tuple-element.28, bf16[8,512,128]{2,1,0:T(8,128)(2,1)S(1)} %bitcast.98), kind=kLoop, calls=%fused_computation | loop fusion | flops 3538944 | bytes 2359296 | tf_op jit(solution)/shard_map/concatenate | solution.py:126
  26.7 5.9 %all-to-all-start = ((bf16[8,576,128]{2,1,0:T(8,128)(2,1)}), bf16[8,576,128]{2,1,0:T(8,128)(2,1)S(1)}, u32[]{:S(2)}, u32[]{:S(2)}) async-start(bf16[8,576,128]{2,1,0:T(8,128)(2,1)} %pad_maximum_fusion), calls=%async_computation | async-start | bytes 2359296 | tf_op jit(solution)/shard_map/all_to_all | solution.py:127
  32.6 0.4 fusion.35
  33.1 0.3 fusion.34
  33.5 0.2 fusion.7
  33.7 1.3 %compare_select_fusion = f32[8,2,128]{2,1,0:T(2,128)} fusion(s32[]{:T(128)} %bitcast, s32[8,2]{1,0:T(8,128)S(1)} %broadcast_add_fusion), kind=kLoop, calls=%fused_computation.43 | loop fusion | flops 6144 | bytes 8260 | tf_op jit(solution)/shard_map/jit(_where)/select_n | solution.py:140
  35.0 0.3 fusion.21
  35.3 1.0 %convolution_add_fusion.1 = f32[8,4,8,128]{3,2,1,0:T(8,128)S(1)} fusion(f32[8,4,8,128]{3,2,1,0:T(8,128)S(1)} %fusion.21, bf16[4,8,128,1]{2,1,0,3:T(8,128)(2,1)} %bitcast.109, f32[4,8,8,4]{2,3,0,1:T(4,128)S(1)} %get-tuple-element.26, f32[4,8,8]{2,0,1:T(4,128)S(1)} %max.57, pred[4,4]{1,0:T(4,128)(4,1)S(1)} %copy-done.6), kind=kOutput, calls=%fused_computation.7 | convolution fusion | flops 300032 | bytes 275472 | tf_op jit(solution)/shard_map/tkgu,ukd->tkgd/dot_general | solution.py:70
  36.3 24.8 %all-to-all-done = bf16[8,576,128]{2,1,0:T(8,128)(2,1)S(1)} async-done(((bf16[8,576,128]{2,1,0:T(8,128)(2,1)}), bf16[8,576,128]{2,1,0:T(8,128)(2,1)S(1)}, u32[]{:S(2)}, u32[]{:S(2)}) %all-to-all-start) | async-done | bytes 1179680 | tf_op jit(solution)/shard_map/all_to_all | solution.py:127
  61.2 0.7 reverse_select_fusion
  61.8 1.1 %fusion.31 = (bf16[8,256,128]{2,1,0:T(8,128)(2,1)}, bf16[8,256,128]{2,1,0:T(8,128)(2,1)}) fusion(bf16[8,576,128]{2,1,0:T(8,128)(2,1)S(1)} %all-to-all-done), kind=kLoop, calls=%fused_computation.69 | loop fusion | bytes 2097152 | tf_op jit(solution)/shard_map/slice | solution.py:130
  62.9 5.6 %shard_map.73 = f32[16,34,128]{2,1,0:T(8,128)} custom-call(f32[1,2048]{1,0:T(1,128)} %bitcast.121, bf16[512,128]{1,0:T(8,128)(2,1)} %bitcast.107, bf16[2048,128]{1,0:T(8,128)(2,1)} %bitcast.103, bf16[2048,128]{1,0:T(8,128)(2,1)} %bitcast.102), custom_call_target="tpu_custom_call" | custom-call | flops 805306368 | bytes 1441792 | tf_op jit(solution)/shard_map/pallas_call | solution.py:43
  68.5 5.8 %all-to-all-start.1 = ((f32[16,34,128]{2,1,0:T(8,128)}), f32[16,34,128]{2,1,0:T(8,128)S(1)}, u32[]{:S(2)}, u32[]{:S(2)}) async-start(f32[16,34,128]{2,1,0:T(8,128)} %shard_map.73), calls=%async_computation.1 | async-start | bytes 655360 | tf_op jit(solution)/shard_map/all_to_all | solution.py:143
  74.3 0.1 fusion.25
  74.6 0.3 fusion.9
  74.9 0.3 fusion.3
  75.4 12.0 %all-to-all-done.1 = f32[16,34,128]{2,1,0:T(8,128)S(1)} async-done(((f32[16,34,128]{2,1,0:T(8,128)}), f32[16,34,128]{2,1,0:T(8,128)S(1)}, u32[]{:S(2)}, u32[]{:S(2)}) %all-to-all-start.1) | async-done | bytes 278560 | tf_op jit(solution)/shard_map/all_to_all | solution.py:143
  87.6 0.1 dynamic-slice_reduce_fusion.3
  87.9 0.1 dynamic-slice_reduce_fusion.1
  88.4 0.1 div.17
  89.2 0.7 fusion.16
  (66 shorter events, 2.1 us)
Async XLA Ops:
  0.0 21.8 %copy-start = (bf16[1,1,256,2,1024]{4,3,2,1,0:T(2,128)(2,1)S(1)}, bf16[1,1,256,2,1024]{4,3,2,1,0:T(2,128)(2,1)}, u32[]{:S(2)}) copy-start(bf16[1,1,256,2,1024]{4,3,2,1,0:T(2,128)(2,1)} %param.9) | copy-start | bytes 3145732
  0.0 24.8 %collective-permute-start = (bf16[1,128,2,1024]{3,2,1,0:T(2,128)(2,1)}, bf16[1,128,2,1024]{3,2,1,0:T(2,128)(2,1)S(1)}, u32[]{:S(2)}, u32[]{:S(2)}) collective-permute-start(bf16[1,128,2,1024]{3,2,1,0:T(2,128)(2,1)} %param.12), channel_id=1, source_target_pairs={{0,496},{16,0},{32,16},{48,32},{64,48},{80,64},{96,80},{112,96},{1... | collective-permute-start | bytes 1572872 | tf_op jit(solution)/shard_map/ppermute | solution.py:63
  8.3 16.5 %collective-permute-start.1 = (bf16[4,8192]{1,0:T(4,128)(2,1)}, bf16[4,8192]{1,0:T(4,128)(2,1)S(1)}, u32[]{:S(2)}, u32[]{:S(2)}) collective-permute-start(bf16[4,8192]{1,0:T(4,128)(2,1)} %bitcast.115), channel_id=1, source_target_pairs={{0,8},{8,0},{1,9},{9,1},{2,10},{10,2},{3,11},{11,3},{4,12},{12,4},... | collective-permute-start | bytes 196616 | tf_op jit(solution)/shard_map/ppermute | solution.py:63
  21.1 1.8 %copy-start.2 = (bf16[1,1,4,2,1024]{4,3,2,1,0:T(2,128)(2,1)S(1)}, bf16[1,1,4,2,1024]{4,3,2,1,0:T(2,128)(2,1)}, u32[]{:S(2)}) copy-start(bf16[1,1,4,2,1024]{4,3,2,1,0:T(2,128)(2,1)} %param.8) | copy-start | bytes 49156
  21.2 2.4 %copy-start.8 = (s32[32]{0:T(128)S(1)}, s32[32]{0:T(128)}, u32[]{:S(2)}) copy-start(s32[32]{0:T(128)} %param.13) | copy-start | bytes 388
  23.6 11.4 %copy-start.1 = (bf16[1,4,8,128]{3,2,1,0:T(8,128)(2,1)}, bf16[1,4,8,128]{3,2,1,0:T(8,128)(2,1)S(1)}, u32[]{:S(2)}) copy-start(bf16[1,4,8,128]{3,2,1,0:T(8,128)(2,1)S(1)} %copy.148) | copy-start | bytes 24580
  26.6 5.9 %copy-start.3 = (bf16[1,4,8,128]{3,2,1,0:T(8,128)(2,1)S(1)}, bf16[1,4,8,128]{3,2,1,0:T(8,128)(2,1)}, u32[]{:S(2)}) copy-start(bf16[1,4,8,128]{3,2,1,0:T(8,128)(2,1)} %copy.149) | copy-start | bytes 24580
  26.6 6.0 %copy-start.6 = (pred[4,4]{1,0:T(4,128)(4,1)S(1)}, pred[4,4]{1,0:T(4,128)(4,1)}, u32[]{:S(2)}) copy-start(pred[4,4]{1,0:T(4,128)(4,1)} %iota_compare_fusion) | copy-start | bytes 52
  26.7 34.5 %all-to-all-start = ((bf16[8,576,128]{2,1,0:T(8,128)(2,1)}), bf16[8,576,128]{2,1,0:T(8,128)(2,1)S(1)}, u32[]{:S(2)}, u32[]{:S(2)}) async-start(bf16[8,576,128]{2,1,0:T(8,128)(2,1)} %pad_maximum_fusion), calls=%async_computation | async-start | bytes 2359296 | tf_op jit(solution)/shard_map/all_to_all | solution.py:127
  32.6 0.9 copy-start.4
  62.9 11.4 %copy-start.7 = (pred[4,4]{1,0:T(4,128)(4,1)S(1)}, pred[4,4]{1,0:T(4,128)(4,1)}, u32[]{:S(2)}) copy-start(pred[4,4]{1,0:T(4,128)(4,1)} %iota_compare_fusion) | copy-start | bytes 52
  62.9 11.7 %copy-start.5 = (pred[256]{0:T(512)(128)(4,1)S(1)}, pred[256]{0:T(512)(128)(4,1)}, u32[]{:S(2)}) copy-start(pred[256]{0:T(512)(128)(4,1)} %copy-done.4) | copy-start | bytes 772
  68.5 18.8 %all-to-all-start.1 = ((f32[16,34,128]{2,1,0:T(8,128)}), f32[16,34,128]{2,1,0:T(8,128)S(1)}, u32[]{:S(2)}, u32[]{:S(2)}) async-start(f32[16,34,128]{2,1,0:T(8,128)} %shard_map.73), calls=%async_computation.1 | async-start | bytes 655360 | tf_op jit(solution)/shard_map/all_to_all | solution.py:143

commit v6 on v5

--- a/solution.py
+++ b/solution.py
@@ -1,3 +1,5 @@
+import functools
+
 import jax
 import jax.numpy as jnp
 from jax import lax
@@ -14,19 +16,32 @@
 ROW_BLOCK = 128
 
 
-def prefix_kernel(bias_ref, query_ref, key_ref, value_ref, out_ref):
-    scores = lax.dot_general(
-        query_ref[...], key_ref[...], (((1,), (1,)), ((), ())), preferred_element_type=jnp.float32
-    ) * HEAD_SIZE ** (-0.5) + bias_ref[...]
-    maxima = jnp.max(scores, axis=1, keepdims=True)
-    weights = jnp.exp(scores - maxima)
-    totals = jnp.sum(weights, axis=1, keepdims=True)
-    high = weights.astype(jnp.bfloat16)
-    low = (weights - high.astype(jnp.float32)).astype(jnp.bfloat16)
-    values = value_ref[...]
-    numer = jnp.dot(high, values, preferred_element_type=jnp.float32) + jnp.dot(
-        low, values, preferred_element_type=jnp.float32
-    )
+def prefix_kernel(block, bias_ref, query_ref, first_ref, second_ref, out_ref):
+    query = query_ref[...]
+    members = first_ref.shape[0]
+    parts = []
+    for index, source in enumerate((first_ref, second_ref)):
+        keys = source[:, :block, :].reshape(members * block, HEAD_SIZE)
+        values = source[:, block : 2 * block, :].reshape(members * block, HEAD_SIZE)
+        scores = lax.dot_general(
+            query, keys, (((1,), (1,)), ((), ())), preferred_element_type=jnp.float32
+        ) * HEAD_SIZE ** (-0.5) + bias_ref[index : index + 1, :]
+        parts.append((scores, values))
+    maxima = jnp.maximum(
+        jnp.max(parts[0][0], axis=1, keepdims=True), jnp.max(parts[1][0], axis=1, keepdims=True)
+    )
+    numer = None
+    totals = None
+    for scores, values in parts:
+        weights = jnp.exp(scores - maxima)
+        part_total = jnp.sum(weights, axis=1, keepdims=True)
+        high = weights.astype(jnp.bfloat16)
+        low = (weights - high.astype(jnp.float32)).astype(jnp.bfloat16)
+        part = jnp.dot(high, values, preferred_element_type=jnp.float32) + jnp.dot(
+            low, values, preferred_element_type=jnp.float32
+        )
+        numer = part if numer is None else numer + part
+        totals = part_total if totals is None else totals + part_total
     samples, rows, width = out_ref.shape
     rows = rows - 2
     out_ref[:, :rows, :] = numer.reshape(samples, rows, width)
@@ -36,25 +51,25 @@
     out_ref[:, rows + 1 : rows + 2, :] = jnp.broadcast_to(total_row[None], (samples, 1, width))
 
 
-def prefix_attention(bias, query_matrix, keys, values, rows_per_sample):
+def prefix_attention(bias, query_matrix, first, second, block, rows_per_sample):
     rows, width = query_matrix.shape
-    span = keys.shape[0]
+    span = first.shape[0] * block
     per_block = ROW_BLOCK // rows_per_sample
     return pl.pallas_call(
-        prefix_kernel,
+        functools.partial(prefix_kernel, block),
         grid=(rows // ROW_BLOCK,),
         in_specs=[
-            pl.BlockSpec((1, span), lambda i: (0, 0)),
+            pl.BlockSpec(bias.shape, lambda i: (0, 0)),
             pl.BlockSpec((ROW_BLOCK, width), lambda i: (i, 0)),
-            pl.BlockSpec((span, width), lambda i: (0, 0)),
-            pl.BlockSpec((span, width), lambda i: (0, 0)),
+            pl.BlockSpec(first.shape, lambda i: (0, 0, 0)),
+            pl.BlockSpec(second.shape, lambda i: (0, 0, 0)),
         ],
         out_specs=pl.BlockSpec((per_block, rows_per_sample + 2, width), lambda i: (i, 0, 0)),
         out_shape=jax.ShapeDtypeStruct((rows // rows_per_sample, rows_per_sample + 2, width), jnp.float32),
         cost_estimate=pl.CostEstimate(
-            flops=6 * rows * span * width, transcendentals=rows * span, bytes_accessed=2 * (rows + 2 * span) * width + 4 * rows * width
+            flops=3 * rows * span * width, transcendentals=rows * span // 2, bytes_accessed=2 * (rows + span) * width + 4 * rows * width
         ),
-    )(bias, query_matrix, keys, values)
+    )(bias, query_matrix, first, second)
 
 
 def shifted(value, axis, steps):
@@ -115,31 +130,31 @@
     own_rows = queries[0, 0]
     partner_rows = shifted(own_rows, "zg", 1)
 
-    halves = jnp.stack(
-        [prefix_head[0].reshape(block_len, 2, KVH, HEAD_SIZE), moved_tail[0].reshape(block_len, 2, KVH, HEAD_SIZE)]
-    )
-    kv_part = halves.transpose(3, 2, 0, 1, 4).reshape(KVH, 2 * 2 * block_len, HEAD_SIZE)
+    def by_head(block):
+        return block[0].reshape(block_len, 2, KVH, HEAD_SIZE).transpose(2, 1, 0, 3).reshape(KVH, 2 * block_len, HEAD_SIZE)
 
     def query_groups(rows):
         return rows.reshape(step_count, KVH, GROUP, HEAD_SIZE).transpose(1, 0, 2, 3).reshape(KVH, rows_per_sample, HEAD_SIZE)
 
-    outgoing = jnp.concatenate([kv_part, query_groups(own_rows), query_groups(partner_rows)], axis=1)
-    gathered = lax.all_to_all(outgoing, ("zl", "core"), 0, 0, tiled=True)
     span = 2 * block_len
-    keys = gathered[:, :span].reshape(team_count * span, HEAD_SIZE)
-    values = gathered[:, span : 2 * span].reshape(team_count * span, HEAD_SIZE)
-    query_parts = gathered[:, 2 * span :].reshape(team_count, 2, rows_per_sample, HEAD_SIZE).transpose(1, 0, 2, 3)
+    first = lax.all_to_all(
+        jnp.concatenate([by_head(prefix_head), query_groups(own_rows)], axis=1), ("zl", "core"), 0, 0, tiled=True
+    )
+    second = lax.all_to_all(
+        jnp.concatenate([by_head(moved_tail), query_groups(partner_rows)], axis=1), ("zl", "core"), 0, 0, tiled=True
+    )
+    query_parts = jnp.stack([first[:, span:], second[:, span:]])
     query_parts = jnp.where(team == 0, query_parts, query_parts[::-1])
     query_matrix = query_parts.reshape(2 * team_count * rows_per_sample, HEAD_SIZE)
 
-    member = jnp.arange(team_count, dtype=jnp.int32)[:, None, None]
-    half = jnp.arange(2, dtype=jnp.int32)[None, :, None]
+    member = jnp.arange(team_count, dtype=jnp.int32)[None, :, None]
+    half = jnp.arange(2, dtype=jnp.int32)[:, None, None]
     offset = jnp.arange(block_len, dtype=jnp.int32)[None, None, :]
     prefix_half_len = block_len * team_count * 2
     positions = half * prefix_half_len + (team * team_count + member) * block_len + offset
-    bias = jnp.where(positions.reshape(1, -1) < prefix_len[prompt_row], 0.0, NEG).astype(jnp.float32)
+    bias = jnp.where(positions.reshape(2, -1) < prefix_len[prompt_row], 0.0, NEG).astype(jnp.float32)
     sample_count = 2 * team_count
-    outgoing_parts = prefix_attention(bias, query_matrix, keys, values, rows_per_sample)
+    outgoing_parts = prefix_attention(bias, query_matrix, first, second, block_len, rows_per_sample)
     returned = lax.all_to_all(outgoing_parts, ("zg", "zl", "core"), 0, 0, tiled=True)
     returned = returned.reshape(2, KVH, rows_per_sample + 2, HEAD_SIZE)
     lane_offset = (lax.axis_index(("zg", "zl", "core")) % (ROW_BLOCK // rows_per_sample)) * rows_per_sample

time: 90.5 us -> 86 us (0.950)
  waiting for transfers between devices: 36.8 us -> 25.2 us
  starting transfers between devices: 30.6 us -> 37.5 us
    all_to_all x1 -> x2, starting transfers between devices: 5.93 us -> 17.7 us  [the longest x1 10.3 us: per_device(): lax.all_to_all(jnp.concatenate([by_head(prefix_head), query_groups(own_ro...]
    all_to_all x1 -> x2, waiting for transfers between devices: 24.8 us -> 13.2 us  [the longest x1 13.2 us: per_device(): lax.all_to_all(jnp.concatenate([by_head(moved_tail), query_groups(partner...]
    ppermute x2, starting transfers between devices: 18.9 us -> 13.7 us  [shifted(): return lax.ppermute(value, axis, pairs)]
    reshape x1 -> x2, local copies, waits for them, and re-layouts: 0.02 us -> 1.7 us  [query_groups(): rows.reshape(step_count, KVH, GROUP, HEAD_SIZE).transpose(1, 0, 2, 3)]
    another operation x2 -> x6, local copies, waits for them, and re-layouts: 1.71 us -> 3.04 us  [the longest x4 3.02 us: by_head(): block[0].reshape(block_len, 2, KVH, HEAD_SIZE).transpose(2, 1, 0, 3)]
    slice x2 -> x0, local copies, waits for them, and re-layouts: 1.07 us -> none  [the longest x1 1.06 us: per_device(): values = gathered[:, span:2 * span].reshape(team_count * span, HEAD_SIZE)]
    unnamed x22 -> x16, local copies, waits for them, and re-layouts: 2.55 us -> 1.85 us
  transfers between devices with their start and end apart: 4 -> 5, of which waited for: 2 -> 2; matrix products, arithmetic and copies ran while one was open for 11% -> 11% of each run, Pallas kernels for 0% -> 0%
where the time goes in v6:
time: 86 us; the launch traced here: 85.3 us
  starting transfers between devices  37.5 us (44%)
  waiting for transfers between devices  25.2 us (29%)
  local copies, waits for them, and re-layouts  9.2 us (11%)
  Pallas kernels  5.59 us (6%)
  other arithmetic  4.89 us (6%)
  matrix products  1.91 us (2%)
  between operations  1.08 us (1%)
    ppermute x2, starting transfers between devices, shifted(): return lax.ppermute(value, axis, pairs)  13.7 us
    all_to_all x1, waiting for transfers between devices, per_device(): lax.all_to_all(jnp.concatenate([by_head(moved_tail), query_groups(partner...  13.2 us
    all_to_all x1, waiting for transfers between devices, per_device(): lax.all_to_all(outgoing_parts, ('zg', 'zl', 'core'), 0, 0, tiled=True)  12 us
    all_to_all x1, starting transfers between devices, per_device(): lax.all_to_all(jnp.concatenate([by_head(prefix_head), query_groups(own_ro...  10.3 us
    all_to_all x1, starting transfers between devices, per_device(): lax.all_to_all(jnp.concatenate([by_head(moved_tail), query_groups(partner...  7.43 us
    all_to_all x1, starting transfers between devices, per_device(): lax.all_to_all(outgoing_parts, ('zg', 'zl', 'core'), 0, 0, tiled=True)  6.07 us
    pallas_call x1, Pallas kernels, prefix_attention(): pl.pallas_call(functools.partial(prefix_kernel, block), grid=(rows // ROW...  5.59 us
    another operation x4, local copies, waits for them, and re-layouts, by_head(): block[0].reshape(block_len, 2, KVH, HEAD_SIZE).transpose(2, 1, 0, 3)  3.02 us
  transfers between devices with their start and end apart: 5, of which 2 were waited for; matrix products, arithmetic and copies ran while one was open for 11% of the time, Pallas kernels for 0%

profile of v6, /device:TPU:1, one launch (start us, length us, event | category | flops | bytes accessed | tf_op | source)
XLA Modules:
  0.0 85.3 jit_solution(14821235074061603854)
XLA Ops:
  0.0 0.8 copy_bitcast_fusion.3
  0.9 1.4 %reshape_squeeze.22 = bf16[128,2,8,128]{3,2,1,0:T(8,128)(2,1)S(1)} reshape(bf16[1,128,2,1024]{3,2,1,0:T(2,128)(2,1)} %param.11) | data formatting | bytes 1048576 | tf_op jit(solution)/shard_map/reshape;squeeze | solution.py:134
  2.2 0.1 copy.77
  2.4 0.8 pad_maximum_fusion
  3.2 10.3 %all-to-all-start = ((bf16[8,288,128]{2,1,0:T(8,128)(2,1)}), bf16[8,288,128]{2,1,0:T(8,128)(2,1)S(1)}, u32[]{:S(2)}, u32[]{:S(2)}) async-start(bf16[8,288,128]{2,1,0:T(8,128)(2,1)} %pad_maximum_fusion), calls=%async_computation | async-start | bytes 1179648 | tf_op jit(solution)/shard_map/all_to_all | solution.py:140
  13.6 5.7 %collective-permute-start = (bf16[1,128,2,1024]{3,2,1,0:T(2,128)(2,1)}, bf16[1,128,2,1024]{3,2,1,0:T(2,128)(2,1)}, u32[]{:S(2)}, u32[]{:S(2)}) collective-permute-start(bf16[1,128,2,1024]{3,2,1,0:T(2,128)(2,1)} %param.12), channel_id=1, source_target_pairs={{0,496},{16,0},{32,16},{48,32},{64,48},{80,64},{96,80},{112,96},{1... | collective-permute-start | bytes 1572872 | tf_op jit(solution)/shard_map/ppermute | solution.py:78
  19.3 7.9 %collective-permute-start.1 = (bf16[4,8192]{1,0:T(4,128)(2,1)S(1)}, bf16[4,8192]{1,0:T(4,128)(2,1)}, u32[]{:S(2)}, u32[]{:S(2)}) collective-permute-start(bf16[4,8192]{1,0:T(4,128)(2,1)S(1)} %bitcast.118), channel_id=1, source_target_pairs={{0,8},{8,0},{1,9},{9,1},{2,10},{10,2},{3,11},{11,3},{4,12},{12,4},... | collective-permute-start | bytes 196616 | tf_op jit(solution)/shard_map/ppermute | solution.py:78
  28.0 1.1 %copy.84 = bf16[1,1,256,2,1024]{2,4,3,1,0:T(8,128)(2,1)S(1)} copy(bf16[1,1,256,2,1024]{4,3,2,1,0:T(2,128)(2,1)S(1)} %copy-done.2) | data formatting | bytes 2097152 | tf_op args[2]
  29.1 0.6 copy-done.3
  29.8 0.3 fusion.32
  30.1 0.4 fusion.33
  30.7 0.9 copy_bitcast_fusion.2
  31.6 1.4 %reshape_squeeze.24 = bf16[128,2,8,128]{3,2,1,0:T(8,128)(2,1)S(1)} reshape(bf16[1,128,2,1024]{3,2,1,0:T(2,128)(2,1)} %collective-permute-done) | data formatting | bytes 1048576 | tf_op jit(solution)/shard_map/reshape;squeeze | solution.py:134
  33.0 0.1 copy.79
  33.1 0.8 pad_maximum_fusion.1
  34.0 7.4 %all-to-all-start.1 = ((bf16[8,288,128]{2,1,0:T(8,128)(2,1)}), bf16[8,288,128]{2,1,0:T(8,128)(2,1)S(1)}, u32[]{:S(2)}, u32[]{:S(2)}) async-start(bf16[8,288,128]{2,1,0:T(8,128)(2,1)} %pad_maximum_fusion.1), calls=%async_computation.1 | async-start | bytes 1179648 | tf_op jit(solution)/shard_map/all_to_all | solution.py:143
  41.4 0.2 fusion.7
  41.6 0.7 dynamic_slice.15
  42.3 1.2 %compare_select_fusion.bias_ref = f32[2,1024]{1,0:T(2,128)} fusion(s32[1,2,8,128]{3,2,1,0:T(8,128)S(1)} %broadcast_bitcast_fusion, s32[]{:T(128)} %bitcast.1, s32[1024]{0:T(1024)S(1)} %iota_bitcast_fusion), kind=kLoop, calls=%fused_computation.45 | loop fusion | flops 6144 | bytes 20484 | tf_op jit(solution)/shard_map/jit(_where)/select_n | solution.py:155
  43.5 0.3 fusion.21
  43.8 0.3 convolution_add_fusion.1
  44.1 13.2 %all-to-all-done.1.second_ref = bf16[8,288,128]{2,1,0:T(8,128)(2,1)S(1)} async-done(((bf16[8,288,128]{2,1,0:T(8,128)(2,1)}), bf16[8,288,128]{2,1,0:T(8,128)(2,1)S(1)}, u32[]{:S(2)}, u32[]{:S(2)}) %all-to-all-start.1) | async-done | bytes 589856 | tf_op jit(solution)/shard_map/all_to_all | solution.py:143
  57.3 0.8 reverse_select_fusion
  58.1 5.6 %shard_map.73 = f32[16,34,128]{2,1,0:T(8,128)} custom-call(f32[2,1024]{1,0:T(2,128)} %compare_select_fusion.bias_ref, bf16[512,128]{1,0:T(8,128)(2,1)} %bitcast.108, bf16[8,288,128]{2,1,0:T(8,128)(2,1)} %copy-done, bf16[8,288,128]{2,1,0:T(8,128)(2,1)} %copy-done.1), custom_call_target="tpu_custom_call" | custom-call | flops 201326592 | bytes 655360 | tf_op jit(solution)/shard_map/pallas_call | solution.py:58
  63.7 6.1 %all-to-all-start.2 = ((f32[16,34,128]{2,1,0:T(8,128)}), f32[16,34,128]{2,1,0:T(8,128)S(1)}, u32[]{:S(2)}, u32[]{:S(2)}) async-start(f32[16,34,128]{2,1,0:T(8,128)} %shard_map.73), calls=%async_computation.2 | async-start | bytes 655360 | tf_op jit(solution)/shard_map/all_to_all | solution.py:158
  69.8 0.1 fusion.25
  70.1 0.3 fusion.9
  70.4 0.3 fusion.3
  70.9 12.0 %all-to-all-done.2 = f32[16,34,128]{2,1,0:T(8,128)S(1)} async-done(((f32[16,34,128]{2,1,0:T(8,128)}), f32[16,34,128]{2,1,0:T(8,128)S(1)}, u32[]{:S(2)}, u32[]{:S(2)}) %all-to-all-start.2) | async-done | bytes 278560 | tf_op jit(solution)/shard_map/all_to_all | solution.py:158
  82.9 0.1 dynamic-slice_reduce_fusion.2
  83.3 0.1 dynamic-slice_reduce_fusion
  84.6 0.7 fusion.16
  (63 shorter events, 2.1 us)
Async XLA Ops:
  2.4 16.9 %copy-start.4 = (bf16[1,1,4,8192]{3,2,1,0:T(4,128)(2,1)S(1)}, bf16[1,1,4,8192]{3,2,1,0:T(4,128)(2,1)}, u32[]{:S(2)}) copy-start(bf16[1,1,4,8192]{3,2,1,0:T(4,128)(2,1)} %param.7) | copy-start | bytes 196612
  2.4 25.6 %copy-start.2 = (bf16[1,1,256,2,1024]{4,3,2,1,0:T(2,128)(2,1)S(1)}, bf16[1,1,256,2,1024]{4,3,2,1,0:T(2,128)(2,1)}, u32[]{:S(2)}) copy-start(bf16[1,1,256,2,1024]{4,3,2,1,0:T(2,128)(2,1)} %param.9) | copy-start | bytes 3145732
  3.2 30.7 %all-to-all-start = ((bf16[8,288,128]{2,1,0:T(8,128)(2,1)}), bf16[8,288,128]{2,1,0:T(8,128)(2,1)S(1)}, u32[]{:S(2)}, u32[]{:S(2)}) async-start(bf16[8,288,128]{2,1,0:T(8,128)(2,1)} %pad_maximum_fusion), calls=%async_computation | async-start | bytes 1179648 | tf_op jit(solution)/shard_map/all_to_all | solution.py:140
  13.6 18.0 %collective-permute-start = (bf16[1,128,2,1024]{3,2,1,0:T(2,128)(2,1)}, bf16[1,128,2,1024]{3,2,1,0:T(2,128)(2,1)}, u32[]{:S(2)}, u32[]{:S(2)}) collective-permute-start(bf16[1,128,2,1024]{3,2,1,0:T(2,128)(2,1)} %param.12), channel_id=1, source_target_pairs={{0,496},{16,0},{32,16},{48,32},{64,48},{80,64},{96,80},{112,96},{1... | collective-permute-start | bytes 1572872 | tf_op jit(solution)/shard_map/ppermute | solution.py:78
  19.3 11.4 %collective-permute-start.1 = (bf16[4,8192]{1,0:T(4,128)(2,1)S(1)}, bf16[4,8192]{1,0:T(4,128)(2,1)}, u32[]{:S(2)}, u32[]{:S(2)}) collective-permute-start(bf16[4,8192]{1,0:T(4,128)(2,1)S(1)} %bitcast.118), channel_id=1, source_target_pairs={{0,8},{8,0},{1,9},{9,1},{2,10},{10,2},{3,11},{11,3},{4,12},{12,4},... | collective-permute-start | bytes 196616 | tf_op jit(solution)/shard_map/ppermute | solution.py:78
  29.0 0.7 copy-start.3
  33.9 7.7 %copy-start.5 = (s32[32]{0:T(128)S(1)}, s32[32]{0:T(128)}, u32[]{:S(2)}) copy-start(s32[32]{0:T(128)} %param.13) | copy-start | bytes 388
  34.0 10.1 %copy-start = (bf16[8,288,128]{2,1,0:T(8,128)(2,1)}, bf16[8,288,128]{2,1,0:T(8,128)(2,1)S(1)}, u32[]{:S(2)}) copy-start(bf16[8,288,128]{2,1,0:T(8,128)(2,1)S(1)} %all-to-all-done.first_ref) | copy-start | bytes 1769476
  34.0 23.3 %all-to-all-start.1 = ((bf16[8,288,128]{2,1,0:T(8,128)(2,1)}), bf16[8,288,128]{2,1,0:T(8,128)(2,1)S(1)}, u32[]{:S(2)}, u32[]{:S(2)}) async-start(bf16[8,288,128]{2,1,0:T(8,128)(2,1)} %pad_maximum_fusion.1), calls=%async_computation.1 | async-start | bytes 1179648 | tf_op jit(solution)/shard_map/all_to_all | solution.py:143
  57.3 0.8 copy-start.1
  63.7 19.1 %all-to-all-start.2 = ((f32[16,34,128]{2,1,0:T(8,128)}), f32[16,34,128]{2,1,0:T(8,128)S(1)}, u32[]{:S(2)}, u32[]{:S(2)}) async-start(f32[16,34,128]{2,1,0:T(8,128)} %shard_map.73), calls=%async_computation.2 | async-start | bytes 655360 | tf_op jit(solution)/shard_map/all_to_all | solution.py:158

commit v7 on v6

--- a/solution.py
+++ b/solution.py
@@ -126,9 +126,7 @@
     step_count = queries.shape[2]
     rows_per_sample = step_count * GROUP
 
-    moved_tail = shifted(prefix_tail, "prompt", -1)
     own_rows = queries[0, 0]
-    partner_rows = shifted(own_rows, "zg", 1)
 
     def by_head(block):
         return block[0].reshape(block_len, 2, KVH, HEAD_SIZE).transpose(2, 1, 0, 3).reshape(KVH, 2 * block_len, HEAD_SIZE)
@@ -136,14 +134,15 @@
     def query_groups(rows):
         return rows.reshape(step_count, KVH, GROUP, HEAD_SIZE).transpose(1, 0, 2, 3).reshape(KVH, rows_per_sample, HEAD_SIZE)
 
+    moved_tail = shifted(by_head(prefix_tail), "prompt", -1)
     span = 2 * block_len
     first = lax.all_to_all(
         jnp.concatenate([by_head(prefix_head), query_groups(own_rows)], axis=1), ("zl", "core"), 0, 0, tiled=True
     )
-    second = lax.all_to_all(
-        jnp.concatenate([by_head(moved_tail), query_groups(partner_rows)], axis=1), ("zl", "core"), 0, 0, tiled=True
-    )
-    query_parts = jnp.stack([first[:, span:], second[:, span:]])
+    second = lax.all_to_all(moved_tail, ("zl", "core"), 0, 0, tiled=True)
+    team_queries = first[:, span:]
+    partner_queries = shifted(team_queries, "zg", 1)
+    query_parts = jnp.stack([team_queries, partner_queries])
     query_parts = jnp.where(team == 0, query_parts, query_parts[::-1])
     query_matrix = query_parts.reshape(2 * team_count * rows_per_sample, HEAD_SIZE)
 

time: 86 us -> 86 us (level)
  waiting for transfers between devices: 25.2 us -> 27 us
  other arithmetic: 4.89 us -> 3.89 us
    ppermute x2, waiting for transfers between devices: 0.01 us -> 15 us  [shifted(): return lax.ppermute(value, axis, pairs)]
    all_to_all x1, waiting for transfers between devices: 13.2 us -> 0.01 us  [per_device(): second = lax.all_to_all(moved_tail, ('zl', 'core'), 0, 0, tiled=True)]
    all_to_all x1, starting transfers between devices: 7.43 us -> 5.54 us  [per_device(): second = lax.all_to_all(moved_tail, ('zl', 'core'), 0, 0, tiled=True)]
    all_to_all x1, starting transfers between devices: 6.07 us -> 7.66 us  [per_device(): lax.all_to_all(outgoing_parts, ('zg', 'zl', 'core'), 0, 0, tiled=True)]
    unnamed x16 -> x18, local copies, waits for them, and re-layouts: 1.85 us -> 2.6 us
  transfers between devices with their start and end apart: 5 -> 5, of which waited for: 2 -> 3; matrix products, arithmetic and copies ran while one was open for 11% -> 9% of each run, Pallas kernels for 0% -> 0%
where the time goes in v7:
time: 86 us; the launch traced here: 85.4 us
  starting transfers between devices  37.2 us (43%)
  waiting for transfers between devices  27 us (31%)
  local copies, waits for them, and re-layouts  8.79 us (10%)
  Pallas kernels  5.57 us (6%)
  other arithmetic  3.89 us (5%)
  matrix products  1.92 us (2%)
  between operations  1.04 us (1%)
    ppermute x2, waiting for transfers between devices, shifted(): return lax.ppermute(value, axis, pairs)  15 us
    ppermute x2, starting transfers between devices, shifted(): return lax.ppermute(value, axis, pairs)  13.7 us
    all_to_all x1, waiting for transfers between devices, per_device(): lax.all_to_all(outgoing_parts, ('zg', 'zl', 'core'), 0, 0, tiled=True)  12 us
    all_to_all x1, starting transfers between devices, per_device(): lax.all_to_all(jnp.concatenate([by_head(prefix_head), query_groups(own_ro...  10.3 us
    all_to_all x1, starting transfers between devices, per_device(): lax.all_to_all(outgoing_parts, ('zg', 'zl', 'core'), 0, 0, tiled=True)  7.66 us
    pallas_call x1, Pallas kernels, prefix_attention(): pl.pallas_call(functools.partial(prefix_kernel, block), grid=(rows // ROW...  5.57 us
    all_to_all x1, starting transfers between devices, per_device(): second = lax.all_to_all(moved_tail, ('zl', 'core'), 0, 0, tiled=True)  5.54 us
    another operation x4, local copies, waits for them, and re-layouts, by_head(): block[0].reshape(block_len, 2, KVH, HEAD_SIZE).transpose(2, 1, 0, 3)  2.79 us
  transfers between devices with their start and end apart: 5, of which 3 were waited for; matrix products, arithmetic and copies ran while one was open for 9% of the time, Pallas kernels for 0%

profile of v7, /device:TPU:1, one launch (start us, length us, event | category | flops | bytes accessed | tf_op | source)
XLA Modules:
  0.0 85.4 jit_solution(3177395741745744979)
XLA Ops:
  0.0 0.8 copy_bitcast_fusion.1
  0.9 1.4 %reshape_squeeze.22 = bf16[128,2,8,128]{3,2,1,0:T(8,128)(2,1)S(1)} reshape(bf16[1,128,2,1024]{3,2,1,0:T(2,128)(2,1)} %param.11) | data formatting | bytes 1048576 | tf_op jit(solution)/shard_map/reshape;squeeze | solution.py:132
  2.2 0.1 copy.73
  2.4 0.8 pad_maximum_fusion
  3.2 10.3 %all-to-all-start = ((bf16[8,288,128]{2,1,0:T(8,128)(2,1)}), bf16[8,288,128]{2,1,0:T(8,128)(2,1)S(1)}, u32[]{:S(2)}, u32[]{:S(2)}) async-start(bf16[8,288,128]{2,1,0:T(8,128)(2,1)} %pad_maximum_fusion), calls=%async_computation | async-start | bytes 1179648 | tf_op jit(solution)/shard_map/all_to_all | solution.py:139
  13.6 0.3 reshape_squeeze.24
  13.9 0.9 %copy.75 = bf16[128,2,8,128]{3,0,1,2:T(8,128)(2,1)} copy(bf16[128,2,8,128]{3,2,1,0:T(8,128)(2,1)S(1)} %reshape_squeeze.24) | data formatting | bytes 1048576 | tf_op jit(solution)/shard_map/reshape;squeeze | solution.py:132
  14.8 5.7 %collective-permute-start.1 = (bf16[8,256,128]{2,1,0:T(8,128)(2,1)}, bf16[8,256,128]{2,1,0:T(8,128)(2,1)}, u32[]{:S(2)}, u32[]{:S(2)}) collective-permute-start(bf16[8,256,128]{2,1,0:T(8,128)(2,1)} %bitcast.10), channel_id=1, source_target_pairs={{0,496},{16,0},{32,16},{48,32},{64,48},{80,64},{96,80},{112,96},{1... | collective-permute-start | bytes 1572872 | tf_op jit(solution)/shard_map/ppermute | solution.py:78
  21.3 1.1 %copy.79 = bf16[1,1,256,2,1024]{2,4,3,1,0:T(8,128)(2,1)S(1)} copy(bf16[1,1,256,2,1024]{4,3,2,1,0:T(2,128)(2,1)S(1)} %copy-done.2) | data formatting | bytes 2097152 | tf_op args[2]
  22.5 0.6 copy-done.4
  23.2 0.3 fusion.32
  23.5 0.4 fusion.33
  23.9 0.6 dynamic_slice.15
  24.7 0.3 fusion.21
  24.9 0.3 convolution_add_fusion.1
  25.2 7.0 %collective-permute-done.1 = bf16[8,256,128]{2,1,0:T(8,128)(2,1)} collective-permute-done((bf16[8,256,128]{2,1,0:T(8,128)(2,1)}, bf16[8,256,128]{2,1,0:T(8,128)(2,1)}, u32[]{:S(2)}, u32[]{:S(2)}) %collective-permute-start.1) | collective-permute-done | bytes 524320 | tf_op jit(solution)/shard_map/ppermute | solution.py:78
  32.2 5.5 %all-to-all-start.1 = ((bf16[8,256,128]{2,1,0:T(8,128)(2,1)}), bf16[8,256,128]{2,1,0:T(8,128)(2,1)S(1)}, u32[]{:S(2)}, u32[]{:S(2)}) async-start(bf16[8,256,128]{2,1,0:T(8,128)(2,1)} %collective-permute-done.1), calls=%async_computation.1 | async-start | bytes 1048576 | tf_op jit(solution)/shard_map/all_to_all | solution.py:142
  37.8 1.1 %compare_select_fusion.bias_ref = f32[2,1024]{1,0:T(2,128)} fusion(s32[1,2,8,128]{3,2,1,0:T(8,128)S(1)} %broadcast_bitcast_fusion, s32[]{:T(128)} %bitcast.1, s32[1024]{0:T(1024)S(1)} %iota_bitcast_fusion), kind=kLoop, calls=%fused_computation.40 | loop fusion | flops 6144 | bytes 20484 | tf_op jit(solution)/shard_map/jit(_where)/select_n | solution.py:154
  38.9 7.9 %collective-permute-start = (bf16[8,32,128]{2,1,0:T(8,128)(2,1)S(1)}, bf16[8,32,128]{2,1,0:T(8,128)(2,1)S(1)}, u32[]{:S(2)}, u32[]{:S(2)}) collective-permute-start(bf16[8,32,128]{2,1,0:T(8,128)(2,1)S(1)} %get-tuple-element.14), channel_id=1, source_target_pairs={{0,8},{8,0},{1,9},{9,1},{2,10},{10,2},{3,11},{11,3},{4,12},{12,4},... | collective-permute-start | bytes 196616 | tf_op jit(solution)/shard_map/ppermute | solution.py:78
  46.9 0.2 fusion.7
  47.1 8.1 %collective-permute-done = bf16[8,32,128]{2,1,0:T(8,128)(2,1)S(1)} collective-permute-done((bf16[8,32,128]{2,1,0:T(8,128)(2,1)S(1)}, bf16[8,32,128]{2,1,0:T(8,128)(2,1)S(1)}, u32[]{:S(2)}, u32[]{:S(2)}) %collective-permute-start) | collective-permute-done | bytes 65568 | tf_op jit(solution)/shard_map/ppermute | solution.py:78
  55.2 0.7 reverse_select_fusion
  55.9 0.8 copy-done.1
  56.7 5.6 %shard_map.73 = f32[16,34,128]{2,1,0:T(8,128)} custom-call(f32[2,1024]{1,0:T(2,128)} %compare_select_fusion.bias_ref, bf16[512,128]{1,0:T(8,128)(2,1)} %bitcast.96, bf16[8,288,128]{2,1,0:T(8,128)(2,1)} %copy-done, bf16[8,256,128]{2,1,0:T(8,128)(2,1)} %copy-done.1), custom_call_target="tpu_custom_call" | custom-call | flops 201326592 | bytes 655360 | tf_op jit(solution)/shard_map/pallas_call | solution.py:58
  62.2 7.7 %all-to-all-start.2 = ((f32[16,34,128]{2,1,0:T(8,128)}), f32[16,34,128]{2,1,0:T(8,128)S(1)}, u32[]{:S(2)}, u32[]{:S(2)}) async-start(f32[16,34,128]{2,1,0:T(8,128)} %shard_map.73), calls=%async_computation.2 | async-start | bytes 655360 | tf_op jit(solution)/shard_map/all_to_all | solution.py:157
  69.9 0.1 fusion.25
  70.2 0.3 fusion.9
  70.5 0.3 fusion.3
  71.0 12.0 %all-to-all-done.2 = f32[16,34,128]{2,1,0:T(8,128)S(1)} async-done(((f32[16,34,128]{2,1,0:T(8,128)}), f32[16,34,128]{2,1,0:T(8,128)S(1)}, u32[]{:S(2)}, u32[]{:S(2)}) %all-to-all-start.2) | async-done | bytes 278560 | tf_op jit(solution)/shard_map/all_to_all | solution.py:157
  83.0 0.1 dynamic-slice_reduce_fusion.2
  83.4 0.1 dynamic-slice_reduce_fusion
  84.7 0.7 fusion.16
  (62 shorter events, 2.1 us)
Async XLA Ops:
  2.4 11.2 %copy-start.3 = (bf16[1,128,2,1024]{3,2,1,0:T(2,128)(2,1)S(1)}, bf16[1,128,2,1024]{3,2,1,0:T(2,128)(2,1)}, u32[]{:S(2)}) copy-start(bf16[1,128,2,1024]{3,2,1,0:T(2,128)(2,1)} %param.12) | copy-start | bytes 1572868
  3.2 29.0 %all-to-all-start = ((bf16[8,288,128]{2,1,0:T(8,128)(2,1)}), bf16[8,288,128]{2,1,0:T(8,128)(2,1)S(1)}, u32[]{:S(2)}, u32[]{:S(2)}) async-start(bf16[8,288,128]{2,1,0:T(8,128)(2,1)} %pad_maximum_fusion), calls=%async_computation | async-start | bytes 1179648 | tf_op jit(solution)/shard_map/all_to_all | solution.py:139
  13.6 7.7 %copy-start.2 = (bf16[1,1,256,2,1024]{4,3,2,1,0:T(2,128)(2,1)S(1)}, bf16[1,1,256,2,1024]{4,3,2,1,0:T(2,128)(2,1)}, u32[]{:S(2)}) copy-start(bf16[1,1,256,2,1024]{4,3,2,1,0:T(2,128)(2,1)} %param.9) | copy-start | bytes 3145732
  14.8 17.4 %collective-permute-start.1 = (bf16[8,256,128]{2,1,0:T(8,128)(2,1)}, bf16[8,256,128]{2,1,0:T(8,128)(2,1)}, u32[]{:S(2)}, u32[]{:S(2)}) collective-permute-start(bf16[8,256,128]{2,1,0:T(8,128)(2,1)} %bitcast.10), channel_id=1, source_target_pairs={{0,496},{16,0},{32,16},{48,32},{64,48},{80,64},{96,80},{112,96},{1... | collective-permute-start | bytes 1572872 | tf_op jit(solution)/shard_map/ppermute | solution.py:78
  22.3 0.7 copy-start.4
  22.4 0.8 copy-start.5
  22.4 1.5 %copy-start.6 = (s32[32]{0:T(128)S(1)}, s32[32]{0:T(128)}, u32[]{:S(2)}) copy-start(s32[32]{0:T(128)} %param.13) | copy-start | bytes 388
  32.2 23.6 %copy-start = (bf16[8,288,128]{2,1,0:T(8,128)(2,1)}, bf16[8,288,128]{2,1,0:T(8,128)(2,1)S(1)}, u32[]{:S(2)}) copy-start(bf16[8,288,128]{2,1,0:T(8,128)(2,1)S(1)} %all-to-all-done.first_ref) | copy-start | bytes 1769476
  32.2 23.7 %all-to-all-start.1 = ((bf16[8,256,128]{2,1,0:T(8,128)(2,1)}), bf16[8,256,128]{2,1,0:T(8,128)(2,1)S(1)}, u32[]{:S(2)}, u32[]{:S(2)}) async-start(bf16[8,256,128]{2,1,0:T(8,128)(2,1)} %collective-permute-done.1), calls=%async_computation.1 | async-start | bytes 1048576 | tf_op jit(solution)/shard_map/all_to_all | solution.py:142
  38.9 16.2 %collective-permute-start = (bf16[8,32,128]{2,1,0:T(8,128)(2,1)S(1)}, bf16[8,32,128]{2,1,0:T(8,128)(2,1)S(1)}, u32[]{:S(2)}, u32[]{:S(2)}) collective-permute-start(bf16[8,32,128]{2,1,0:T(8,128)(2,1)S(1)} %get-tuple-element.14), channel_id=1, source_target_pairs={{0,8},{8,0},{1,9},{9,1},{2,10},{10,2},{3,11},{11,3},{4,12},{12,4},... | collective-permute-start | bytes 196616 | tf_op jit(solution)/shard_map/ppermute | solution.py:78
  55.9 0.8 copy-start.1
  62.2 20.7 %all-to-all-start.2 = ((f32[16,34,128]{2,1,0:T(8,128)}), f32[16,34,128]{2,1,0:T(8,128)S(1)}, u32[]{:S(2)}, u32[]{:S(2)}) async-start(f32[16,34,128]{2,1,0:T(8,128)} %shard_map.73), calls=%async_computation.2 | async-start | bytes 655360 | tf_op jit(solution)/shard_map/all_to_all | solution.py:157

commit v8 on v6

--- a/solution.py
+++ b/solution.py
@@ -126,7 +126,6 @@
     step_count = queries.shape[2]
     rows_per_sample = step_count * GROUP
 
-    moved_tail = shifted(prefix_tail, "prompt", -1)
     own_rows = queries[0, 0]
     partner_rows = shifted(own_rows, "zg", 1)
 
@@ -136,12 +135,13 @@
     def query_groups(rows):
         return rows.reshape(step_count, KVH, GROUP, HEAD_SIZE).transpose(1, 0, 2, 3).reshape(KVH, rows_per_sample, HEAD_SIZE)
 
+    moved_tail = shifted(by_head(prefix_tail), "prompt", -1)
     span = 2 * block_len
     first = lax.all_to_all(
         jnp.concatenate([by_head(prefix_head), query_groups(own_rows)], axis=1), ("zl", "core"), 0, 0, tiled=True
     )
     second = lax.all_to_all(
-        jnp.concatenate([by_head(moved_tail), query_groups(partner_rows)], axis=1), ("zl", "core"), 0, 0, tiled=True
+        jnp.concatenate([moved_tail, query_groups(partner_rows)], axis=1), ("zl", "core"), 0, 0, tiled=True
     )
     query_parts = jnp.stack([first[:, span:], second[:, span:]])
     query_parts = jnp.where(team == 0, query_parts, query_parts[::-1])

time: 86 us -> 86.8 us (level)
  other arithmetic: 4.89 us -> 5.93 us
    concatenate x1, other arithmetic: 0.85 us -> 1.89 us  [per_device(): jnp.concatenate([moved_tail, query_groups(partner_rows)], axis=1)]
    unnamed x16 -> x18, local copies, waits for them, and re-layouts: 1.85 us -> 1.85 us
where the time goes in v8:
time: 86.8 us; the launch traced here: 86.1 us
  starting transfers between devices  37.5 us (43%)
  waiting for transfers between devices  25.2 us (29%)
  local copies, waits for them, and re-layouts  8.95 us (10%)
  other arithmetic  5.93 us (7%)
  Pallas kernels  5.58 us (6%)
  matrix products  1.91 us (2%)
  between operations  1.07 us (1%)
    ppermute x2, starting transfers between devices, shifted(): return lax.ppermute(value, axis, pairs)  13.7 us
    all_to_all x1, waiting for transfers between devices, per_device(): lax.all_to_all(jnp.concatenate([moved_tail, query_groups(partner_rows)],...  13.2 us
    all_to_all x1, waiting for transfers between devices, per_device(): lax.all_to_all(outgoing_parts, ('zg', 'zl', 'core'), 0, 0, tiled=True)  12 us
    all_to_all x1, starting transfers between devices, per_device(): lax.all_to_all(jnp.concatenate([by_head(prefix_head), query_groups(own_ro...  10.3 us
    all_to_all x1, starting transfers between devices, per_device(): lax.all_to_all(jnp.concatenate([moved_tail, query_groups(partner_rows)],...  6.91 us
    all_to_all x1, starting transfers between devices, per_device(): lax.all_to_all(outgoing_parts, ('zg', 'zl', 'core'), 0, 0, tiled=True)  6.59 us
    pallas_call x1, Pallas kernels, prefix_attention(): pl.pallas_call(functools.partial(prefix_kernel, block), grid=(rows // ROW...  5.58 us
    another operation x4, local copies, waits for them, and re-layouts, by_head(): block[0].reshape(block_len, 2, KVH, HEAD_SIZE).transpose(2, 1, 0, 3)  2.77 us
  transfers between devices with their start and end apart: 5, of which 2 were waited for; matrix products, arithmetic and copies ran while one was open for 11% of the time, Pallas kernels for 0%

profile of v8, /device:TPU:1, one launch (start us, length us, event | category | flops | bytes accessed | tf_op | source)
XLA Modules:
  0.0 86.1 jit_solution(15637692736928621757)
XLA Ops:
  0.0 0.8 copy_bitcast_fusion.3
  0.9 1.4 %reshape_squeeze.22 = bf16[128,2,8,128]{3,2,1,0:T(8,128)(2,1)S(1)} reshape(bf16[1,128,2,1024]{3,2,1,0:T(2,128)(2,1)} %param.11) | data formatting | bytes 1048576 | tf_op jit(solution)/shard_map/reshape;squeeze | solution.py:133
  2.2 0.1 copy.77
  2.4 0.8 pad_maximum_fusion
  3.2 10.3 %all-to-all-start = ((bf16[8,288,128]{2,1,0:T(8,128)(2,1)}), bf16[8,288,128]{2,1,0:T(8,128)(2,1)S(1)}, u32[]{:S(2)}, u32[]{:S(2)}) async-start(bf16[8,288,128]{2,1,0:T(8,128)(2,1)} %pad_maximum_fusion), calls=%async_computation | async-start | bytes 1179648 | tf_op jit(solution)/shard_map/all_to_all | solution.py:140
  13.6 0.3 reshape_squeeze.24
  13.9 0.9 %copy.79 = bf16[128,2,8,128]{3,0,1,2:T(8,128)(2,1)} copy(bf16[128,2,8,128]{3,2,1,0:T(8,128)(2,1)S(1)} %reshape_squeeze.24) | data formatting | bytes 1048576 | tf_op jit(solution)/shard_map/reshape;squeeze | solution.py:133
  14.8 5.7 %collective-permute-start = (bf16[8,256,128]{2,1,0:T(8,128)(2,1)}, bf16[8,256,128]{2,1,0:T(8,128)(2,1)}, u32[]{:S(2)}, u32[]{:S(2)}) collective-permute-start(bf16[8,256,128]{2,1,0:T(8,128)(2,1)} %bitcast.8), channel_id=1, source_target_pairs={{0,496},{16,0},{32,16},{48,32},{64,48},{80,64},{96,80},{112,96},{1... | collective-permute-start | bytes 1572872 | tf_op jit(solution)/shard_map/ppermute | solution.py:78
  20.6 7.9 %collective-permute-start.1 = (bf16[4,8192]{1,0:T(4,128)(2,1)S(1)}, bf16[4,8192]{1,0:T(4,128)(2,1)}, u32[]{:S(2)}, u32[]{:S(2)}) collective-permute-start(bf16[4,8192]{1,0:T(4,128)(2,1)S(1)} %bitcast.117), channel_id=1, source_target_pairs={{0,8},{8,0},{1,9},{9,1},{2,10},{10,2},{3,11},{11,3},{4,12},{12,4},... | collective-permute-start | bytes 196616 | tf_op jit(solution)/shard_map/ppermute | solution.py:78
  29.2 1.1 %copy.84 = bf16[1,1,256,2,1024]{2,4,3,1,0:T(8,128)(2,1)S(1)} copy(bf16[1,1,256,2,1024]{4,3,2,1,0:T(2,128)(2,1)S(1)} %copy-done.2) | data formatting | bytes 2097152 | tf_op args[2]
  30.4 0.6 copy-done.4
  31.1 0.3 fusion.32
  31.4 0.4 fusion.33
  32.0 0.9 copy_bitcast_fusion.2
  32.8 1.9 %pad_maximum_fusion.1 = bf16[8,288,128]{2,1,0:T(8,128)(2,1)} fusion(bf16[8,32,128]{2,1,0:T(8,128)(2,1)S(1)} %copy_bitcast_fusion.2, bf16[8,256,128]{2,1,0:T(8,128)(2,1)} %collective-permute-done), kind=kLoop, calls=%fused_computation.11 | loop fusion | flops 1179648 | bytes 1179648 | tf_op jit(solution)/shard_map/concatenate | solution.py:144
  34.7 6.9 %all-to-all-start.1 = ((bf16[8,288,128]{2,1,0:T(8,128)(2,1)}), bf16[8,288,128]{2,1,0:T(8,128)(2,1)S(1)}, u32[]{:S(2)}, u32[]{:S(2)}) async-start(bf16[8,288,128]{2,1,0:T(8,128)(2,1)} %pad_maximum_fusion.1), calls=%async_computation.1 | async-start | bytes 1179648 | tf_op jit(solution)/shard_map/all_to_all | solution.py:143
  41.7 0.2 fusion.7
  41.9 0.7 dynamic_slice.15
  42.6 1.2 %compare_select_fusion.bias_ref = f32[2,1024]{1,0:T(2,128)} fusion(s32[1,2,8,128]{3,2,1,0:T(8,128)S(1)} %broadcast_bitcast_fusion, s32[]{:T(128)} %bitcast.1, s32[1024]{0:T(1024)S(1)} %iota_bitcast_fusion), kind=kLoop, calls=%fused_computation.45 | loop fusion | flops 6144 | bytes 20484 | tf_op jit(solution)/shard_map/jit(_where)/select_n | solution.py:155
  43.8 0.3 fusion.21
  44.1 0.3 convolution_add_fusion.1
  44.4 13.2 %all-to-all-done.1.second_ref = bf16[8,288,128]{2,1,0:T(8,128)(2,1)S(1)} async-done(((bf16[8,288,128]{2,1,0:T(8,128)(2,1)}), bf16[8,288,128]{2,1,0:T(8,128)(2,1)S(1)}, u32[]{:S(2)}, u32[]{:S(2)}) %all-to-all-start.1) | async-done | bytes 589856 | tf_op jit(solution)/shard_map/all_to_all | solution.py:143
  57.6 0.8 reverse_select_fusion
  58.4 5.6 %shard_map.73 = f32[16,34,128]{2,1,0:T(8,128)} custom-call(f32[2,1024]{1,0:T(2,128)} %compare_select_fusion.bias_ref, bf16[512,128]{1,0:T(8,128)(2,1)} %bitcast.107, bf16[8,288,128]{2,1,0:T(8,128)(2,1)} %copy-done, bf16[8,288,128]{2,1,0:T(8,128)(2,1)} %copy-done.1), custom_call_target="tpu_custom_call" | custom-call | flops 201326592 | bytes 655360 | tf_op jit(solution)/shard_map/pallas_call | solution.py:58
  64.0 6.6 %all-to-all-start.2 = ((f32[16,34,128]{2,1,0:T(8,128)}), f32[16,34,128]{2,1,0:T(8,128)S(1)}, u32[]{:S(2)}, u32[]{:S(2)}) async-start(f32[16,34,128]{2,1,0:T(8,128)} %shard_map.73), calls=%async_computation.2 | async-start | bytes 655360 | tf_op jit(solution)/shard_map/all_to_all | solution.py:158
  70.6 0.1 fusion.25
  70.9 0.3 fusion.9
  71.2 0.3 fusion.3
  71.7 12.0 %all-to-all-done.2 = f32[16,34,128]{2,1,0:T(8,128)S(1)} async-done(((f32[16,34,128]{2,1,0:T(8,128)}), f32[16,34,128]{2,1,0:T(8,128)S(1)}, u32[]{:S(2)}, u32[]{:S(2)}) %all-to-all-start.2) | async-done | bytes 278560 | tf_op jit(solution)/shard_map/all_to_all | solution.py:158
  83.7 0.1 dynamic-slice_reduce_fusion.2
  84.1 0.1 dynamic-slice_reduce_fusion
  85.4 0.7 fusion.16
  (65 shorter events, 2.1 us)
Async XLA Ops:
  2.4 11.2 %copy-start.3 = (bf16[1,128,2,1024]{3,2,1,0:T(2,128)(2,1)S(1)}, bf16[1,128,2,1024]{3,2,1,0:T(2,128)(2,1)}, u32[]{:S(2)}) copy-start(bf16[1,128,2,1024]{3,2,1,0:T(2,128)(2,1)} %param.12) | copy-start | bytes 1572868
  3.2 31.5 %all-to-all-start = ((bf16[8,288,128]{2,1,0:T(8,128)(2,1)}), bf16[8,288,128]{2,1,0:T(8,128)(2,1)S(1)}, u32[]{:S(2)}, u32[]{:S(2)}) async-start(bf16[8,288,128]{2,1,0:T(8,128)(2,1)} %pad_maximum_fusion), calls=%async_computation | async-start | bytes 1179648 | tf_op jit(solution)/shard_map/all_to_all | solution.py:140
  13.6 7.0 %copy-start.5 = (bf16[1,1,4,8192]{3,2,1,0:T(4,128)(2,1)S(1)}, bf16[1,1,4,8192]{3,2,1,0:T(4,128)(2,1)}, u32[]{:S(2)}) copy-start(bf16[1,1,4,8192]{3,2,1,0:T(4,128)(2,1)} %param.7) | copy-start | bytes 196612
  13.6 15.7 %copy-start.2 = (bf16[1,1,256,2,1024]{4,3,2,1,0:T(2,128)(2,1)S(1)}, bf16[1,1,256,2,1024]{4,3,2,1,0:T(2,128)(2,1)}, u32[]{:S(2)}) copy-start(bf16[1,1,256,2,1024]{4,3,2,1,0:T(2,128)(2,1)} %param.9) | copy-start | bytes 3145732
  14.8 18.0 %collective-permute-start = (bf16[8,256,128]{2,1,0:T(8,128)(2,1)}, bf16[8,256,128]{2,1,0:T(8,128)(2,1)}, u32[]{:S(2)}, u32[]{:S(2)}) collective-permute-start(bf16[8,256,128]{2,1,0:T(8,128)(2,1)} %bitcast.8), channel_id=1, source_target_pairs={{0,496},{16,0},{32,16},{48,32},{64,48},{80,64},{96,80},{112,96},{1... | collective-permute-start | bytes 1572872 | tf_op jit(solution)/shard_map/ppermute | solution.py:78
  20.6 11.4 %collective-permute-start.1 = (bf16[4,8192]{1,0:T(4,128)(2,1)S(1)}, bf16[4,8192]{1,0:T(4,128)(2,1)}, u32[]{:S(2)}, u32[]{:S(2)}) collective-permute-start(bf16[4,8192]{1,0:T(4,128)(2,1)S(1)} %bitcast.117), channel_id=1, source_target_pairs={{0,8},{8,0},{1,9},{9,1},{2,10},{10,2},{3,11},{11,3},{4,12},{12,4},... | collective-permute-start | bytes 196616 | tf_op jit(solution)/shard_map/ppermute | solution.py:78
  30.3 0.7 copy-start.4
  34.7 7.2 %copy-start.6 = (s32[32]{0:T(128)S(1)}, s32[32]{0:T(128)}, u32[]{:S(2)}) copy-start(s32[32]{0:T(128)} %param.13) | copy-start | bytes 388
  34.7 9.6 %copy-start = (bf16[8,288,128]{2,1,0:T(8,128)(2,1)}, bf16[8,288,128]{2,1,0:T(8,128)(2,1)S(1)}, u32[]{:S(2)}) copy-start(bf16[8,288,128]{2,1,0:T(8,128)(2,1)S(1)} %all-to-all-done.first_ref) | copy-start | bytes 1769476
  34.7 22.8 %all-to-all-start.1 = ((bf16[8,288,128]{2,1,0:T(8,128)(2,1)}), bf16[8,288,128]{2,1,0:T(8,128)(2,1)S(1)}, u32[]{:S(2)}, u32[]{:S(2)}) async-start(bf16[8,288,128]{2,1,0:T(8,128)(2,1)} %pad_maximum_fusion.1), calls=%async_computation.1 | async-start | bytes 1179648 | tf_op jit(solution)/shard_map/all_to_all | solution.py:143
  57.6 0.8 copy-start.1
  64.0 19.7 %all-to-all-start.2 = ((f32[16,34,128]{2,1,0:T(8,128)}), f32[16,34,128]{2,1,0:T(8,128)S(1)}, u32[]{:S(2)}, u32[]{:S(2)}) async-start(f32[16,34,128]{2,1,0:T(8,128)} %shard_map.73), calls=%async_computation.2 | async-start | bytes 655360 | tf_op jit(solution)/shard_map/all_to_all | solution.py:158

commit v9 on v6

--- a/solution.py
+++ b/solution.py
@@ -4,6 +4,7 @@
 import jax.numpy as jnp
 from jax import lax
 from jax.experimental import pallas as pl
+from jax.experimental.pallas import tpu as pltpu
 from jax.sharding import PartitionSpec as P
 
 QH = 64
@@ -16,16 +17,24 @@
 ROW_BLOCK = 128
 
 
-def prefix_kernel(block, bias_ref, query_ref, first_ref, second_ref, out_ref):
-    query = query_ref[...]
+def prefix_kernel(block, team_ref, bias_ref, first_ref, second_ref, out_ref):
+    samples, rows, width = out_ref.shape
+    rows = rows - 2
     members = first_ref.shape[0]
+    blocks_per_team = members // samples
+    index = pl.program_id(0)
+    start = (index % blocks_per_team) * samples
+    from_first = index // blocks_per_team == team_ref[0]
+    first_rows = first_ref[pl.ds(start, samples), 2 * block :, :]
+    second_rows = second_ref[pl.ds(start, samples), 2 * block :, :]
+    query = jnp.where(from_first, first_rows, second_rows).reshape(samples * rows, width)
     parts = []
-    for index, source in enumerate((first_ref, second_ref)):
+    for which, source in enumerate((first_ref, second_ref)):
         keys = source[:, :block, :].reshape(members * block, HEAD_SIZE)
         values = source[:, block : 2 * block, :].reshape(members * block, HEAD_SIZE)
         scores = lax.dot_general(
             query, keys, (((1,), (1,)), ((), ())), preferred_element_type=jnp.float32
-        ) * HEAD_SIZE ** (-0.5) + bias_ref[index : index + 1, :]
+        ) * HEAD_SIZE ** (-0.5) + bias_ref[which : which + 1, :]
         parts.append((scores, values))
     maxima = jnp.maximum(
         jnp.max(parts[0][0], axis=1, keepdims=True), jnp.max(parts[1][0], axis=1, keepdims=True)
@@ -42,8 +51,6 @@
         )
         numer = part if numer is None else numer + part
         totals = part_total if totals is None else totals + part_total
-    samples, rows, width = out_ref.shape
-    rows = rows - 2
     out_ref[:, :rows, :] = numer.reshape(samples, rows, width)
     max_row = jnp.transpose(jnp.broadcast_to(maxima, (ROW_BLOCK, ROW_BLOCK)))[0:1, :]
     total_row = jnp.transpose(jnp.broadcast_to(totals, (ROW_BLOCK, ROW_BLOCK)))[0:1, :]
@@ -51,16 +58,17 @@
     out_ref[:, rows + 1 : rows + 2, :] = jnp.broadcast_to(total_row[None], (samples, 1, width))
 
 
-def prefix_attention(bias, query_matrix, first, second, block, rows_per_sample):
-    rows, width = query_matrix.shape
+def prefix_attention(team, bias, first, second, block, rows_per_sample):
+    width = first.shape[2]
+    rows = 2 * first.shape[0] * rows_per_sample
     span = first.shape[0] * block
     per_block = ROW_BLOCK // rows_per_sample
     return pl.pallas_call(
         functools.partial(prefix_kernel, block),
         grid=(rows // ROW_BLOCK,),
         in_specs=[
+            pl.BlockSpec(memory_space=pltpu.SMEM),
             pl.BlockSpec(bias.shape, lambda i: (0, 0)),
-            pl.BlockSpec((ROW_BLOCK, width), lambda i: (i, 0)),
             pl.BlockSpec(first.shape, lambda i: (0, 0, 0)),
             pl.BlockSpec(second.shape, lambda i: (0, 0, 0)),
         ],
@@ -69,7 +77,7 @@
         cost_estimate=pl.CostEstimate(
             flops=3 * rows * span * width, transcendentals=rows * span // 2, bytes_accessed=2 * (rows + span) * width + 4 * rows * width
         ),
-    )(bias, query_matrix, first, second)
+    )(team, bias, first, second)
 
 
 def shifted(value, axis, steps):
@@ -143,9 +151,6 @@
     second = lax.all_to_all(
         jnp.concatenate([by_head(moved_tail), query_groups(partner_rows)], axis=1), ("zl", "core"), 0, 0, tiled=True
     )
-    query_parts = jnp.stack([first[:, span:], second[:, span:]])
-    query_parts = jnp.where(team == 0, query_parts, query_parts[::-1])
-    query_matrix = query_parts.reshape(2 * team_count * rows_per_sample, HEAD_SIZE)
 
     member = jnp.arange(team_count, dtype=jnp.int32)[None, :, None]
     half = jnp.arange(2, dtype=jnp.int32)[:, None, None]
@@ -154,7 +159,7 @@
     positions = half * prefix_half_len + (team * team_count + member) * block_len + offset
     bias = jnp.where(positions.reshape(2, -1) < prefix_len[prompt_row], 0.0, NEG).astype(jnp.float32)
     sample_count = 2 * team_count
-    outgoing_parts = prefix_attention(bias, query_matrix, first, second, block_len, rows_per_sample)
+    outgoing_parts = prefix_attention(team.reshape(1), bias, first, second, block_len, rows_per_sample)
     returned = lax.all_to_all(outgoing_parts, ("zg", "zl", "core"), 0, 0, tiled=True)
     returned = returned.reshape(2, KVH, rows_per_sample + 2, HEAD_SIZE)
     lane_offset = (lax.axis_index(("zg", "zl", "core")) % (ROW_BLOCK // rows_per_sample)) * rows_per_sample

time: 86 us -> 85.9 us (level)
  no operation moved by 1% of the time
where the time goes in v9:
time: 85.9 us; the launch traced here: 85.2 us
  starting transfers between devices  37.6 us (44%)
  waiting for transfers between devices  25.1 us (29%)
  local copies, waits for them, and re-layouts  9.94 us (12%)
  Pallas kernels  5.51 us (6%)
  other arithmetic  4.12 us (5%)
  matrix products  1.91 us (2%)
  between operations  1.05 us (1%)
    ppermute x2, starting transfers between devices, shifted(): return lax.ppermute(value, axis, pairs)  13.7 us
    all_to_all x1, waiting for transfers between devices, per_device(): lax.all_to_all(jnp.concatenate([by_head(moved_tail), query_groups(partner...  13.1 us
    all_to_all x1, waiting for transfers between devices, per_device(): lax.all_to_all(outgoing_parts, ('zg', 'zl', 'core'), 0, 0, tiled=True)  12 us
    all_to_all x1, starting transfers between devices, per_device(): lax.all_to_all(jnp.concatenate([by_head(prefix_head), query_groups(own_ro...  10.3 us
    all_to_all x1, starting transfers between devices, per_device(): lax.all_to_all(jnp.concatenate([by_head(moved_tail), query_groups(partner...  7.51 us
    all_to_all x1, starting transfers between devices, per_device(): lax.all_to_all(outgoing_parts, ('zg', 'zl', 'core'), 0, 0, tiled=True)  6.07 us
    pallas_call x1, Pallas kernels, prefix_attention(): pl.pallas_call(functools.partial(prefix_kernel, block), grid=(rows // ROW...  5.51 us
    another operation x4, local copies, waits for them, and re-layouts, by_head(): block[0].reshape(block_len, 2, KVH, HEAD_SIZE).transpose(2, 1, 0, 3)  3.02 us
  transfers between devices with their start and end apart: 5, of which 2 were waited for; matrix products, arithmetic and copies ran while one was open for 11% of the time, Pallas kernels for 0%

profile of v9, /device:TPU:1, one launch (start us, length us, event | category | flops | bytes accessed | tf_op | source)
XLA Modules:
  0.0 85.2 jit_solution(12296525464280707995)
XLA Ops:
  0.0 0.8 copy_bitcast_fusion.3
  0.9 1.4 %reshape_squeeze.22 = bf16[128,2,8,128]{3,2,1,0:T(8,128)(2,1)S(1)} reshape(bf16[1,128,2,1024]{3,2,1,0:T(2,128)(2,1)} %param.11) | data formatting | bytes 1048576 | tf_op jit(solution)/shard_map/reshape;squeeze | solution.py:142
  2.2 0.1 copy.77
  2.4 0.8 pad_maximum_fusion
  3.2 10.3 %all-to-all-start = ((bf16[8,288,128]{2,1,0:T(8,128)(2,1)}), bf16[8,288,128]{2,1,0:T(8,128)(2,1)S(1)}, u32[]{:S(2)}, u32[]{:S(2)}) async-start(bf16[8,288,128]{2,1,0:T(8,128)(2,1)} %pad_maximum_fusion), calls=%async_computation | async-start | bytes 1179648 | tf_op jit(solution)/shard_map/all_to_all | solution.py:148
  13.6 5.7 %collective-permute-start = (bf16[1,128,2,1024]{3,2,1,0:T(2,128)(2,1)}, bf16[1,128,2,1024]{3,2,1,0:T(2,128)(2,1)}, u32[]{:S(2)}, u32[]{:S(2)}) collective-permute-start(bf16[1,128,2,1024]{3,2,1,0:T(2,128)(2,1)} %param.12), channel_id=1, source_target_pairs={{0,496},{16,0},{32,16},{48,32},{64,48},{80,64},{96,80},{112,96},{1... | collective-permute-start | bytes 1572872 | tf_op jit(solution)/shard_map/ppermute | solution.py:86
  19.3 7.9 %collective-permute-start.1 = (bf16[4,8192]{1,0:T(4,128)(2,1)S(1)}, bf16[4,8192]{1,0:T(4,128)(2,1)}, u32[]{:S(2)}, u32[]{:S(2)}) collective-permute-start(bf16[4,8192]{1,0:T(4,128)(2,1)S(1)} %bitcast.113), channel_id=1, source_target_pairs={{0,8},{8,0},{1,9},{9,1},{2,10},{10,2},{3,11},{11,3},{4,12},{12,4},... | collective-permute-start | bytes 196616 | tf_op jit(solution)/shard_map/ppermute | solution.py:86
  28.0 1.1 %copy.84 = bf16[1,1,256,2,1024]{2,4,3,1,0:T(8,128)(2,1)S(1)} copy(bf16[1,1,256,2,1024]{4,3,2,1,0:T(2,128)(2,1)S(1)} %copy-done.2) | data formatting | bytes 2097152 | tf_op args[2]
  29.1 0.6 copy-done.3
  29.8 0.4 fusion.33
  30.3 0.3 fusion.32
  30.6 0.9 copy_bitcast_fusion.2
  31.5 1.4 %reshape_squeeze.24 = bf16[128,2,8,128]{3,2,1,0:T(8,128)(2,1)S(1)} reshape(bf16[1,128,2,1024]{3,2,1,0:T(2,128)(2,1)} %collective-permute-done) | data formatting | bytes 1048576 | tf_op jit(solution)/shard_map/reshape;squeeze | solution.py:142
  32.9 0.1 copy.79
  33.0 0.8 pad_maximum_fusion.1
  33.9 7.5 %all-to-all-start.1 = ((bf16[8,288,128]{2,1,0:T(8,128)(2,1)}), bf16[8,288,128]{2,1,0:T(8,128)(2,1)S(1)}, u32[]{:S(2)}, u32[]{:S(2)}) async-start(bf16[8,288,128]{2,1,0:T(8,128)(2,1)} %pad_maximum_fusion.1), calls=%async_computation.1 | async-start | bytes 1179648 | tf_op jit(solution)/shard_map/all_to_all | solution.py:151
  41.4 0.2 fusion.7
  41.6 0.7 dynamic_slice.15
  42.4 1.2 %compare_select_fusion.bias_ref = f32[2,1024]{1,0:T(2,128)} fusion(s32[1,2,8,128]{3,2,1,0:T(8,128)S(1)} %broadcast_bitcast_fusion, s32[]{:T(128)} %bitcast.2, s32[1024]{0:T(1024)S(1)} %iota_bitcast_fusion), kind=kLoop, calls=%fused_computation.41 | loop fusion | flops 6144 | bytes 20484 | tf_op jit(solution)/shard_map/jit(_where)/select_n | solution.py:160
  43.6 0.3 fusion.21
  43.9 0.3 convolution_add_fusion.1
  44.2 13.1 %all-to-all-done.1.second_ref = bf16[8,288,128]{2,1,0:T(8,128)(2,1)S(1)} async-done(((bf16[8,288,128]{2,1,0:T(8,128)(2,1)}), bf16[8,288,128]{2,1,0:T(8,128)(2,1)S(1)}, u32[]{:S(2)}, u32[]{:S(2)}) %all-to-all-start.1) | async-done | bytes 589856 | tf_op jit(solution)/shard_map/all_to_all | solution.py:151
  57.3 0.8 copy-done.1
  58.1 5.5 %shard_map.73 = f32[16,34,128]{2,1,0:T(8,128)} custom-call(s32[1]{0:T(128)} %bitcast.team_ref, f32[2,1024]{1,0:T(2,128)} %compare_select_fusion.bias_ref, bf16[8,288,128]{2,1,0:T(8,128)(2,1)} %copy-done, bf16[8,288,128]{2,1,0:T(8,128)(2,1)} %copy-done.1), custom_call_target="tpu_custom_call" | custom-call | flops 201326592 | bytes 655360 | tf_op jit(solution)/shard_map/pallas_call | solution.py:66
  63.6 6.1 %all-to-all-start.2 = ((f32[16,34,128]{2,1,0:T(8,128)}), f32[16,34,128]{2,1,0:T(8,128)S(1)}, u32[]{:S(2)}, u32[]{:S(2)}) async-start(f32[16,34,128]{2,1,0:T(8,128)} %shard_map.73), calls=%async_computation.2 | async-start | bytes 655360 | tf_op jit(solution)/shard_map/all_to_all | solution.py:163
  69.7 0.1 fusion.25
  70.0 0.3 fusion.9
  70.3 0.3 fusion.3
  70.8 12.0 %all-to-all-done.2 = f32[16,34,128]{2,1,0:T(8,128)S(1)} async-done(((f32[16,34,128]{2,1,0:T(8,128)}), f32[16,34,128]{2,1,0:T(8,128)S(1)}, u32[]{:S(2)}, u32[]{:S(2)}) %all-to-all-start.2) | async-done | bytes 278560 | tf_op jit(solution)/shard_map/all_to_all | solution.py:163
  82.8 0.1 dynamic-slice_reduce_fusion.2
  83.2 0.1 dynamic-slice_reduce_fusion
  84.5 0.7 fusion.16
  (59 shorter events, 2.0 us)
Async XLA Ops:
  2.4 16.9 %copy-start.4 = (bf16[1,1,4,8192]{3,2,1,0:T(4,128)(2,1)S(1)}, bf16[1,1,4,8192]{3,2,1,0:T(4,128)(2,1)}, u32[]{:S(2)}) copy-start(bf16[1,1,4,8192]{3,2,1,0:T(4,128)(2,1)} %param.7) | copy-start | bytes 196612
  2.4 25.6 %copy-start.2 = (bf16[1,1,256,2,1024]{4,3,2,1,0:T(2,128)(2,1)S(1)}, bf16[1,1,256,2,1024]{4,3,2,1,0:T(2,128)(2,1)}, u32[]{:S(2)}) copy-start(bf16[1,1,256,2,1024]{4,3,2,1,0:T(2,128)(2,1)} %param.9) | copy-start | bytes 3145732
  3.2 30.6 %all-to-all-start = ((bf16[8,288,128]{2,1,0:T(8,128)(2,1)}), bf16[8,288,128]{2,1,0:T(8,128)(2,1)S(1)}, u32[]{:S(2)}, u32[]{:S(2)}) async-start(bf16[8,288,128]{2,1,0:T(8,128)(2,1)} %pad_maximum_fusion), calls=%async_computation | async-start | bytes 1179648 | tf_op jit(solution)/shard_map/all_to_all | solution.py:148
  13.6 17.9 %collective-permute-start = (bf16[1,128,2,1024]{3,2,1,0:T(2,128)(2,1)}, bf16[1,128,2,1024]{3,2,1,0:T(2,128)(2,1)}, u32[]{:S(2)}, u32[]{:S(2)}) collective-permute-start(bf16[1,128,2,1024]{3,2,1,0:T(2,128)(2,1)} %param.12), channel_id=1, source_target_pairs={{0,496},{16,0},{32,16},{48,32},{64,48},{80,64},{96,80},{112,96},{1... | collective-permute-start | bytes 1572872 | tf_op jit(solution)/shard_map/ppermute | solution.py:86
  19.3 11.3 %collective-permute-start.1 = (bf16[4,8192]{1,0:T(4,128)(2,1)S(1)}, bf16[4,8192]{1,0:T(4,128)(2,1)}, u32[]{:S(2)}, u32[]{:S(2)}) collective-permute-start(bf16[4,8192]{1,0:T(4,128)(2,1)S(1)} %bitcast.113), channel_id=1, source_target_pairs={{0,8},{8,0},{1,9},{9,1},{2,10},{10,2},{3,11},{11,3},{4,12},{12,4},... | collective-permute-start | bytes 196616 | tf_op jit(solution)/shard_map/ppermute | solution.py:86
  29.0 0.7 copy-start.3
  33.9 7.8 %copy-start.5 = (s32[32]{0:T(128)S(1)}, s32[32]{0:T(128)}, u32[]{:S(2)}) copy-start(s32[32]{0:T(128)} %param.13) | copy-start | bytes 388
  33.9 10.3 %copy-start = (bf16[8,288,128]{2,1,0:T(8,128)(2,1)}, bf16[8,288,128]{2,1,0:T(8,128)(2,1)S(1)}, u32[]{:S(2)}) copy-start(bf16[8,288,128]{2,1,0:T(8,128)(2,1)S(1)} %all-to-all-done.first_ref) | copy-start | bytes 1769476
  33.9 23.4 %all-to-all-start.1 = ((bf16[8,288,128]{2,1,0:T(8,128)(2,1)}), bf16[8,288,128]{2,1,0:T(8,128)(2,1)S(1)}, u32[]{:S(2)}, u32[]{:S(2)}) async-start(bf16[8,288,128]{2,1,0:T(8,128)(2,1)} %pad_maximum_fusion.1), calls=%async_computation.1 | async-start | bytes 1179648 | tf_op jit(solution)/shard_map/all_to_all | solution.py:151
  57.3 0.8 copy-start.1
  63.6 19.1 %all-to-all-start.2 = ((f32[16,34,128]{2,1,0:T(8,128)}), f32[16,34,128]{2,1,0:T(8,128)S(1)}, u32[]{:S(2)}, u32[]{:S(2)}) async-start(f32[16,34,128]{2,1,0:T(8,128)} %shard_map.73), calls=%async_computation.2 | async-start | bytes 655360 | tf_op jit(solution)/shard_map/all_to_all | solution.py:163

commit v10 on v6

--- a/solution.py
+++ b/solution.py
@@ -128,7 +128,8 @@
 
     moved_tail = shifted(prefix_tail, "prompt", -1)
     own_rows = queries[0, 0]
-    partner_rows = shifted(own_rows, "zg", 1)
+    pair_count = lax.axis_size(("zg", "zl"))
+    partner_rows = lax.ppermute(own_rows, ("zg", "zl"), [(k, pair_count - 1 - k) for k in range(pair_count)])
 
     def by_head(block):
         return block[0].reshape(block_len, 2, KVH, HEAD_SIZE).transpose(2, 1, 0, 3).reshape(KVH, 2 * block_len, HEAD_SIZE)
@@ -143,7 +144,8 @@
     second = lax.all_to_all(
         jnp.concatenate([by_head(moved_tail), query_groups(partner_rows)], axis=1), ("zl", "core"), 0, 0, tiled=True
     )
-    query_parts = jnp.stack([first[:, span:], second[:, span:]])
+    partner_part = second[:, span:].reshape(team_count // 2, 2, rows_per_sample, HEAD_SIZE)[::-1]
+    query_parts = jnp.stack([first[:, span:], partner_part.reshape(team_count, rows_per_sample, HEAD_SIZE)])
     query_parts = jnp.where(team == 0, query_parts, query_parts[::-1])
     query_matrix = query_parts.reshape(2 * team_count * rows_per_sample, HEAD_SIZE)
 

time: 86 us -> 86 us (level)
    ppermute x0 -> x1, starting transfers between devices: none -> 8.15 us  [per_device(): lax.ppermute(own_rows, ('zg', 'zl'), [(k, pair_count - 1 - k) for k in ra...]
    ppermute x2 -> x1, starting transfers between devices: 13.7 us -> 5.73 us  [shifted(): return lax.ppermute(value, axis, pairs)]
    all_to_all x1, starting transfers between devices: 7.43 us -> 4.71 us  [per_device(): lax.all_to_all(jnp.concatenate([by_head(moved_tail), query_groups(partner...]
    all_to_all x1, starting transfers between devices: 6.07 us -> 8.37 us  [per_device(): lax.all_to_all(outgoing_parts, ('zg', 'zl', 'core'), 0, 0, tiled=True)]
  transfers between devices with their start and end apart: 5 -> 5, of which waited for: 2 -> 3; matrix products, arithmetic and copies ran while one was open for 11% -> 11% of each run, Pallas kernels for 0% -> 0%
where the time goes in v10:
time: 86 us; the launch traced here: 85.3 us
  starting transfers between devices  37.3 us (43%)
  waiting for transfers between devices  25.4 us (30%)
  local copies, waits for them, and re-layouts  9.17 us (11%)
  Pallas kernels  5.58 us (6%)
  other arithmetic  4.91 us (6%)
  matrix products  1.91 us (2%)
  between operations  1.08 us (1%)
    all_to_all x1, waiting for transfers between devices, per_device(): lax.all_to_all(jnp.concatenate([by_head(moved_tail), query_groups(partner...  13.2 us
    all_to_all x1, waiting for transfers between devices, per_device(): lax.all_to_all(outgoing_parts, ('zg', 'zl', 'core'), 0, 0, tiled=True)  12 us
    all_to_all x1, starting transfers between devices, per_device(): lax.all_to_all(jnp.concatenate([by_head(prefix_head), query_groups(own_ro...  10.3 us
    all_to_all x1, starting transfers between devices, per_device(): lax.all_to_all(outgoing_parts, ('zg', 'zl', 'core'), 0, 0, tiled=True)  8.37 us
    ppermute x1, starting transfers between devices, per_device(): lax.ppermute(own_rows, ('zg', 'zl'), [(k, pair_count - 1 - k) for k in ra...  8.15 us
    ppermute x1, starting transfers between devices, shifted(): return lax.ppermute(value, axis, pairs)  5.73 us
    pallas_call x1, Pallas kernels, prefix_attention(): pl.pallas_call(functools.partial(prefix_kernel, block), grid=(rows // ROW...  5.58 us
    all_to_all x1, starting transfers between devices, per_device(): lax.all_to_all(jnp.concatenate([by_head(moved_tail), query_groups(partner...  4.71 us
  transfers between devices with their start and end apart: 5, of which 3 were waited for; matrix products, arithmetic and copies ran while one was open for 11% of the time, Pallas kernels for 0%

profile of v10, /device:TPU:1, one launch (start us, length us, event | category | flops | bytes accessed | tf_op | source)
XLA Modules:
  0.0 85.3 jit_solution(7382877403067890240)
XLA Ops:
  0.0 0.8 copy_bitcast_fusion.3
  0.9 1.4 %reshape_squeeze.22 = bf16[128,2,8,128]{3,2,1,0:T(8,128)(2,1)S(1)} reshape(bf16[1,128,2,1024]{3,2,1,0:T(2,128)(2,1)} %param.11) | data formatting | bytes 1048576 | tf_op jit(solution)/shard_map/reshape;squeeze | solution.py:135
  2.2 0.1 copy.77
  2.4 0.8 pad_maximum_fusion
  3.2 10.3 %all-to-all-start = ((bf16[8,288,128]{2,1,0:T(8,128)(2,1)}), bf16[8,288,128]{2,1,0:T(8,128)(2,1)S(1)}, u32[]{:S(2)}, u32[]{:S(2)}) async-start(bf16[8,288,128]{2,1,0:T(8,128)(2,1)} %pad_maximum_fusion), calls=%async_computation | async-start | bytes 1179648 | tf_op jit(solution)/shard_map/all_to_all | solution.py:141
  13.6 5.7 %collective-permute-start = (bf16[1,128,2,1024]{3,2,1,0:T(2,128)(2,1)}, bf16[1,128,2,1024]{3,2,1,0:T(2,128)(2,1)}, u32[]{:S(2)}, u32[]{:S(2)}) collective-permute-start(bf16[1,128,2,1024]{3,2,1,0:T(2,128)(2,1)} %param.12), channel_id=1, source_target_pairs={{0,496},{16,0},{32,16},{48,32},{64,48},{80,64},{96,80},{112,96},{1... | collective-permute-start | bytes 1572872 | tf_op jit(solution)/shard_map/ppermute | solution.py:78
  19.3 8.1 %collective-permute-start.1 = (bf16[4,8192]{1,0:T(4,128)(2,1)S(1)}, bf16[4,8192]{1,0:T(4,128)(2,1)}, u32[]{:S(2)}, u32[]{:S(2)}) collective-permute-start(bf16[4,8192]{1,0:T(4,128)(2,1)S(1)} %bitcast.120), channel_id=1, source_target_pairs={{0,14},{2,12},{4,10},{6,8},{8,6},{10,4},{12,2},{14,0},{1,15},{3,13... | collective-permute-start | bytes 196616 | tf_op jit(solution)/shard_map/ppermute | solution.py:132
  28.2 1.1 %copy.84 = bf16[1,1,256,2,1024]{2,4,3,1,0:T(8,128)(2,1)S(1)} copy(bf16[1,1,256,2,1024]{4,3,2,1,0:T(2,128)(2,1)S(1)} %copy-done.2) | data formatting | bytes 2097152 | tf_op args[2]
  29.3 0.6 copy-done.3
  30.0 0.3 fusion.32
  30.3 0.4 fusion.33
  30.9 0.2 collective-permute-done.1
  31.1 0.8 copy_bitcast_fusion.2
  32.0 1.4 %reshape_squeeze.24 = bf16[128,2,8,128]{3,2,1,0:T(8,128)(2,1)S(1)} reshape(bf16[1,128,2,1024]{3,2,1,0:T(2,128)(2,1)} %collective-permute-done) | data formatting | bytes 1048576 | tf_op jit(solution)/shard_map/reshape;squeeze | solution.py:135
  33.4 0.1 copy.79
  33.5 0.8 pad_maximum_fusion.1
  34.4 4.7 %all-to-all-start.1 = ((bf16[8,288,128]{2,1,0:T(8,128)(2,1)}), bf16[8,288,128]{2,1,0:T(8,128)(2,1)S(1)}, u32[]{:S(2)}, u32[]{:S(2)}) async-start(bf16[8,288,128]{2,1,0:T(8,128)(2,1)} %pad_maximum_fusion.1), calls=%async_computation.1 | async-start | bytes 1179648 | tf_op jit(solution)/shard_map/all_to_all | solution.py:144
  39.1 0.2 fusion.7
  39.3 0.7 dynamic_slice.15
  40.0 1.2 %compare_select_fusion.bias_ref = f32[2,1024]{1,0:T(2,128)} fusion(s32[1,2,8,128]{3,2,1,0:T(8,128)S(1)} %broadcast_bitcast_fusion, s32[]{:T(128)} %bitcast.1, s32[1024]{0:T(1024)S(1)} %iota_bitcast_fusion), kind=kLoop, calls=%fused_computation.44 | loop fusion | flops 6144 | bytes 20484 | tf_op jit(solution)/shard_map/jit(_where)/select_n | solution.py:157
  41.2 0.3 fusion.21
  41.5 0.3 convolution_add_fusion.1
  41.8 13.2 %all-to-all-done.1.second_ref = bf16[8,288,128]{2,1,0:T(8,128)(2,1)S(1)} async-done(((bf16[8,288,128]{2,1,0:T(8,128)(2,1)}), bf16[8,288,128]{2,1,0:T(8,128)(2,1)S(1)}, u32[]{:S(2)}, u32[]{:S(2)}) %all-to-all-start.1) | async-done | bytes 589856 | tf_op jit(solution)/shard_map/all_to_all | solution.py:144
  55.0 0.8 reverse_select_fusion
  55.8 5.6 %shard_map.73 = f32[16,34,128]{2,1,0:T(8,128)} custom-call(f32[2,1024]{1,0:T(2,128)} %compare_select_fusion.bias_ref, bf16[512,128]{1,0:T(8,128)(2,1)} %bitcast.108, bf16[8,288,128]{2,1,0:T(8,128)(2,1)} %copy-done, bf16[8,288,128]{2,1,0:T(8,128)(2,1)} %copy-done.1), custom_call_target="tpu_custom_call" | custom-call | flops 201326592 | bytes 655360 | tf_op jit(solution)/shard_map/pallas_call | solution.py:58
  61.4 8.4 %all-to-all-start.2 = ((f32[16,34,128]{2,1,0:T(8,128)}), f32[16,34,128]{2,1,0:T(8,128)S(1)}, u32[]{:S(2)}, u32[]{:S(2)}) async-start(f32[16,34,128]{2,1,0:T(8,128)} %shard_map.73), calls=%async_computation.2 | async-start | bytes 655360 | tf_op jit(solution)/shard_map/all_to_all | solution.py:160
  69.8 0.1 fusion.25
  70.1 0.3 fusion.9
  70.4 0.3 fusion.3
  70.9 12.0 %all-to-all-done.2 = f32[16,34,128]{2,1,0:T(8,128)S(1)} async-done(((f32[16,34,128]{2,1,0:T(8,128)}), f32[16,34,128]{2,1,0:T(8,128)S(1)}, u32[]{:S(2)}, u32[]{:S(2)}) %all-to-all-start.2) | async-done | bytes 278560 | tf_op jit(solution)/shard_map/all_to_all | solution.py:160
  83.3 0.1 dynamic-slice_reduce_fusion
  84.6 0.7 fusion.16
  (64 shorter events, 2.2 us)
Async XLA Ops:
  2.4 16.9 %copy-start.4 = (bf16[1,1,4,8192]{3,2,1,0:T(4,128)(2,1)S(1)}, bf16[1,1,4,8192]{3,2,1,0:T(4,128)(2,1)}, u32[]{:S(2)}) copy-start(bf16[1,1,4,8192]{3,2,1,0:T(4,128)(2,1)} %param.7) | copy-start | bytes 196612
  2.4 25.8 %copy-start.2 = (bf16[1,1,256,2,1024]{4,3,2,1,0:T(2,128)(2,1)S(1)}, bf16[1,1,256,2,1024]{4,3,2,1,0:T(2,128)(2,1)}, u32[]{:S(2)}) copy-start(bf16[1,1,256,2,1024]{4,3,2,1,0:T(2,128)(2,1)} %param.9) | copy-start | bytes 3145732
  3.2 31.1 %all-to-all-start = ((bf16[8,288,128]{2,1,0:T(8,128)(2,1)}), bf16[8,288,128]{2,1,0:T(8,128)(2,1)S(1)}, u32[]{:S(2)}, u32[]{:S(2)}) async-start(bf16[8,288,128]{2,1,0:T(8,128)(2,1)} %pad_maximum_fusion), calls=%async_computation | async-start | bytes 1179648 | tf_op jit(solution)/shard_map/all_to_all | solution.py:141
  13.6 18.4 %collective-permute-start = (bf16[1,128,2,1024]{3,2,1,0:T(2,128)(2,1)}, bf16[1,128,2,1024]{3,2,1,0:T(2,128)(2,1)}, u32[]{:S(2)}, u32[]{:S(2)}) collective-permute-start(bf16[1,128,2,1024]{3,2,1,0:T(2,128)(2,1)} %param.12), channel_id=1, source_target_pairs={{0,496},{16,0},{32,16},{48,32},{64,48},{80,64},{96,80},{112,96},{1... | collective-permute-start | bytes 1572872 | tf_op jit(solution)/shard_map/ppermute | solution.py:78
  19.3 11.8 %collective-permute-start.1 = (bf16[4,8192]{1,0:T(4,128)(2,1)S(1)}, bf16[4,8192]{1,0:T(4,128)(2,1)}, u32[]{:S(2)}, u32[]{:S(2)}) collective-permute-start(bf16[4,8192]{1,0:T(4,128)(2,1)S(1)} %bitcast.120), channel_id=1, source_target_pairs={{0,14},{2,12},{4,10},{6,8},{8,6},{10,4},{12,2},{14,0},{1,15},{3,13... | collective-permute-start | bytes 196616 | tf_op jit(solution)/shard_map/ppermute | solution.py:132
  29.2 0.7 copy-start.3
  34.4 5.0 %copy-start.5 = (s32[32]{0:T(128)S(1)}, s32[32]{0:T(128)}, u32[]{:S(2)}) copy-start(s32[32]{0:T(128)} %param.13) | copy-start | bytes 388
  34.4 7.4 %copy-start = (bf16[8,288,128]{2,1,0:T(8,128)(2,1)}, bf16[8,288,128]{2,1,0:T(8,128)(2,1)S(1)}, u32[]{:S(2)}) copy-start(bf16[8,288,128]{2,1,0:T(8,128)(2,1)S(1)} %all-to-all-done.first_ref) | copy-start | bytes 1769476
  34.4 20.6 %all-to-all-start.1 = ((bf16[8,288,128]{2,1,0:T(8,128)(2,1)}), bf16[8,288,128]{2,1,0:T(8,128)(2,1)S(1)}, u32[]{:S(2)}, u32[]{:S(2)}) async-start(bf16[8,288,128]{2,1,0:T(8,128)(2,1)} %pad_maximum_fusion.1), calls=%async_computation.1 | async-start | bytes 1179648 | tf_op jit(solution)/shard_map/all_to_all | solution.py:144
  55.0 0.8 copy-start.1
  61.4 21.4 %all-to-all-start.2 = ((f32[16,34,128]{2,1,0:T(8,128)}), f32[16,34,128]{2,1,0:T(8,128)S(1)}, u32[]{:S(2)}, u32[]{:S(2)}) async-start(f32[16,34,128]{2,1,0:T(8,128)} %shard_map.73), calls=%async_computation.2 | async-start | bytes 655360 | tf_op jit(solution)/shard_map/all_to_all | solution.py:160

commit v11 on v6

--- a/solution.py
+++ b/solution.py
@@ -108,13 +108,13 @@
     cache_weights = jnp.where(cache_live, jnp.exp(cache_masked - maxima[..., None]), 0.0)
     fresh_weights = jnp.where(steps_live, jnp.exp(fresh_masked - maxima[..., None]), 0.0)
     totals = jnp.sum(cache_weights, axis=-1) + jnp.sum(fresh_weights, axis=-1)
-    numerator = split_dot(cache_weights, cache_values, "tkgl,lkd->tkgd") + split_dot(
-        fresh_weights, fresh_values, "tkgu,ukd->tkgd"
+    numerator = split_dot(cache_weights, cache_values, "tkgl,lkd->ktgd") + split_dot(
+        fresh_weights, fresh_values, "tkgu,ukd->ktgd"
     )
     return (
-        numerator.reshape(step_count, QH, HEAD_SIZE),
-        maxima.reshape(step_count, QH),
-        totals.reshape(step_count, QH),
+        numerator.reshape(KVH, step_count * GROUP, HEAD_SIZE),
+        maxima.transpose(1, 0, 2).reshape(KVH, step_count * GROUP),
+        totals.transpose(1, 0, 2).reshape(KVH, step_count * GROUP),
     )
 
 
@@ -158,33 +158,23 @@
     returned = lax.all_to_all(outgoing_parts, ("zg", "zl", "core"), 0, 0, tiled=True)
     returned = returned.reshape(2, KVH, rows_per_sample + 2, HEAD_SIZE)
     lane_offset = (lax.axis_index(("zg", "zl", "core")) % (ROW_BLOCK // rows_per_sample)) * rows_per_sample
-
-    def unpack(parts):
-        numer = parts[:, :rows_per_sample].reshape(KVH, step_count, GROUP, HEAD_SIZE)
-        numer = numer.transpose(1, 0, 2, 3).reshape(step_count, QH, HEAD_SIZE)
-        maxi = lax.dynamic_slice_in_dim(parts[:, rows_per_sample], lane_offset, rows_per_sample, axis=1)
-        maxi = maxi.reshape(KVH, step_count, GROUP)
-        maxi = maxi.transpose(1, 0, 2).reshape(step_count, QH)
-        tot = lax.dynamic_slice_in_dim(parts[:, rows_per_sample + 1], lane_offset, rows_per_sample, axis=1)
-        tot = tot.reshape(KVH, step_count, GROUP)
-        tot = tot.transpose(1, 0, 2).reshape(step_count, QH)
-        return numer, maxi, tot
-
-    first_numer, first_max, first_tot = unpack(returned[0])
-    second_numer, second_max, second_tot = unpack(returned[1])
+    part_numer = returned[:, :, :rows_per_sample]
+    part_stats = lax.dynamic_slice_in_dim(returned[:, :, rows_per_sample:], lane_offset, rows_per_sample, axis=3)
+    part_max = part_stats[:, :, 0]
+    part_tot = part_stats[:, :, 1]
     near_numer, near_max, near_tot = suffix_terms(own_rows, suffix_kv[0, 0], new_kv[0, 0], suffix_len[0, 0])
 
-    top = jnp.maximum(jnp.maximum(first_max, second_max), near_max)
-    first_scale = jnp.exp(first_max - top)
-    second_scale = jnp.exp(second_max - top)
+    top = jnp.maximum(jnp.maximum(part_max[0], part_max[1]), near_max)
+    part_scale = jnp.exp(part_max - top[None])
     near_scale = jnp.exp(near_max - top)
     numer = (
-        first_numer * first_scale[..., None]
-        + second_numer * second_scale[..., None]
+        part_numer[0] * part_scale[0][..., None]
+        + part_numer[1] * part_scale[1][..., None]
         + near_numer * near_scale[..., None]
     )
-    total = first_tot * first_scale + second_tot * second_scale + near_tot * near_scale
+    total = part_tot[0] * part_scale[0] + part_tot[1] * part_scale[1] + near_tot * near_scale
     attended = (numer / total[..., None]).astype(jnp.bfloat16)
+    attended = attended.reshape(KVH, step_count, GROUP, HEAD_SIZE).transpose(1, 0, 2, 3)
     return attended.reshape(queries.shape)
 
 

time: 86 us -> 86.2 us (level)
  waiting for transfers between devices: 25.2 us -> 26.3 us
  local copies, waits for them, and re-layouts: 9.2 us -> 8.24 us
    all_to_all x1, starting transfers between devices: 6.07 us -> 7.01 us  [per_device(): lax.all_to_all(outgoing_parts, ('zg', 'zl', 'core'), 0, 0, tiled=True)]
    all_to_all x1, waiting for transfers between devices: 13.2 us -> 14.1 us  [per_device(): lax.all_to_all(jnp.concatenate([by_head(moved_tail), query_groups(partner...]
  transfers between devices with their start and end apart: 5 -> 5, of which waited for: 2 -> 2; matrix products, arithmetic and copies ran while one was open for 11% -> 9% of each run, Pallas kernels for 0% -> 0%
where the time goes in v11:
time: 86.2 us; the launch traced here: 85.6 us
  starting transfers between devices  37.6 us (44%)
  waiting for transfers between devices  26.3 us (31%)
  local copies, waits for them, and re-layouts  8.24 us (10%)
  Pallas kernels  5.59 us (6%)
  other arithmetic  4.97 us (6%)
  matrix products  1.89 us (2%)
  between operations  0.95 us (1%)
    all_to_all x1, waiting for transfers between devices, per_device(): lax.all_to_all(jnp.concatenate([by_head(moved_tail), query_groups(partner...  14.1 us
    ppermute x2, starting transfers between devices, shifted(): return lax.ppermute(value, axis, pairs)  13.7 us
    all_to_all x1, waiting for transfers between devices, per_device(): lax.all_to_all(outgoing_parts, ('zg', 'zl', 'core'), 0, 0, tiled=True)  12.3 us
    all_to_all x1, starting transfers between devices, per_device(): lax.all_to_all(jnp.concatenate([by_head(prefix_head), query_groups(own_ro...  10.3 us
    all_to_all x1, starting transfers between devices, per_device(): lax.all_to_all(outgoing_parts, ('zg', 'zl', 'core'), 0, 0, tiled=True)  7.01 us
    all_to_all x1, starting transfers between devices, per_device(): lax.all_to_all(jnp.concatenate([by_head(moved_tail), query_groups(partner...  6.58 us
    pallas_call x1, Pallas kernels, prefix_attention(): pl.pallas_call(functools.partial(prefix_kernel, block), grid=(rows // ROW...  5.59 us
    another operation x4, local copies, waits for them, and re-layouts, by_head(): block[0].reshape(block_len, 2, KVH, HEAD_SIZE).transpose(2, 1, 0, 3)  3.02 us
  transfers between devices with their start and end apart: 5, of which 2 were waited for; matrix products, arithmetic and copies ran while one was open for 9% of the time, Pallas kernels for 0%

profile of v11, /device:TPU:1, one launch (start us, length us, event | category | flops | bytes accessed | tf_op | source)
XLA Modules:
  0.0 85.6 jit_solution(16198962414367598833)
XLA Ops:
  0.0 0.8 copy_bitcast_fusion.3
  0.9 1.4 %reshape_squeeze.22 = bf16[128,2,8,128]{3,2,1,0:T(8,128)(2,1)S(1)} reshape(bf16[1,128,2,1024]{3,2,1,0:T(2,128)(2,1)} %param.11) | data formatting | bytes 1048576 | tf_op jit(solution)/shard_map/reshape;squeeze | solution.py:134
  2.2 0.1 copy.14
  2.4 0.8 pad_maximum_fusion
  3.2 10.3 %all-to-all-start = ((bf16[8,288,128]{2,1,0:T(8,128)(2,1)}), bf16[8,288,128]{2,1,0:T(8,128)(2,1)S(1)}, u32[]{:S(2)}, u32[]{:S(2)}) async-start(bf16[8,288,128]{2,1,0:T(8,128)(2,1)} %pad_maximum_fusion), calls=%async_computation | async-start | bytes 1179648 | tf_op jit(solution)/shard_map/all_to_all | solution.py:140
  13.6 5.7 %collective-permute-start = (bf16[1,128,2,1024]{3,2,1,0:T(2,128)(2,1)}, bf16[1,128,2,1024]{3,2,1,0:T(2,128)(2,1)}, u32[]{:S(2)}, u32[]{:S(2)}) collective-permute-start(bf16[1,128,2,1024]{3,2,1,0:T(2,128)(2,1)} %param.12), channel_id=1, source_target_pairs={{0,496},{16,0},{32,16},{48,32},{64,48},{80,64},{96,80},{112,96},{1... | collective-permute-start | bytes 1572872 | tf_op jit(solution)/shard_map/ppermute | solution.py:78
  19.3 7.9 %collective-permute-start.1 = (bf16[4,8192]{1,0:T(4,128)(2,1)S(1)}, bf16[4,8192]{1,0:T(4,128)(2,1)S(1)}, u32[]{:S(2)}, u32[]{:S(2)}) collective-permute-start(bf16[4,8192]{1,0:T(4,128)(2,1)S(1)} %bitcast.125), channel_id=1, source_target_pairs={{0,8},{8,0},{1,9},{9,1},{2,10},{10,2},{3,11},{11,3},{4,12},{12,4},... | collective-permute-start | bytes 196616 | tf_op jit(solution)/shard_map/ppermute | solution.py:78
  28.0 1.1 %copy.18 = bf16[1,1,256,2,1024]{2,4,3,1,0:T(8,128)(2,1)S(1)} copy(bf16[1,1,256,2,1024]{4,3,2,1,0:T(2,128)(2,1)S(1)} %copy-done.2) | data formatting | bytes 2097152 | tf_op args[2]
  29.1 0.6 copy-done.3
  29.8 0.7 dynamic_slice.6
  30.5 0.3 fusion.42
  30.8 0.4 fusion.43
  31.3 1.4 %reshape_squeeze.24 = bf16[128,2,8,128]{3,2,1,0:T(8,128)(2,1)S(1)} reshape(bf16[1,128,2,1024]{3,2,1,0:T(2,128)(2,1)} %collective-permute-done) | data formatting | bytes 1048576 | tf_op jit(solution)/shard_map/reshape;squeeze | solution.py:134
  32.7 0.1 copy.16
  32.9 0.8 pad_maximum_fusion.1
  33.7 6.6 %all-to-all-start.1 = ((bf16[8,288,128]{2,1,0:T(8,128)(2,1)}), bf16[8,288,128]{2,1,0:T(8,128)(2,1)S(1)}, u32[]{:S(2)}, u32[]{:S(2)}) async-start(bf16[8,288,128]{2,1,0:T(8,128)(2,1)} %pad_maximum_fusion.1), calls=%async_computation.1 | async-start | bytes 1179648 | tf_op jit(solution)/shard_map/all_to_all | solution.py:143
  40.3 0.2 fusion.11
  40.6 1.2 %compare_select_fusion.bias_ref = f32[2,1024]{1,0:T(2,128)} fusion(s32[1,2,8,128]{3,2,1,0:T(8,128)S(1)} %broadcast_bitcast_fusion, s32[]{:T(128)} %bitcast.1, s32[1024]{0:T(1024)S(1)} %iota_bitcast_fusion), kind=kLoop, calls=%fused_computation.54 | loop fusion | flops 6144 | bytes 20484 | tf_op jit(solution)/shard_map/jit(_where)/select_n | solution.py:155
  41.8 0.3 fusion.27
  42.1 14.1 %all-to-all-done.1.second_ref = bf16[8,288,128]{2,1,0:T(8,128)(2,1)S(1)} async-done(((bf16[8,288,128]{2,1,0:T(8,128)(2,1)}), bf16[8,288,128]{2,1,0:T(8,128)(2,1)S(1)}, u32[]{:S(2)}, u32[]{:S(2)}) %all-to-all-start.1) | async-done | bytes 589856 | tf_op jit(solution)/shard_map/all_to_all | solution.py:143
  56.3 0.8 reverse_select_fusion
  57.1 5.6 %shard_map.73 = f32[16,34,128]{2,1,0:T(8,128)} custom-call(f32[2,1024]{1,0:T(2,128)} %compare_select_fusion.bias_ref, bf16[512,128]{1,0:T(8,128)(2,1)} %bitcast.117, bf16[8,288,128]{2,1,0:T(8,128)(2,1)} %copy-done, bf16[8,288,128]{2,1,0:T(8,128)(2,1)} %copy-done.1), custom_call_target="tpu_custom_call" | custom-call | flops 201326592 | bytes 655360 | tf_op jit(solution)/shard_map/pallas_call | solution.py:58
  62.6 7.0 %all-to-all-start.2 = ((f32[16,34,128]{2,1,0:T(8,128)}), f32[16,34,128]{2,1,0:T(8,128)S(1)}, u32[]{:S(2)}, u32[]{:S(2)}) async-start(f32[16,34,128]{2,1,0:T(8,128)} %shard_map.73), calls=%async_computation.2 | async-start | bytes 655360 | tf_op jit(solution)/shard_map/all_to_all | solution.py:158
  69.7 0.1 fusion.33
  69.8 0.1 reshape.190
  69.9 0.3 convolution_add_fusion.1
  70.2 0.3 fusion.13
  70.5 12.3 %all-to-all-done.2 = f32[16,34,128]{2,1,0:T(8,128)S(1)} async-done(((f32[16,34,128]{2,1,0:T(8,128)}), f32[16,34,128]{2,1,0:T(8,128)S(1)}, u32[]{:S(2)}, u32[]{:S(2)}) %all-to-all-start.2) | async-done | bytes 278560 | tf_op jit(solution)/shard_map/all_to_all | solution.py:158
  82.8 0.5 broadcast.81
  83.3 0.8 fusion.39
  84.6 0.3 fusion.7
  84.9 0.7 reshape.191
  (42 shorter events, 1.0 us)
Async XLA Ops:
  2.4 16.9 %copy-start.4 = (bf16[1,1,4,8192]{3,2,1,0:T(4,128)(2,1)S(1)}, bf16[1,1,4,8192]{3,2,1,0:T(4,128)(2,1)}, u32[]{:S(2)}) copy-start(bf16[1,1,4,8192]{3,2,1,0:T(4,128)(2,1)} %param.7) | copy-start | bytes 196612
  2.4 25.6 %copy-start.2 = (bf16[1,1,256,2,1024]{4,3,2,1,0:T(2,128)(2,1)S(1)}, bf16[1,1,256,2,1024]{4,3,2,1,0:T(2,128)(2,1)}, u32[]{:S(2)}) copy-start(bf16[1,1,256,2,1024]{4,3,2,1,0:T(2,128)(2,1)} %param.9) | copy-start | bytes 3145732
  3.2 30.5 %all-to-all-start = ((bf16[8,288,128]{2,1,0:T(8,128)(2,1)}), bf16[8,288,128]{2,1,0:T(8,128)(2,1)S(1)}, u32[]{:S(2)}, u32[]{:S(2)}) async-start(bf16[8,288,128]{2,1,0:T(8,128)(2,1)} %pad_maximum_fusion), calls=%async_computation | async-start | bytes 1179648 | tf_op jit(solution)/shard_map/all_to_all | solution.py:140
  13.6 17.8 %collective-permute-start = (bf16[1,128,2,1024]{3,2,1,0:T(2,128)(2,1)}, bf16[1,128,2,1024]{3,2,1,0:T(2,128)(2,1)}, u32[]{:S(2)}, u32[]{:S(2)}) collective-permute-start(bf16[1,128,2,1024]{3,2,1,0:T(2,128)(2,1)} %param.12), channel_id=1, source_target_pairs={{0,496},{16,0},{32,16},{48,32},{64,48},{80,64},{96,80},{112,96},{1... | collective-permute-start | bytes 1572872 | tf_op jit(solution)/shard_map/ppermute | solution.py:78
  19.3 12.0 %collective-permute-start.1 = (bf16[4,8192]{1,0:T(4,128)(2,1)S(1)}, bf16[4,8192]{1,0:T(4,128)(2,1)S(1)}, u32[]{:S(2)}, u32[]{:S(2)}) collective-permute-start(bf16[4,8192]{1,0:T(4,128)(2,1)S(1)} %bitcast.125), channel_id=1, source_target_pairs={{0,8},{8,0},{1,9},{9,1},{2,10},{10,2},{3,11},{11,3},{4,12},{12,4},... | collective-permute-start | bytes 196616 | tf_op jit(solution)/shard_map/ppermute | solution.py:78
  29.0 0.7 copy-start.3
  29.0 0.8 copy-start.5
  33.7 22.5 %copy-start = (bf16[8,288,128]{2,1,0:T(8,128)(2,1)}, bf16[8,288,128]{2,1,0:T(8,128)(2,1)S(1)}, u32[]{:S(2)}) copy-start(bf16[8,288,128]{2,1,0:T(8,128)(2,1)S(1)} %all-to-all-done.first_ref) | copy-start | bytes 1769476
  33.7 22.5 %all-to-all-start.1 = ((bf16[8,288,128]{2,1,0:T(8,128)(2,1)}), bf16[8,288,128]{2,1,0:T(8,128)(2,1)S(1)}, u32[]{:S(2)}, u32[]{:S(2)}) async-start(bf16[8,288,128]{2,1,0:T(8,128)(2,1)} %pad_maximum_fusion.1), calls=%async_computation.1 | async-start | bytes 1179648 | tf_op jit(solution)/shard_map/all_to_all | solution.py:143
  56.2 0.8 copy-start.1
  62.6 20.1 %all-to-all-start.2 = ((f32[16,34,128]{2,1,0:T(8,128)}), f32[16,34,128]{2,1,0:T(8,128)S(1)}, u32[]{:S(2)}, u32[]{:S(2)}) async-start(f32[16,34,128]{2,1,0:T(8,128)} %shard_map.73), calls=%async_computation.2 | async-start | bytes 655360 | tf_op jit(solution)/shard_map/all_to_all | solution.py:158

commit v12 on v11

--- a/solution.py
+++ b/solution.py
@@ -70,6 +70,17 @@
             flops=3 * rows * span * width, transcendentals=rows * span // 2, bytes_accessed=2 * (rows + span) * width + 4 * rows * width
         ),
     )(bias, query_matrix, first, second)
+
+
+def combine_kernel(stats_ref, first_ref, second_ref, near_ref, out_ref):
+    for head in range(out_ref.shape[0]):
+        maxima = [stats_ref[source, 0, :, head : head + 1] for source in range(3)]
+        totals = [stats_ref[source, 1, :, head : head + 1] for source in range(3)]
+        top = jnp.maximum(jnp.maximum(maxima[0], maxima[1]), maxima[2])
+        scales = [jnp.exp(m - top) for m in maxima]
+        numer = first_ref[head] * scales[0] + second_ref[head] * scales[1] + near_ref[head] * scales[2]
+        total = totals[0] * scales[0] + totals[1] * scales[1] + totals[2] * scales[2]
+        out_ref[head] = (numer / total).astype(out_ref.dtype)
 
 
 def shifted(value, axis, steps):
@@ -164,16 +175,17 @@
     part_tot = part_stats[:, :, 1]
     near_numer, near_max, near_tot = suffix_terms(own_rows, suffix_kv[0, 0], new_kv[0, 0], suffix_len[0, 0])
 
-    top = jnp.maximum(jnp.maximum(part_max[0], part_max[1]), near_max)
-    part_scale = jnp.exp(part_max - top[None])
-    near_scale = jnp.exp(near_max - top)
-    numer = (
-        part_numer[0] * part_scale[0][..., None]
-        + part_numer[1] * part_scale[1][..., None]
-        + near_numer * near_scale[..., None]
-    )
-    total = part_tot[0] * part_scale[0] + part_tot[1] * part_scale[1] + near_tot * near_scale
-    attended = (numer / total[..., None]).astype(jnp.bfloat16)
+    stats = jnp.stack(
+        [
+            jnp.stack([part_max[0], part_tot[0]]),
+            jnp.stack([part_max[1], part_tot[1]]),
+            jnp.stack([near_max, near_tot]),
+        ]
+    ).transpose(0, 1, 3, 2)
+    attended = pl.pallas_call(
+        combine_kernel,
+        out_shape=jax.ShapeDtypeStruct((KVH, rows_per_sample, HEAD_SIZE), jnp.bfloat16),
+    )(stats, part_numer[0], part_numer[1], near_numer)
     attended = attended.reshape(KVH, step_count, GROUP, HEAD_SIZE).transpose(1, 0, 2, 3)
     return attended.reshape(queries.shape)
 

time: 86.2 us -> 88.6 us (1.028)
  local copies, waits for them, and re-layouts: 8.24 us -> 10.5 us
  Pallas kernels: 5.59 us -> 7.52 us
  waiting for transfers between devices: 26.3 us -> 25.1 us
    pallas_call x0 -> x1, Pallas kernels: none -> 1.93 us  [per_device(): pl.pallas_call(combine_kernel, out_shape=jax.ShapeDtypeStruct((KVH, rows_...]
    all_to_all x1, starting transfers between devices: 7.01 us -> 6.07 us  [per_device(): lax.all_to_all(outgoing_parts, ('zg', 'zl', 'core'), 0, 0, tiled=True)]
  transfers between devices with their start and end apart: 5 -> 5, of which waited for: 2 -> 2; matrix products, arithmetic and copies ran while one was open for 9% -> 11% of each run, Pallas kernels for 0% -> 0%
where the time goes in v12:
time: 88.6 us; the launch traced here: 87.8 us
  starting transfers between devices  37.1 us (42%)
  waiting for transfers between devices  25.1 us (28%)
  local copies, waits for them, and re-layouts  10.5 us (12%)
  Pallas kernels  7.52 us (8%)
  other arithmetic  4.14 us (5%)
  matrix products  2.56 us (3%)
  between operations  0.9 us (1%)
    ppermute x2, starting transfers between devices, shifted(): return lax.ppermute(value, axis, pairs)  13.7 us
    all_to_all x1, waiting for transfers between devices, per_device(): lax.all_to_all(jnp.concatenate([by_head(moved_tail), query_groups(partner...  13.3 us
    all_to_all x1, waiting for transfers between devices, per_device(): lax.all_to_all(outgoing_parts, ('zg', 'zl', 'core'), 0, 0, tiled=True)  11.8 us
    all_to_all x1, starting transfers between devices, per_device(): lax.all_to_all(jnp.concatenate([by_head(prefix_head), query_groups(own_ro...  10.3 us
    all_to_all x1, starting transfers between devices, per_device(): lax.all_to_all(jnp.concatenate([by_head(moved_tail), query_groups(partner...  7 us
    all_to_all x1, starting transfers between devices, per_device(): lax.all_to_all(outgoing_parts, ('zg', 'zl', 'core'), 0, 0, tiled=True)  6.07 us
    pallas_call x1, Pallas kernels, prefix_attention(): pl.pallas_call(functools.partial(prefix_kernel, block), grid=(rows // ROW...  5.59 us
    another operation x4, local copies, waits for them, and re-layouts, by_head(): block[0].reshape(block_len, 2, KVH, HEAD_SIZE).transpose(2, 1, 0, 3)  3.02 us
  transfers between devices with their start and end apart: 5, of which 2 were waited for; matrix products, arithmetic and copies ran while one was open for 11% of the time, Pallas kernels for 0%

profile of v12, /device:TPU:1, one launch (start us, length us, event | category | flops | bytes accessed | tf_op | source)
XLA Modules:
  0.0 87.8 jit_solution(968013015464466830)
XLA Ops:
  0.0 0.8 copy_bitcast_fusion.3
  0.9 1.4 %reshape_squeeze.22 = bf16[128,2,8,128]{3,2,1,0:T(8,128)(2,1)S(1)} reshape(bf16[1,128,2,1024]{3,2,1,0:T(2,128)(2,1)} %param.11) | data formatting | bytes 1048576 | tf_op jit(solution)/shard_map/reshape;squeeze | solution.py:145
  2.2 0.1 copy.19
  2.4 0.9 pad_maximum_fusion
  3.3 10.3 %all-to-all-start = ((bf16[8,288,128]{2,1,0:T(8,128)(2,1)}), bf16[8,288,128]{2,1,0:T(8,128)(2,1)S(1)}, u32[]{:S(2)}, u32[]{:S(2)}) async-start(bf16[8,288,128]{2,1,0:T(8,128)(2,1)} %pad_maximum_fusion), calls=%async_computation | async-start | bytes 1179648 | tf_op jit(solution)/shard_map/all_to_all | solution.py:151
  13.6 5.7 %collective-permute-start = (bf16[1,128,2,1024]{3,2,1,0:T(2,128)(2,1)}, bf16[1,128,2,1024]{3,2,1,0:T(2,128)(2,1)}, u32[]{:S(2)}, u32[]{:S(2)}) collective-permute-start(bf16[1,128,2,1024]{3,2,1,0:T(2,128)(2,1)} %param.12), channel_id=1, source_target_pairs={{0,496},{16,0},{32,16},{48,32},{64,48},{80,64},{96,80},{112,96},{1... | collective-permute-start | bytes 1572872 | tf_op jit(solution)/shard_map/ppermute | solution.py:89
  19.3 7.9 %collective-permute-start.1 = (bf16[4,8192]{1,0:T(4,128)(2,1)S(1)}, bf16[4,8192]{1,0:T(4,128)(2,1)}, u32[]{:S(2)}, u32[]{:S(2)}) collective-permute-start(bf16[4,8192]{1,0:T(4,128)(2,1)S(1)} %bitcast.131), channel_id=1, source_target_pairs={{0,8},{8,0},{1,9},{9,1},{2,10},{10,2},{3,11},{11,3},{4,12},{12,4},... | collective-permute-start | bytes 196616 | tf_op jit(solution)/shard_map/ppermute | solution.py:89
  28.0 1.1 %copy.26 = bf16[1,1,256,2,1024]{2,4,3,1,0:T(8,128)(2,1)S(1)} copy(bf16[1,1,256,2,1024]{4,3,2,1,0:T(2,128)(2,1)S(1)} %copy-done.2) | data formatting | bytes 2097152 | tf_op args[2]
  29.1 0.6 copy-done.3
  29.8 0.3 fusion.30
  30.1 0.4 fusion.31
  30.6 0.2 fusion.7
  31.0 0.9 copy_bitcast_fusion.2
  31.9 1.4 %reshape_squeeze.24 = bf16[128,2,8,128]{3,2,1,0:T(8,128)(2,1)S(1)} reshape(bf16[1,128,2,1024]{3,2,1,0:T(2,128)(2,1)} %collective-permute-done) | data formatting | bytes 1048576 | tf_op jit(solution)/shard_map/reshape;squeeze | solution.py:145
  33.4 0.9 pad_maximum_fusion.1
  34.3 7.0 %all-to-all-start.1 = ((bf16[8,288,128]{2,1,0:T(8,128)(2,1)}), bf16[8,288,128]{2,1,0:T(8,128)(2,1)S(1)}, u32[]{:S(2)}, u32[]{:S(2)}) async-start(bf16[8,288,128]{2,1,0:T(8,128)(2,1)} %pad_maximum_fusion.1), calls=%async_computation.1 | async-start | bytes 1179648 | tf_op jit(solution)/shard_map/all_to_all | solution.py:154
  41.5 0.6 dynamic_slice.6
  42.1 1.2 %compare_select_fusion.bias_ref = f32[2,1024]{1,0:T(2,128)} fusion(s32[1,2,8,128]{3,2,1,0:T(8,128)S(1)} %broadcast_bitcast_fusion, s32[]{:T(128)} %bitcast.1, s32[1024]{0:T(1024)S(1)} %iota_bitcast_fusion), kind=kLoop, calls=%fused_computation.45 | loop fusion | flops 6144 | bytes 20484 | tf_op jit(solution)/shard_map/jit(_where)/select_n | solution.py:166
  43.3 0.3 fusion.20
  43.6 0.3 convolution_add_fusion.1
  43.9 13.3 %all-to-all-done.1.second_ref = bf16[8,288,128]{2,1,0:T(8,128)(2,1)S(1)} async-done(((bf16[8,288,128]{2,1,0:T(8,128)(2,1)}), bf16[8,288,128]{2,1,0:T(8,128)(2,1)S(1)}, u32[]{:S(2)}, u32[]{:S(2)}) %all-to-all-start.1) | async-done | bytes 589856 | tf_op jit(solution)/shard_map/all_to_all | solution.py:154
  57.2 0.8 reverse_select_fusion
  58.0 5.6 %shard_map.73 = f32[16,34,128]{2,1,0:T(8,128)} custom-call(f32[2,1024]{1,0:T(2,128)} %compare_select_fusion.bias_ref, bf16[512,128]{1,0:T(8,128)(2,1)} %bitcast.124, bf16[8,288,128]{2,1,0:T(8,128)(2,1)} %copy-done, bf16[8,288,128]{2,1,0:T(8,128)(2,1)} %copy-done.1), custom_call_target="tpu_custom_call" | custom-call | flops 201326592 | bytes 655360 | tf_op jit(solution)/shard_map/pallas_call | solution.py:58
  63.6 6.1 %all-to-all-start.2 = ((f32[16,34,128]{2,1,0:T(8,128)}), f32[16,34,128]{2,1,0:T(8,128)S(1)}, u32[]{:S(2)}, u32[]{:S(2)}) async-start(f32[16,34,128]{2,1,0:T(8,128)} %shard_map.73), calls=%async_computation.2 | async-start | bytes 655360 | tf_op jit(solution)/shard_map/all_to_all | solution.py:169
  69.7 0.3 fusion.9
  70.0 1.0 %fusion.3.near_ref = f32[8,32,128]{2,1,0:T(8,128)} fusion(f32[8,4,8,128]{3,2,1,0:T(8,128)S(1)} %convolution_add_fusion.1, f32[8,4,8,128]{3,2,1,0:T(8,128)S(1)} %fusion.9, bf16[256,8,128,1]{0,2,3,1:T(8,128)(2,1)S(1)} %bitcast.117, f32[4,8,8,256]{3,2,0,1:T(8,128)S(1)} %get-tuple-element.16, f32[4,8,8]{2,0,1:T(4,128)S(1)} %max.11, ...), kind=kOutput, calls=%fused_computation.5 | convolution fusion | flops 17170432 | bytes 1180928 | tf_op jit(solution)/shard_map/tkgl,lkd->ktgd/dot_general | solution.py:96
  71.0 11.8 %all-to-all-done.2 = f32[16,34,128]{2,1,0:T(8,128)S(1)} async-done(((f32[16,34,128]{2,1,0:T(8,128)}), f32[16,34,128]{2,1,0:T(8,128)S(1)}, u32[]{:S(2)}, u32[]{:S(2)}) %all-to-all-start.2) | async-done | bytes 278560 | tf_op jit(solution)/shard_map/all_to_all | solution.py:169
  82.8 0.7 slice_bitcast_fusion
  83.6 0.7 copy.35.stats_ref
  84.4 1.9 %shard_map.74 = bf16[8,32,128]{2,1,0:T(8,128)(2,1)} custom-call(f32[3,2,32,8]{3,2,1,0:T(8,128)} %copy.35.stats_ref, f32[8,32,128]{2,1,0:T(8,128)} %get-tuple-element.10.first_ref, f32[8,32,128]{2,1,0:T(8,128)} %get-tuple-element.9.second_ref, f32[8,32,128]{2,1,0:T(8,128)} %fusion.3.near_ref), custom_call_target="tpu_custom_call" | custom-call | tf_op jit(solution)/shard_map/pallas_call | solution.py:185
  86.3 0.9 copy.36
  87.2 0.7 reshape.110
  (39 shorter events, 1.0 us)
Async XLA Ops:
  2.4 16.9 %copy-start.4 = (bf16[1,1,4,8192]{3,2,1,0:T(4,128)(2,1)S(1)}, bf16[1,1,4,8192]{3,2,1,0:T(4,128)(2,1)}, u32[]{:S(2)}) copy-start(bf16[1,1,4,8192]{3,2,1,0:T(4,128)(2,1)} %param.7) | copy-start | bytes 196612
  2.4 25.6 %copy-start.2 = (bf16[1,1,256,2,1024]{4,3,2,1,0:T(2,128)(2,1)S(1)}, bf16[1,1,256,2,1024]{4,3,2,1,0:T(2,128)(2,1)}, u32[]{:S(2)}) copy-start(bf16[1,1,256,2,1024]{4,3,2,1,0:T(2,128)(2,1)} %param.9) | copy-start | bytes 3145732
  3.3 31.0 %all-to-all-start = ((bf16[8,288,128]{2,1,0:T(8,128)(2,1)}), bf16[8,288,128]{2,1,0:T(8,128)(2,1)S(1)}, u32[]{:S(2)}, u32[]{:S(2)}) async-start(bf16[8,288,128]{2,1,0:T(8,128)(2,1)} %pad_maximum_fusion), calls=%async_computation | async-start | bytes 1179648 | tf_op jit(solution)/shard_map/all_to_all | solution.py:151
  13.6 18.3 %collective-permute-start = (bf16[1,128,2,1024]{3,2,1,0:T(2,128)(2,1)}, bf16[1,128,2,1024]{3,2,1,0:T(2,128)(2,1)}, u32[]{:S(2)}, u32[]{:S(2)}) collective-permute-start(bf16[1,128,2,1024]{3,2,1,0:T(2,128)(2,1)} %param.12), channel_id=1, source_target_pairs={{0,496},{16,0},{32,16},{48,32},{64,48},{80,64},{96,80},{112,96},{1... | collective-permute-start | bytes 1572872 | tf_op jit(solution)/shard_map/ppermute | solution.py:89
  19.3 11.7 %collective-permute-start.1 = (bf16[4,8192]{1,0:T(4,128)(2,1)S(1)}, bf16[4,8192]{1,0:T(4,128)(2,1)}, u32[]{:S(2)}, u32[]{:S(2)}) collective-permute-start(bf16[4,8192]{1,0:T(4,128)(2,1)S(1)} %bitcast.131), channel_id=1, source_target_pairs={{0,8},{8,0},{1,9},{9,1},{2,10},{10,2},{3,11},{11,3},{4,12},{12,4},... | collective-permute-start | bytes 196616 | tf_op jit(solution)/shard_map/ppermute | solution.py:89
  29.0 0.7 copy-start.3
  33.4 8.1 %copy-start.5 = (s32[32]{0:T(128)S(1)}, s32[32]{0:T(128)}, u32[]{:S(2)}) copy-start(s32[32]{0:T(128)} %param.13) | copy-start | bytes 388
  34.3 22.9 %copy-start = (bf16[8,288,128]{2,1,0:T(8,128)(2,1)}, bf16[8,288,128]{2,1,0:T(8,128)(2,1)S(1)}, u32[]{:S(2)}) copy-start(bf16[8,288,128]{2,1,0:T(8,128)(2,1)S(1)} %all-to-all-done.first_ref) | copy-start | bytes 1769476
  34.3 22.9 %all-to-all-start.1 = ((bf16[8,288,128]{2,1,0:T(8,128)(2,1)}), bf16[8,288,128]{2,1,0:T(8,128)(2,1)S(1)}, u32[]{:S(2)}, u32[]{:S(2)}) async-start(bf16[8,288,128]{2,1,0:T(8,128)(2,1)} %pad_maximum_fusion.1), calls=%async_computation.1 | async-start | bytes 1179648 | tf_op jit(solution)/shard_map/all_to_all | solution.py:154
  57.2 0.9 copy-start.1
  63.6 19.1 %all-to-all-start.2 = ((f32[16,34,128]{2,1,0:T(8,128)}), f32[16,34,128]{2,1,0:T(8,128)S(1)}, u32[]{:S(2)}, u32[]{:S(2)}) async-start(f32[16,34,128]{2,1,0:T(8,128)} %shard_map.73), calls=%async_computation.2 | async-start | bytes 655360 | tf_op jit(solution)/shard_map/all_to_all | solution.py:169

commit v13 on v6

--- a/solution.py
+++ b/solution.py
@@ -137,13 +137,15 @@
         return rows.reshape(step_count, KVH, GROUP, HEAD_SIZE).transpose(1, 0, 2, 3).reshape(KVH, rows_per_sample, HEAD_SIZE)
 
     span = 2 * block_len
-    first = lax.all_to_all(
-        jnp.concatenate([by_head(prefix_head), query_groups(own_rows)], axis=1), ("zl", "core"), 0, 0, tiled=True
-    )
+    first = lax.all_to_all(by_head(prefix_head), ("zl", "core"), 0, 0, tiled=True)
     second = lax.all_to_all(
-        jnp.concatenate([by_head(moved_tail), query_groups(partner_rows)], axis=1), ("zl", "core"), 0, 0, tiled=True
-    )
-    query_parts = jnp.stack([first[:, span:], second[:, span:]])
+        jnp.concatenate([by_head(moved_tail), query_groups(own_rows), query_groups(partner_rows)], axis=1),
+        ("zl", "core"),
+        0,
+        0,
+        tiled=True,
+    )
+    query_parts = jnp.stack([second[:, span : span + rows_per_sample], second[:, span + rows_per_sample :]])
     query_parts = jnp.where(team == 0, query_parts, query_parts[::-1])
     query_matrix = query_parts.reshape(2 * team_count * rows_per_sample, HEAD_SIZE)
 

time: 86 us -> 100 us (1.16)
  waiting for transfers between devices: 25.2 us -> 44.8 us
  starting transfers between devices: 37.5 us -> 33.6 us
    all_to_all x2, waiting for transfers between devices: 13.2 us -> 27 us  [the longest x1 13.7 us: per_device(): lax.all_to_all(jnp.concatenate([by_head(moved_tail), query_groups(own_row...]
    all_to_all x2, starting transfers between devices: 17.7 us -> 10.7 us  [the longest x1 6.43 us: per_device(): lax.all_to_all(jnp.concatenate([by_head(moved_tail), query_groups(own_row...]
    ppermute x2, waiting for transfers between devices: 0.01 us -> 5.87 us  [shifted(): return lax.ppermute(value, axis, pairs)]
    ppermute x2, starting transfers between devices: 13.7 us -> 18.7 us  [shifted(): return lax.ppermute(value, axis, pairs)]
    unnamed x16, local copies, waits for them, and re-layouts: 1.85 us -> 3.98 us
    all_to_all x1, starting transfers between devices: 6.07 us -> 4.2 us  [per_device(): lax.all_to_all(outgoing_parts, ('zg', 'zl', 'core'), 0, 0, tiled=True)]
    reshape x2 -> x1, local copies, waits for them, and re-layouts: 1.7 us -> 0.02 us  [query_groups(): rows.reshape(step_count, KVH, GROUP, HEAD_SIZE).transpose(1, 0, 2, 3)]
    another operation x4, local copies, waits for them, and re-layouts: 3.02 us -> 1.73 us  [by_head(): block[0].reshape(block_len, 2, KVH, HEAD_SIZE).transpose(2, 1, 0, 3)]
  transfers between devices with their start and end apart: 5 -> 5, of which waited for: 2 -> 4; matrix products, arithmetic and copies ran while one was open for 11% -> 9% of each run, Pallas kernels for 0% -> 0%
where the time goes in v13:
time: 100 us; the launch traced here: 99.5 us
  waiting for transfers between devices  44.8 us (45%)
  starting transfers between devices  33.6 us (34%)
  local copies, waits for them, and re-layouts  8.52 us (9%)
  Pallas kernels  5.59 us (6%)
  other arithmetic  3.99 us (4%)
  matrix products  1.91 us (2%)
  between operations  1.04 us (1%)
    ppermute x2, starting transfers between devices, shifted(): return lax.ppermute(value, axis, pairs)  18.7 us
    all_to_all x1, waiting for transfers between devices, per_device(): lax.all_to_all(jnp.concatenate([by_head(moved_tail), query_groups(own_row...  13.7 us
    all_to_all x1, waiting for transfers between devices, per_device(): lax.all_to_all(by_head(prefix_head), ('zl', 'core'), 0, 0, tiled=True)  13.3 us
    all_to_all x1, waiting for transfers between devices, per_device(): lax.all_to_all(outgoing_parts, ('zg', 'zl', 'core'), 0, 0, tiled=True)  12 us
    all_to_all x1, starting transfers between devices, per_device(): lax.all_to_all(jnp.concatenate([by_head(moved_tail), query_groups(own_row...  6.43 us
    ppermute x2, waiting for transfers between devices, shifted(): return lax.ppermute(value, axis, pairs)  5.87 us
    pallas_call x1, Pallas kernels, prefix_attention(): pl.pallas_call(functools.partial(prefix_kernel, block), grid=(rows // ROW...  5.59 us
    all_to_all x1, starting transfers between devices, per_device(): lax.all_to_all(by_head(prefix_head), ('zl', 'core'), 0, 0, tiled=True)  4.27 us
  transfers between devices with their start and end apart: 5, of which 4 were waited for; matrix products, arithmetic and copies ran while one was open for 9% of the time, Pallas kernels for 0%

profile of v13, /device:TPU:1, one launch (start us, length us, event | category | flops | bytes accessed | tf_op | source)
XLA Modules:
  0.0 99.5 jit_solution(11291669557592782986)
XLA Ops:
  0.0 11.5 %collective-permute-start.1 = (bf16[4,8192]{1,0:T(4,128)(2,1)}, bf16[4,8192]{1,0:T(4,128)(2,1)S(1)}, u32[]{:S(2)}, u32[]{:S(2)}) collective-permute-start(bf16[4,8192]{1,0:T(4,128)(2,1)} %bitcast.116), channel_id=1, source_target_pairs={{0,8},{8,0},{1,9},{9,1},{2,10},{10,2},{3,11},{11,3},{4,12},{12,4},... | collective-permute-start | bytes 196616 | tf_op jit(solution)/shard_map/ppermute | solution.py:78
  11.5 7.3 %collective-permute-start = (bf16[1,128,2,1024]{3,2,1,0:T(2,128)(2,1)}, bf16[1,128,2,1024]{3,2,1,0:T(2,128)(2,1)S(1)}, u32[]{:S(2)}, u32[]{:S(2)}) collective-permute-start(bf16[1,128,2,1024]{3,2,1,0:T(2,128)(2,1)} %param.12), channel_id=1, source_target_pairs={{0,496},{16,0},{32,16},{48,32},{64,48},{80,64},{96,80},{112,96},{1... | collective-permute-start | bytes 1572872 | tf_op jit(solution)/shard_map/ppermute | solution.py:78
  19.4 2.4 %copy.84 = bf16[1,1,256,2,1024]{2,4,3,1,0:T(8,128)(2,1)S(1)} copy(bf16[1,1,256,2,1024]{4,3,2,1,0:T(2,128)(2,1)} %param.9) | data formatting | bytes 2097152 | tf_op args[2]
  21.9 0.6 copy-done.3
  22.7 0.3 fusion.32
  23.0 0.4 fusion.33
  23.5 5.9 %collective-permute-done = bf16[1,128,2,1024]{3,2,1,0:T(2,128)(2,1)S(1)} collective-permute-done((bf16[1,128,2,1024]{3,2,1,0:T(2,128)(2,1)}, bf16[1,128,2,1024]{3,2,1,0:T(2,128)(2,1)S(1)}, u32[]{:S(2)}, u32[]{:S(2)}) %collective-permute-start) | collective-permute-done | bytes 524320 | tf_op jit(solution)/shard_map/ppermute | solution.py:78
  29.3 0.3 reshape_squeeze.22
  29.7 0.1 copy.77
  29.8 0.9 pad_maximum_fusion
  30.7 6.4 %all-to-all-start = ((bf16[8,320,128]{2,1,0:T(8,128)(2,1)}), bf16[8,320,128]{2,1,0:T(8,128)(2,1)S(1)}, u32[]{:S(2)}, u32[]{:S(2)}) async-start(bf16[8,320,128]{2,1,0:T(8,128)(2,1)} %pad_maximum_fusion), calls=%async_computation | async-start | bytes 1310720 | tf_op jit(solution)/shard_map/all_to_all | solution.py:141
  37.1 0.3 reshape_squeeze.24
  37.5 0.9 copy.80
  38.4 0.6 dynamic_slice.15
  39.2 1.2 %compare_select_fusion.bias_ref = f32[2,1024]{1,0:T(2,128)} fusion(s32[1,2,8,128]{3,2,1,0:T(8,128)S(1)} %broadcast_bitcast_fusion, s32[]{:T(128)} %bitcast.1, s32[1024]{0:T(1024)S(1)} %iota_bitcast_fusion), kind=kLoop, calls=%fused_computation.44 | loop fusion | flops 6144 | bytes 20484 | tf_op jit(solution)/shard_map/jit(_where)/select_n | solution.py:157
  40.5 0.3 fusion.21
  40.7 13.7 %all-to-all-done.second_ref = bf16[8,320,128]{2,1,0:T(8,128)(2,1)S(1)} async-done(((bf16[8,320,128]{2,1,0:T(8,128)(2,1)}), bf16[8,320,128]{2,1,0:T(8,128)(2,1)S(1)}, u32[]{:S(2)}, u32[]{:S(2)}) %all-to-all-start) | async-done | bytes 655392 | tf_op jit(solution)/shard_map/all_to_all | solution.py:141
  54.4 4.3 %all-to-all-start.1 = ((bf16[8,256,128]{2,1,0:T(8,128)(2,1)}), bf16[8,256,128]{2,1,0:T(8,128)(2,1)S(1)}, u32[]{:S(2)}, u32[]{:S(2)}) async-start(bf16[8,256,128]{2,1,0:T(8,128)(2,1)} %bitcast.13), calls=%async_computation.1 | async-start | bytes 1048576 | tf_op jit(solution)/shard_map/all_to_all | solution.py:140
  58.7 0.2 fusion.7
  58.9 0.3 convolution_add_fusion.1
  59.3 0.7 reverse_select_fusion
  59.9 13.3 %all-to-all-done.1.first_ref = bf16[8,256,128]{2,1,0:T(8,128)(2,1)S(1)} async-done(((bf16[8,256,128]{2,1,0:T(8,128)(2,1)}), bf16[8,256,128]{2,1,0:T(8,128)(2,1)S(1)}, u32[]{:S(2)}, u32[]{:S(2)}) %all-to-all-start.1) | async-done | bytes 524320 | tf_op jit(solution)/shard_map/all_to_all | solution.py:140
  73.2 0.8 copy-done.1
  74.0 5.6 %shard_map.73 = f32[16,34,128]{2,1,0:T(8,128)} custom-call(f32[2,1024]{1,0:T(2,128)} %compare_select_fusion.bias_ref, bf16[512,128]{1,0:T(8,128)(2,1)} %bitcast.107, bf16[8,256,128]{2,1,0:T(8,128)(2,1)} %copy-done.1, bf16[8,320,128]{2,1,0:T(8,128)(2,1)} %copy-done), custom_call_target="tpu_custom_call" | custom-call | flops 201326592 | bytes 655360 | tf_op jit(solution)/shard_map/pallas_call | solution.py:58
  79.6 4.2 %all-to-all-start.2 = ((f32[16,34,128]{2,1,0:T(8,128)}), f32[16,34,128]{2,1,0:T(8,128)S(1)}, u32[]{:S(2)}, u32[]{:S(2)}) async-start(f32[16,34,128]{2,1,0:T(8,128)} %shard_map.73), calls=%async_computation.2 | async-start | bytes 655360 | tf_op jit(solution)/shard_map/all_to_all | solution.py:160
  83.8 0.1 fusion.25
  84.1 0.3 fusion.9
  84.4 0.3 fusion.3
  84.9 12.0 %all-to-all-done.2 = f32[16,34,128]{2,1,0:T(8,128)S(1)} async-done(((f32[16,34,128]{2,1,0:T(8,128)}), f32[16,34,128]{2,1,0:T(8,128)S(1)}, u32[]{:S(2)}, u32[]{:S(2)}) %all-to-all-start.2) | async-done | bytes 278560 | tf_op jit(solution)/shard_map/all_to_all | solution.py:160
  97.1 0.1 dynamic-slice_reduce_fusion.3
  97.9 0.1 div.17
  98.7 0.7 fusion.16
  (62 shorter events, 2.3 us)
Async XLA Ops:
  0.0 23.4 %collective-permute-start.1 = (bf16[4,8192]{1,0:T(4,128)(2,1)}, bf16[4,8192]{1,0:T(4,128)(2,1)S(1)}, u32[]{:S(2)}, u32[]{:S(2)}) collective-permute-start(bf16[4,8192]{1,0:T(4,128)(2,1)} %bitcast.116), channel_id=1, source_target_pairs={{0,8},{8,0},{1,9},{9,1},{2,10},{10,2},{3,11},{11,3},{4,12},{12,4},... | collective-permute-start | bytes 196616 | tf_op jit(solution)/shard_map/ppermute | solution.py:78
  11.5 17.9 %collective-permute-start = (bf16[1,128,2,1024]{3,2,1,0:T(2,128)(2,1)}, bf16[1,128,2,1024]{3,2,1,0:T(2,128)(2,1)S(1)}, u32[]{:S(2)}, u32[]{:S(2)}) collective-permute-start(bf16[1,128,2,1024]{3,2,1,0:T(2,128)(2,1)} %param.12), channel_id=1, source_target_pairs={{0,496},{16,0},{32,16},{48,32},{64,48},{80,64},{96,80},{112,96},{1... | collective-permute-start | bytes 1572872 | tf_op jit(solution)/shard_map/ppermute | solution.py:78
  21.8 0.7 copy-start.3
  21.9 0.8 copy-start.4
  29.8 7.3 %copy-start.2 = (bf16[1,128,2,1024]{3,2,1,0:T(2,128)(2,1)S(1)}, bf16[1,128,2,1024]{3,2,1,0:T(2,128)(2,1)}, u32[]{:S(2)}) copy-start(bf16[1,128,2,1024]{3,2,1,0:T(2,128)(2,1)} %param.11) | copy-start | bytes 1572868
  30.7 23.7 %all-to-all-start = ((bf16[8,320,128]{2,1,0:T(8,128)(2,1)}), bf16[8,320,128]{2,1,0:T(8,128)(2,1)S(1)}, u32[]{:S(2)}, u32[]{:S(2)}) async-start(bf16[8,320,128]{2,1,0:T(8,128)(2,1)} %pad_maximum_fusion), calls=%async_computation | async-start | bytes 1310720 | tf_op jit(solution)/shard_map/all_to_all | solution.py:141
  37.1 1.3 %copy-start.5 = (s32[32]{0:T(128)S(1)}, s32[32]{0:T(128)}, u32[]{:S(2)}) copy-start(s32[32]{0:T(128)} %param.13) | copy-start | bytes 388
  54.4 4.8 %copy-start = (bf16[8,320,128]{2,1,0:T(8,128)(2,1)}, bf16[8,320,128]{2,1,0:T(8,128)(2,1)S(1)}, u32[]{:S(2)}) copy-start(bf16[8,320,128]{2,1,0:T(8,128)(2,1)S(1)} %all-to-all-done.second_ref) | copy-start | bytes 1966084
  54.4 18.8 %all-to-all-start.1 = ((bf16[8,256,128]{2,1,0:T(8,128)(2,1)}), bf16[8,256,128]{2,1,0:T(8,128)(2,1)S(1)}, u32[]{:S(2)}, u32[]{:S(2)}) async-start(bf16[8,256,128]{2,1,0:T(8,128)(2,1)} %bitcast.13), calls=%async_computation.1 | async-start | bytes 1048576 | tf_op jit(solution)/shard_map/all_to_all | solution.py:140
  73.2 0.8 copy-start.1
  79.6 17.2 %all-to-all-start.2 = ((f32[16,34,128]{2,1,0:T(8,128)}), f32[16,34,128]{2,1,0:T(8,128)S(1)}, u32[]{:S(2)}, u32[]{:S(2)}) async-start(f32[16,34,128]{2,1,0:T(8,128)} %shard_map.73), calls=%async_computation.2 | async-start | bytes 655360 | tf_op jit(solution)/shard_map/all_to_all | solution.py:160
